TPU v7x, 512 devices: a whole 4x4x16 slice. The times are simulated.
512 devices in a mesh: row: 32 (over z_lo, y), col: 16 (over z_hi, x, core).
Axes of the slice: x: 4, y: 4, z: 16 (z_hi: 2, z_lo: 8; z = z_hi * 8 + z_lo), core: 2. Of those that a mesh axis runs over, the one named last changes fastest.
Arguments:
- pair_act: bfloat16 [256, 256, 128], P('row', 'col'), may hold values from -6 to 6
- token_mask: int32 [256], replicated, may hold values from 0 to 1, as said below
- step_offset: int32 [1], replicated, may hold values from 0 to 65535
- triangle_weight: bfloat16 [128, 512], replicated, may hold values from -0.5 to 0.5
- query_weight: bfloat16 [128, 128], replicated, may hold values from -60 to 60
- key_value_weight: bfloat16 [128, 256], replicated, may hold values from -0.5 to 0.5
- bias_weight: bfloat16 [128, 4], replicated, may hold values from -0.5 to 0.5
- triangle_carry: float32 [256, 256, 128], P('row', 'col'), may hold values from -24 to 24
- log_carry: float32 [4, 256, 256], P(None, 'row', 'col'), may hold values from 4 to 8
- output_carry: float32 [256, 256, 128], P('row', 'col'), may hold values from -6 to 6
Outputs:
- triangle_sums: float32 [256, 256, 128], P('row', 'col')
- log_norms: float32 [4, 256, 256], P(None, 'row', 'col')
- attention_out: float32 [256, 256, 128], P('row', 'col')
Inputs may be any that keep to these rules, and one draw needn't show every extreme that they name: token_mask is 1 on a leading run of tokens and 0 on a padded tail of 1 to 128 tokens. `step_offset`: only its value modulo 256 // 16 matters.
All inputs are finite; a program needn't handle non-finite values.
Results may differ from a plain program's by a relative error of at most 0.024.
The roundings to bfloat16 on the way count: a program that leaves them out, or rounds other values in their place, can miss the bound.
Values may be sent and summed in bfloat16 or wider, within the bound.
No kernel may reach another device: no remote copies, remote signals or barrier semaphores. Data moves between devices by JAX's collectives and lax.ppermute only.
A program may use at most 64 MiB of HBM per device.

v0:
```python
import math

import jax
import jax.numpy as jnp
from jax import lax
from jax.sharding import PartitionSpec as P

TRI_DIM = 128
HEADS = 4
HEAD_DIM = 32
STEPS = 4


def broadcast(block, axis, source):
    block = jnp.where(lax.axis_index(axis) == source, block, jnp.zeros_like(block))
    return lax.psum(block, axis)


def layer_norm(values):
    floats = values.astype(jnp.float32)
    average = jnp.mean(floats, axis=-1, keepdims=True)
    centred = floats - average
    variance = jnp.mean(centred * centred, axis=-1, keepdims=True)
    return (centred * lax.rsqrt(variance + 1e-05)).astype(jnp.bfloat16)


def project(normed, weight):
    flattened = normed.reshape(-1, normed.shape[-1])
    result = jnp.dot(flattened, weight, preferred_element_type=jnp.float32)
    return result.reshape(normed.shape[:-1] + (weight.shape[1],))


def gate_pair(projected, pair_keep, start):
    gate_part = projected[..., start : start + TRI_DIM]
    value_part = projected[..., start + TRI_DIM : start + 2 * TRI_DIM]
    return (jax.nn.sigmoid(gate_part) * value_part * pair_keep).astype(jnp.bfloat16)


def head_bias(normed, bias_weight):
    return jnp.transpose(project(normed, bias_weight).astype(jnp.bfloat16), (2, 0, 1))


def softmax_merge(scores, values, log_norm, outputs):
    row_max = jnp.max(scores, axis=-1)
    shifted = jnp.exp(scores - row_max[..., None])
    block_log = row_max + jnp.log(jnp.sum(shifted, axis=-1))
    merged = jnp.logaddexp(log_norm, block_log)
    weights = shifted.astype(jnp.bfloat16)
    weighted = jnp.einsum("ihjk,ikhd->ijhd", weights, values, preferred_element_type=jnp.float32)
    old_scale = jnp.transpose(jnp.exp(log_norm - merged), (0, 2, 1))[..., None]
    new_scale = jnp.transpose(jnp.exp(row_max - merged), (0, 2, 1))[..., None]
    return (merged, outputs * old_scale + weighted * new_scale)


def column_rows(right_part, bias_part, groups, col_index):
    rights = []
    biases = []
    for member in range(groups):
        right_here, bias_here = (
            broadcast(right_part, "row", groups * col_index + member),
            broadcast(bias_part, "row", groups * col_index + member),
        )
        rights.append(right_here)
        biases.append(bias_here)
    return (jnp.concatenate(rights, axis=0), jnp.concatenate(biases, axis=1))


def shards(
    pair_act,
    token_mask,
    step_offset,
    triangle_weight,
    query_weight,
    key_value_weight,
    bias_weight,
    triangle_carry,
    log_carry,
    output_carry,
):
    row_count = pair_act.shape[0]
    col_width = pair_act.shape[1]
    groups = lax.axis_size("row") // lax.axis_size("col")
    col_total = lax.axis_size("col")
    row_index = lax.axis_index("row")
    col_index = lax.axis_index("col")
    width = HEADS * HEAD_DIM
    mask_float = token_mask.astype(jnp.float32)
    row_mask = lax.dynamic_slice_in_dim(mask_float, row_index * row_count, row_count)
    col_mask = lax.dynamic_slice_in_dim(mask_float, col_index * col_width, col_width)
    normed = layer_norm(pair_act)
    queries = (project(normed, query_weight) * (1.0 / math.sqrt(HEAD_DIM))).astype(jnp.bfloat16)
    queries = queries.reshape(row_count, col_width, HEADS, HEAD_DIM)
    left_blocks = []
    right_blocks = []
    key_values = []
    bias_blocks = []
    key_masks = []
    pair_keep = row_mask[:, None, None] * col_mask[None, :, None]
    projected = project(normed, triangle_weight)
    left_op = gate_pair(projected, pair_keep, 0)
    right_op = gate_pair(projected, pair_keep, 2 * TRI_DIM)
    key_value = project(normed, key_value_weight).astype(jnp.bfloat16)
    pair_bias = head_bias(normed, bias_weight)
    for window_step in range(STEPS):
        block_id = (step_offset[0] + window_step) % col_total
        key_masks.append(lax.dynamic_slice_in_dim(token_mask, block_id * col_width, col_width))
        left_here, right_here, keys_here, bias_here = (
            broadcast(left_op, "col", block_id),
            broadcast(right_op, "col", block_id),
            broadcast(key_value, "col", block_id),
            broadcast(pair_bias, "col", block_id),
        )
        right_cols, bias_cols = column_rows(right_here, bias_here, groups, col_index)
        left_blocks.append(left_here)
        right_blocks.append(right_cols)
        key_values.append(keys_here)
        bias_blocks.append(bias_cols)
    triangle_sums = triangle_carry
    for window_step in range(STEPS):
        triangle_sums = triangle_sums + jnp.einsum(
            "ikc,jkc->ijc",
            left_blocks[window_step],
            right_blocks[window_step],
            preferred_element_type=jnp.float32,
        )
    log_norm = jnp.transpose(log_carry, (1, 0, 2))
    outputs = output_carry.reshape(row_count, col_width, HEADS, HEAD_DIM)
    for window_step in range(STEPS):
        keys_part = key_values[window_step][..., :width].reshape(
            row_count, col_width, HEADS, HEAD_DIM
        )
        values_part = key_values[window_step][..., width:].reshape(
            row_count, col_width, HEADS, HEAD_DIM
        )
        scores = jnp.einsum(
            "ijhd,ikhd->ihjk", queries, keys_part, preferred_element_type=jnp.float32
        )
        scores = scores + bias_blocks[window_step][None].astype(jnp.float32)
        scores = jnp.where(key_masks[window_step][None, None, None, :] == 1, scores, -1000000000.0)
        log_norm, outputs = softmax_merge(scores, values_part, log_norm, outputs)
    return (
        triangle_sums,
        jnp.transpose(log_norm, (1, 0, 2)),
        outputs.reshape(row_count, col_width, width),
    )


def solution(mesh):
    return jax.shard_map(
        shards,
        mesh=mesh,
        in_specs=(
            P("row", "col", None),
            P(),
            P(),
            P(),
            P(),
            P(),
            P(),
            P("row", "col", None),
            P(None, "row", "col"),
            P("row", "col", None),
        ),
        out_specs=(P("row", "col", None), P(None, "row", "col"), P("row", "col", None)),
        check_vma=False,
    )
```

profile of v0, /device:TPU:6, one launch (start us, length us, event | category | flops | bytes accessed | tf_op | source)
XLA Modules:
  0.0 999.6 jit_solution(4048793808337576733)
XLA Ops:
  8.0 0.7 copy-done.50
  9.4 0.4 copy-done.63
  10.1 0.6 select_bitcast_fusion.3
  10.8 0.7 broadcast_select_fusion.14
  11.5 0.6 select_bitcast_fusion.2
  12.1 0.7 broadcast_select_fusion.8
  12.9 0.8 copy-done.61
  13.6 0.9 broadcast_select_fusion.3
  14.7 0.7 copy-done.26
  15.6 0.5 copy-done.62
  16.5 0.7 copy-done.27
  17.2 0.9 reshape.188
  18.2 249.1 %all-reduce.9.cloned.1.call-done = (bf16[8,16,128]{2,1,0:T(8,128)(2,1)}, bf16[8,16,128]{2,1,0:T(8,128)(2,1)}, bf16[8,16,128]{2,1,0:T(8,128)(2,1)}, bf16[8,16,128...) async-done(((bf16[8,16,128]{2,1,0:T(8,128)(2,1)}, ...) | async-done | bytes 266256 | tf_op jit(solution)/shard_map/psum | solution.py:16
  267.3 1.4 broadcast_select_fusion.16
  268.8 0.6 broadcast_select_fusion.17
  269.5 0.6 broadcast_select_fusion.18
  270.2 0.6 broadcast_select_fusion.24
  270.9 0.6 broadcast_select_fusion.25
  271.6 0.6 broadcast_select_fusion.26
  272.2 0.6 broadcast_select_fusion.27
  272.8 0.6 broadcast_select_fusion.19
  273.5 253.3 %all-reduce.11.cloned.1.call-done = (bf16[8,16,256]{2,1,0:T(8,128)(2,1)}, bf16[8,16,256]{2,1,0:T(8,128)(2,1)}, bf16[8,16,256]{2,1,0:T(8,128)(2,1)}, bf16[8,16,256]{2,1,0:T(8,128)(2,1)}) async-done(((bf16[8,16,256]{2,1,0:T(8,128)(2,1)}, bf16[8,16,256]{2,1,0:T(8,128)(2,1)}, bf16[8,16,256]{2,1,0:T(8,128)(2,1)}, bf16[8,16,256]{2,1,0:T(8,128)(2,1)}), (bf16[8,16,256]{2,1,0:T(8,128)(2,1)}, ...) | async-done | bytes 262160 | tf_op jit(solution)/shard_map/psum | solution.py:16
  526.8 0.8 fusion.90
  527.9 0.7 copy-done.29
  528.9 0.8 reshape.189
  529.6 0.8 reshape.190
  530.4 0.8 reshape.191
  531.2 0.8 reshape.192
  532.1 0.6 copy-done.37
  532.9 0.6 copy-done.36
  533.6 0.6 copy-done.35
  534.2 0.9 copy.137
  535.1 437.9 %all-reduce.7.cloned.1.call-done = (bf16[8,16,128]{2,1,0:T(8,128)(2,1)}, bf16[8,16,128]{2,1,0:T(8,128)(2,1)}, bf16[8,16,128]{2,1,0:T(8,128)(2,1)}, bf16[8,16,128...) async-done(((bf16[8,16,128]{2,1,0:T(8,128)(2,1)}, ...) | async-done | bytes 270352 | tf_op jit(solution)/shard_map/psum | solution.py:16
  973.0 0.7 maximum_convert_fusion.3
  973.8 0.6 copy-done.59
  974.5 0.6 copy-done.57
  975.2 0.6 copy-done.55
  976.5 0.4 copy-done.1
  977.2 0.4 copy-done.7
  977.9 0.4 copy-done.9
  978.4 0.6 copy-done.21
  979.1 0.7 fusion.73
  979.8 0.7 fusion.66
  980.6 0.4 copy.143
  981.0 0.3 copy-done.46
  981.4 0.4 copy.141
  981.8 0.3 copy-done.44
  982.2 0.4 copy.139
  982.6 0.3 copy-done.42
  983.0 0.6 pad_maximum_fusion
  983.6 1.3 copy.136
  984.9 0.4 convolution_bitcast_fusion
  985.2 0.4 convolution_bitcast_fusion.1
  985.6 0.4 convolution_bitcast_fusion.2
  986.0 0.6 copy-done.3
  986.6 0.4 fusion.3
  987.1 0.8 copy.172
  987.9 0.6 copy.173
  988.9 0.4 fusion.18
  989.3 0.6 copy-done.10
  989.9 0.3 fusion.15
  990.2 0.6 copy-done.8
  991.2 0.6 copy-done.2
  992.2 0.8 reshape.193
  (154 shorter events, 6.1 us)
Async XLA Ops:
  7.2 2.0 copy-start
  7.2 260.2 %all-reduce.9.cloned.1.call-start = ((), (), s32[]{:S(2)}) async-start(), calls=%async_computation.1 | async-start | bytes 589824 | tf_op jit(solution)/shard_map/psum | solution.py:16
  7.9 0.9 copy-start.5
  12.8 0.8 copy-start.61
  12.8 514.0 %all-reduce.11.cloned.1.call-start = ((), (), s32[]{:S(2)}) async-start(), calls=%async_computation.2 | async-start | bytes 524288 | tf_op jit(solution)/shard_map/psum | solution.py:16
  14.6 0.8 copy-start.26
  14.6 958.4 %all-reduce.7.cloned.1.call-start = ((), (), s32[]{:S(2)}) async-start(), calls=%async_computation | async-start | bytes 655360 | tf_op jit(solution)/shard_map/psum | solution.py:16
  15.4 0.8 copy-start.62
  16.4 0.8 copy-start.27
  267.3 1.4 copy-start.41
  268.8 0.8 copy-start.40
  269.5 0.7 copy-start.54
  270.2 0.7 copy-start.53
  270.9 0.7 copy-start.52
  270.9 1.3 copy-start.51
  271.5 1.3 copy-start.39
  527.7 0.8 copy-start.29
  527.7 0.9 copy-start.30
  531.2 0.8 copy-start.38
  531.9 0.8 copy-start.37
  532.7 0.8 copy-start.36
  533.5 0.8 copy-start.35
  973.7 0.7 copy-start.59
  973.7 0.7 copy-start.60
  974.4 0.7 copy-start.57
  974.4 0.7 copy-start.58
  975.2 0.7 copy-start.56
  976.2 0.7 copy-start.1
  976.3 3.5 copy-start.17
  976.9 0.7 copy-start.7
  976.9 2.9 copy-start.13
  977.6 0.7 copy-start.9
  977.6 2.2 copy-start.15
  978.3 1.5 copy-start.19
  978.3 2.2 copy-start.11
  978.3 0.7 copy-start.21
  979.8 0.8 copy-start.48
  979.8 0.8 copy-start.49
  980.6 0.8 copy-start.46
  980.6 0.8 copy-start.47
  981.4 0.8 copy-start.44
  981.4 0.8 copy-start.45
  982.2 0.8 copy-start.42
  982.2 0.8 copy-start.43
  985.6 1.0 copy-start.3
  987.0 0.9 copy-start.28
  987.0 1.6 copy-start.14
  987.0 1.5 copy-start.16
  987.0 1.5 copy-start.18
  987.0 1.5 copy-start.20
  987.0 1.5 copy-start.22
  987.0 1.5 copy-start.31
  987.0 1.5 copy-start.32
  987.1 1.5 copy-start.33
  987.1 1.6 copy-start.12
  987.1 1.6 copy-start.25
  987.9 1.0 copy-start.6
  988.9 0.9 copy-start.10
  988.9 1.0 copy-start.24
  989.9 0.9 copy-start.8
  989.9 1.0 copy-start.23
  990.9 0.9 copy-start.2
  990.9 1.0 copy-start.4
  990.9 1.0 copy-start.34
  (3 other events, 2.1 us)
Sparse Core Ops, SparseCore 0:
  13.0 254.3 all-reduce.8
  271.0 255.7 all-reduce.10
  531.4 441.5 all-reduce.6
where the time goes:
time: 1000 us
  waiting for transfers between devices  940 us (94%)
  local copies, waits for them, and re-layouts  26.6 us (3%)
  between operations  15.1 us (2%)
  other arithmetic  12.1 us (1%)
    psum x3, waiting for transfers between devices, broadcast(): return lax.psum(block, axis)  940 us
  transfers between devices with their start and end apart: 3, of which 3 were waited for; matrix products, arithmetic and copies ran while one was open for 1% of the time, Pallas kernels for 0%

commit v1 on v0

v1 whole, which is shorter than its diff:
```python
import math

import jax
import jax.numpy as jnp
from jax import lax
from jax.sharding import PartitionSpec as P

TRI_DIM = 128
HEADS = 4
HEAD_DIM = 32
STEPS = 4


def layer_norm(values):
    floats = values.astype(jnp.float32)
    average = jnp.mean(floats, axis=-1, keepdims=True)
    centred = floats - average
    variance = jnp.mean(centred * centred, axis=-1, keepdims=True)
    return (centred * lax.rsqrt(variance + 1e-05)).astype(jnp.bfloat16)


def project(normed, weight):
    flattened = normed.reshape(-1, normed.shape[-1])
    result = jnp.dot(flattened, weight, preferred_element_type=jnp.float32)
    return result.reshape(normed.shape[:-1] + (weight.shape[1],))


def gate_pair(projected, pair_keep):
    gate_part = projected[..., :TRI_DIM]
    value_part = projected[..., TRI_DIM : 2 * TRI_DIM]
    return (jax.nn.sigmoid(gate_part) * value_part * pair_keep).astype(jnp.bfloat16)


def softmax_merge(scores, values, log_norm, outputs):
    row_max = jnp.max(scores, axis=-1)
    shifted = jnp.exp(scores - row_max[..., None])
    block_log = row_max + jnp.log(jnp.sum(shifted, axis=-1))
    merged = jnp.logaddexp(log_norm, block_log)
    weights = shifted.astype(jnp.bfloat16)
    weighted = jnp.einsum("ihjk,ikhd->ijhd", weights, values, preferred_element_type=jnp.float32)
    old_scale = jnp.transpose(jnp.exp(log_norm - merged), (0, 2, 1))[..., None]
    new_scale = jnp.transpose(jnp.exp(row_max - merged), (0, 2, 1))[..., None]
    return (merged, outputs * old_scale + weighted * new_scale)


def shards(
    pair_act,
    token_mask,
    step_offset,
    triangle_weight,
    query_weight,
    key_value_weight,
    bias_weight,
    triangle_carry,
    log_carry,
    output_carry,
):
    row_count, col_width, channels = pair_act.shape
    n_row = lax.axis_size("row")
    n_col = lax.axis_size("col")
    groups = col_width // row_count
    row_index = lax.axis_index("row")
    col_index = lax.axis_index("col")
    width = HEADS * HEAD_DIM
    window = STEPS * col_width
    piece = window // n_col

    start = step_offset[0] % n_col
    block_ids = (start + jnp.arange(STEPS, dtype=jnp.int32)) % n_col
    columns = (block_ids[:, None] * col_width + jnp.arange(col_width, dtype=jnp.int32)[None, :]).reshape(-1)
    mask_float = token_mask.astype(jnp.float32)
    key_mask = jnp.take(token_mask, columns)
    key_keep = jnp.take(mask_float, columns)
    row_mask = lax.dynamic_slice_in_dim(mask_float, row_index * row_count, row_count)
    col_mask = lax.dynamic_slice_in_dim(mask_float, col_index * col_width, col_width)

    gathered = lax.all_gather(pair_act, "col", axis=1, tiled=True)
    blocks = gathered.reshape(row_count, n_col, col_width, channels)
    doubled = jnp.concatenate([blocks, blocks[:, :STEPS]], axis=1)
    rows_act = lax.dynamic_slice_in_dim(doubled, start, STEPS, axis=1).reshape(row_count, window, channels)

    mine = lax.dynamic_slice_in_dim(rows_act, col_index * piece, piece, axis=1)
    perm = [
        (src_row * n_col + src_col, ((src_row % groups) * n_col + src_col) * n_col + src_row // groups)
        for src_row in range(n_row)
        for src_col in range(n_col)
    ]
    moved = lax.ppermute(mine, ("row", "col"), perm)
    pieces = lax.all_gather(moved, "row", axis=0, tiled=False)
    cols_act = (
        pieces.reshape(groups, n_col, row_count, piece, channels)
        .transpose(0, 2, 1, 3, 4)
        .reshape(groups * row_count, window, channels)
    )

    normed = layer_norm(pair_act)
    queries = (project(normed, query_weight) * (1.0 / math.sqrt(HEAD_DIM))).astype(jnp.bfloat16)
    queries = queries.reshape(row_count, col_width, HEADS, HEAD_DIM)

    rows_normed = layer_norm(rows_act)
    cols_normed = layer_norm(cols_act)
    left = gate_pair(
        project(rows_normed, triangle_weight[:, : 2 * TRI_DIM]),
        row_mask[:, None, None] * key_keep[None, :, None],
    )
    right = gate_pair(
        project(cols_normed, triangle_weight[:, 2 * TRI_DIM :]),
        col_mask[:, None, None] * key_keep[None, :, None],
    )
    key_value = project(rows_normed, key_value_weight).astype(jnp.bfloat16)
    pair_bias = jnp.transpose(project(cols_normed, bias_weight).astype(jnp.bfloat16), (2, 0, 1))

    triangle_sums = triangle_carry + jnp.einsum(
        "ikc,jkc->ijc", left, right, preferred_element_type=jnp.float32
    )

    keys = key_value[..., :width].reshape(row_count, window, HEADS, HEAD_DIM)
    values = key_value[..., width:].reshape(row_count, window, HEADS, HEAD_DIM)
    scores = jnp.einsum("ijhd,ikhd->ihjk", queries, keys, preferred_element_type=jnp.float32)
    scores = scores + pair_bias[None].astype(jnp.float32)
    scores = jnp.where(key_mask[None, None, None, :] == 1, scores, -1000000000.0)

    log_norm = jnp.transpose(log_carry, (1, 0, 2))
    outputs = output_carry.reshape(row_count, col_width, HEADS, HEAD_DIM)
    for window_step in range(STEPS):
        lo = window_step * col_width
        hi = lo + col_width
        log_norm, outputs = softmax_merge(scores[..., lo:hi], values[:, lo:hi], log_norm, outputs)
    return (
        triangle_sums,
        jnp.transpose(log_norm, (1, 0, 2)),
        outputs.reshape(row_count, col_width, width),
    )


def solution(mesh):
    return jax.shard_map(
        shards,
        mesh=mesh,
        in_specs=(
            P("row", "col", None),
            P(),
            P(),
            P(),
            P(),
            P(),
            P(),
            P("row", "col", None),
            P(None, "row", "col"),
            P("row", "col", None),
        ),
        out_specs=(P("row", "col", None), P(None, "row", "col"), P("row", "col", None)),
        check_vma=False,
    )
```

time: 1000 us -> 191 us (0.19)
  waiting for transfers between devices: 940 us -> 0.01 us
  blocking collectives: 0 us -> 152 us
  starting transfers between devices: 0.12 us -> 18.4 us
  local copies, waits for them, and re-layouts: 26.6 us -> 9.86 us
  between operations: 15.1 us -> 1.74 us
    psum x3 -> x0, waiting for transfers between devices: 940 us -> none  [broadcast(): return lax.psum(block, axis)]
    all_gather x0 -> x2, blocking collectives: none -> 152 us  [the longest x1 114 us: shards(): pieces = lax.all_gather(moved, 'row', axis=0, tiled=False)]
    ppermute x0 -> x1, starting transfers between devices: none -> 18.4 us  [shards(): moved = lax.ppermute(mine, ('row', 'col'), perm)]
    unnamed x131 -> x21, local copies, waits for them, and re-layouts: 15.9 us -> 4.42 us
  transfers between devices with their start and end apart: 3 -> 1, of which waited for: 3 -> 0; matrix products, arithmetic and copies ran while one was open for 1% -> 3% of each run, Pallas kernels for 0% -> 0%
where the time goes in v1:
time: 191 us
  blocking collectives  152 us (80%)
  starting transfers between devices  18.4 us (10%)
  local copies, waits for them, and re-layouts  9.86 us (5%)
  other arithmetic  4.29 us (2%)
  matrix products  4.21 us (2%)
    all_gather x1, blocking collectives, shards(): pieces = lax.all_gather(moved, 'row', axis=0, tiled=False)  114 us
    all_gather x1, blocking collectives, shards(): gathered = lax.all_gather(pair_act, 'col', axis=1, tiled=True)  38.2 us
    ppermute x1, starting transfers between devices, shards(): moved = lax.ppermute(mine, ('row', 'col'), perm)  18.4 us
    unnamed x21, local copies, waits for them, and re-layouts  4.42 us
  transfers between devices with their start and end apart: 1, of which 0 were waited for; matrix products, arithmetic and copies ran while one was open for 3% of the time, Pallas kernels for 0%

profile of v1, /device:TPU:6, one launch (start us, length us, event | category | flops | bytes accessed | tf_op | source)
XLA Modules:
  0.0 190.9 jit_solution(955438746403045785)
XLA Ops:
  1.4 0.1 copy-done.2
  1.5 38.2 %all_gather.9 = bf16[8,256,128]{2,1,0:T(8,128)(2,1)S(1)} all-gather(bf16[8,16,128]{2,1,0:T(8,128)(2,1)S(1)} %copy-done.2), channel_id=1, replica_groups=mesh['row'=32,'col'=16] {'col'}, dimensions={1}, use_global_device_ids=true | all-gather | bytes 557056 | tf_op jit(solution)/shard_map/all_gather | solution.py:77
  39.7 0.2 convert_reduce_fusion
  39.9 18.4 %collective-permute-start = (bf16[8,4,128]{2,1,0:T(4,128)(2,1)S(1)}, bf16[8,4,128]{2,1,0:T(4,128)(2,1)S(1)}, u32[]{:S(2)}, u32[]{:S(2)}) collective-permute-start(bf16[8,4,128]{2,1,0:T(4,128)(2,1)S(1)} %constant_dynamic-slice_fusion), channel_id=1, source_target_pairs={{0,0},{1,16},{2,32},{3,48},{4,64},{5,80},{6,96},{7,112},{8,128},{9... | collective-permute-start | bytes 24584 | tf_op jit(solution)/shard_map/ppermute | solution.py:88
  58.3 0.3 fusion.24
  58.6 0.1 div.33
  58.7 0.1 iota_add_fusion
  58.7 0.1 add.330
  58.8 0.1 add.327
  58.9 0.1 convert_reduce_fusion.1
  59.0 0.1 rsqrt.33
  59.1 0.3 convolution_convert_fusion
  59.5 0.7 copy-done.1
  60.2 0.8 gather_fusion.1
  61.0 0.2 fusion.55
  61.2 0.3 fusion.52
  61.5 0.8 gather_fusion
  62.3 0.1 dynamic_slice.15
  62.4 0.1 dynamic_slice.14
  62.5 0.1 broadcast_multiply_fusion.4
  62.5 0.1 broadcast_multiply_fusion.2
  62.6 0.2 fusion.13
  62.8 0.1 fusion.30
  63.0 0.2 copy.102
  63.2 0.1 reshape.351
  63.3 0.2 copy.110
  63.5 0.6 copy-done.5
  64.2 0.2 reshape.353
  64.3 0.2 copy.100
  64.5 0.6 copy-done.6
  65.2 0.2 copy.101
  65.4 114.3 %all-gather = bf16[256,4,128]{2,1,0:T(4,128)(2,1)S(1)} all-gather(bf16[8,4,128]{2,1,0:T(4,128)(2,1)S(1)} %collective-permute-done), channel_id=2, replica_groups=mesh['row'=32,'col'=16] {'row'}, dimensions={0}, use_global_device_ids=true | all-gather | bytes 270336 | tf_op jit(solution)/shard_map/all_gather | solution.py:89
  179.7 0.3 bitcast_reduce_fusion
  180.1 0.1 copy.92
  180.3 0.2 copy.95
  180.4 0.1 copy.93
  180.6 0.7 fusion.22
  181.2 0.1 copy.96
  181.4 0.1 copy.97
  181.5 0.1 rsqrt.31
  181.6 0.1 copy.98
  181.7 0.1 div.29
  181.8 0.1 copy.94
  181.9 0.1 copy.91
  182.0 0.7 copy-done.7
  182.7 0.4 fusion.15
  183.1 0.2 fusion.9
  183.3 0.6 slice_reduce_fusion.3
  184.0 0.9 fusion.35
  184.9 0.1 fusion.67
  185.0 0.1 fusion.74
  185.1 0.5 fusion.59
  185.6 0.1 fusion.68
  185.7 0.5 fusion.10
  186.2 0.4 fusion.11
  186.7 0.4 fusion.12
  187.1 0.4 fusion.2
  187.5 0.1 copy.115
  187.7 0.8 reshape.355
  188.5 0.6 copy.117
  189.1 0.2 fusion.17
  189.3 0.4 copy.99
  189.7 0.4 fusion
  190.1 0.8 copy.116
  (31 shorter events, 0.3 us)
Async XLA Ops:
  0.6 58.5 %copy-start = (bf16[128,256]{1,0:T(8,128)(2,1)S(1)}, bf16[128,256]{1,0:T(8,128)(2,1)}, u32[]{:S(2)}) copy-start(bf16[128,256]{1,0:T(8,128)(2,1)} %param.15) | copy-start | bytes 196612
  0.6 0.8 copy-start.2
  39.9 25.5 %collective-permute-start = (bf16[8,4,128]{2,1,0:T(4,128)(2,1)S(1)}, bf16[8,4,128]{2,1,0:T(4,128)(2,1)S(1)}, u32[]{:S(2)}, u32[]{:S(2)}) collective-permute-start(bf16[8,4,128]{2,1,0:T(4,128)(2,1)S(1)} %constant_dynamic-slice_fusion), channel_id=1, source_target_pairs={{0,0},{1,16},{2,32},{3,48},{4,64},{5,80},{6,96},{7,112},{8,128},{9... | collective-permute-start | bytes 24584 | tf_op jit(solution)/shard_map/ppermute | solution.py:88
  59.5 0.7 copy-start.1
  60.2 1.0 copy-start.4
  61.5 1.1 copy-start.8
  63.3 0.8 copy-start.5
  64.3 0.8 copy-start.6
  182.0 0.7 copy-start.7
  184.0 0.9 copy-start.3

commit v2 on v1

--- a/solution.py
+++ b/solution.py
@@ -74,8 +74,8 @@
     row_mask = lax.dynamic_slice_in_dim(mask_float, row_index * row_count, row_count)
     col_mask = lax.dynamic_slice_in_dim(mask_float, col_index * col_width, col_width)
 
-    gathered = lax.all_gather(pair_act, "col", axis=1, tiled=True)
-    blocks = gathered.reshape(row_count, n_col, col_width, channels)
+    spread = jnp.broadcast_to(pair_act[None], (n_col,) + pair_act.shape)
+    blocks = lax.all_to_all(spread, "col", 0, 0).transpose(1, 0, 2, 3)
     doubled = jnp.concatenate([blocks, blocks[:, :STEPS]], axis=1)
     rows_act = lax.dynamic_slice_in_dim(doubled, start, STEPS, axis=1).reshape(row_count, window, channels)
 
@@ -86,7 +86,7 @@
         for src_col in range(n_col)
     ]
     moved = lax.ppermute(mine, ("row", "col"), perm)
-    pieces = lax.all_gather(moved, "row", axis=0, tiled=False)
+    pieces = lax.all_to_all(jnp.broadcast_to(moved[None], (n_row,) + moved.shape), "row", 0, 0)
     cols_act = (
         pieces.reshape(groups, n_col, row_count, piece, channels)
         .transpose(0, 2, 1, 3, 4)

time: 191 us -> 108 us (0.57)
  blocking collectives: 152 us -> 0 us
  starting transfers between devices: 18.4 us -> 54.8 us
  waiting for transfers between devices: 0.01 us -> 29.7 us
  local copies, waits for them, and re-layouts: 9.86 us -> 12.3 us
    all_gather x2 -> x0, blocking collectives: 152 us -> none  [the longest x1 114 us: shards(): pieces = lax.all_gather(moved, 'row', axis=0, tiled=False)]
    all_to_all x0 -> x2, starting transfers between devices: none -> 31.4 us  [the longest x1 18 us: shards(): blocks = lax.all_to_all(spread, 'col', 0, 0).transpose(1, 0, 2, 3)]
    all_to_all x0 -> x2, waiting for transfers between devices: none -> 28.6 us  [the longest x1 16.4 us: shards(): lax.all_to_all(jnp.broadcast_to(moved[None], (n_row,) + moved.shape), 'ro...]
    ppermute x1, starting transfers between devices: 18.4 us -> 23.4 us  [shards(): moved = lax.ppermute(mine, ('row', 'col'), perm)]
    broadcast_in_dim x0 -> x2, local copies, waits for them, and re-layouts: none -> 2.41 us  [the longest x1 1.68 us: shards(): spread = jnp.broadcast_to(pair_act[None], (n_col,) + pair_act.shape)]
  transfers between devices with their start and end apart: 1 -> 3, of which waited for: 0 -> 3; matrix products, arithmetic and copies ran while one was open for 3% -> 5% of each run, Pallas kernels for 0% -> 0%
where the time goes in v2:
time: 108 us; the launch traced here: 107 us
  starting transfers between devices  54.8 us (51%)
  waiting for transfers between devices  29.7 us (28%)
  local copies, waits for them, and re-layouts  12.3 us (11%)
  other arithmetic  4.3 us (4%)
  matrix products  4.3 us (4%)
  between operations  1.68 us (2%)
    ppermute x1, starting transfers between devices, shards(): moved = lax.ppermute(mine, ('row', 'col'), perm)  23.4 us
    all_to_all x1, starting transfers between devices, shards(): blocks = lax.all_to_all(spread, 'col', 0, 0).transpose(1, 0, 2, 3)  18 us
    all_to_all x1, waiting for transfers between devices, shards(): lax.all_to_all(jnp.broadcast_to(moved[None], (n_row,) + moved.shape), 'ro...  16.4 us
    all_to_all x1, starting transfers between devices, shards(): lax.all_to_all(jnp.broadcast_to(moved[None], (n_row,) + moved.shape), 'ro...  13.3 us
    all_to_all x1, waiting for transfers between devices, shards(): blocks = lax.all_to_all(spread, 'col', 0, 0).transpose(1, 0, 2, 3)  12.2 us
    unnamed x21, local copies, waits for them, and re-layouts  4.73 us
  transfers between devices with their start and end apart: 3, of which 3 were waited for; matrix products, arithmetic and copies ran while one was open for 5% of the time, Pallas kernels for 0%

profile of v2, /device:TPU:6, one launch (start us, length us, event | category | flops | bytes accessed | tf_op | source)
XLA Modules:
  0.0 107.0 jit_solution(6895571618099463127)
XLA Ops:
  0.6 1.7 %broadcast_in_dim.24 = bf16[16,8,16,128]{3,2,1,0:T(8,128)(2,1)} broadcast(bf16[8,16,128]{2,1,0:T(8,128)(2,1)} %param.10), dimensions={1,2,3} | broadcast | bytes 557056 | tf_op jit(solution)/shard_map/broadcast_in_dim | solution.py:77
  2.3 18.0 %all-to-all-start = ((bf16[16,8,16,128]{3,2,1,0:T(8,128)(2,1)}), bf16[16,8,16,128]{3,2,1,0:T(8,128)(2,1)S(1)}, u32[]{:S(2)}, u32[]{:S(2)}) async-start(bf16[16,8,16,128]{3,2,1,0:T(8,128)(2,1)} %broadcast_in_dim.24), calls=%async_computation | async-start | bytes 1048576 | tf_op jit(solution)/shard_map/all_to_all | solution.py:78
  21.1 0.1 add.330
  21.2 0.1 add.327
  21.3 0.7 copy-done.1
  22.0 0.8 gather_fusion.1
  22.8 0.1 convert_reduce_fusion.1
  22.9 0.2 fusion.56
  23.1 0.6 copy-done.8
  23.7 0.2 fusion.15
  23.9 0.1 reshape.349
  24.0 0.7 copy-done.5
  24.7 0.2 reshape.351
  24.9 0.8 gather_fusion
  25.7 0.1 dynamic_slice.15
  25.8 0.2 copy.157
  26.3 12.2 %all-to-all-done = bf16[16,8,16,128]{3,2,1,0:T(8,128)(2,1)S(1)} async-done(((bf16[16,8,16,128]{3,2,1,0:T(8,128)(2,1)}), bf16[16,8,16,128]{3,2,1,0:T(8,128)(2,1)S(1)}, u32[]{:S(2)}, u32[]{:S(2)}) %all-to-all-start) | async-done | bytes 524320 | tf_op jit(solution)/shard_map/all_to_all | solution.py:78
  38.5 0.2 convert_reduce_fusion
  38.7 23.4 %collective-permute-start = (bf16[8,4,128]{2,1,0:T(4,128)(2,1)S(1)}, bf16[8,4,128]{2,1,0:T(4,128)(2,1)S(1)}, u32[]{:S(2)}, u32[]{:S(2)}) collective-permute-start(bf16[8,4,128]{2,1,0:T(4,128)(2,1)S(1)} %constant_dynamic-slice_fusion), channel_id=1, source_target_pairs={{0,0},{1,16},{2,32},{3,48},{4,64},{5,80},{6,96},{7,112},{8,128},{9... | collective-permute-start | bytes 24584 | tf_op jit(solution)/shard_map/ppermute | solution.py:88
  62.2 0.3 fusion.22
  62.4 1.1 collective-permute-done
  63.5 0.7 broadcast_in_dim.25
  64.2 13.3 %all-to-all-start.1 = ((bf16[32,8,4,128]{3,1,2,0:T(8,128)(2,1)}), bf16[32,8,4,128]{3,1,2,0:T(8,128)(2,1)S(1)}, u32[]{:S(2)}, u32[]{:S(2)}) async-start(bf16[32,8,4,128]{3,1,2,0:T(8,128)(2,1)} %broadcast_in_dim.25), calls=%async_computation.1 | async-start | bytes 524288 | tf_op jit(solution)/shard_map/all_to_all | solution.py:89
  77.6 0.1 div.33
  77.7 0.1 rsqrt.33
  77.7 0.3 convolution_convert_fusion
  78.1 0.2 copy.158
  78.3 0.2 copy.166
  78.5 0.7 copy-done.4
  79.2 0.3 fusion.53
  79.6 0.1 fusion.29
  79.7 0.2 copy.156
  79.9 16.4 %all-to-all-done.1 = bf16[32,8,4,128]{3,1,2,0:T(8,128)(2,1)S(1)} async-done(((bf16[32,8,4,128]{3,1,2,0:T(8,128)(2,1)}), bf16[32,8,4,128]{3,1,2,0:T(8,128)(2,1)S(1)}, u32[]{:S(2)}, u32[]{:S(2)}) %all-to-all-start.1) | async-done | bytes 262176 | tf_op jit(solution)/shard_map/all_to_all | solution.py:89
  96.3 0.3 fusion.23
  96.6 0.1 copy.149
  96.7 0.1 copy.151
  96.8 0.1 copy.150
  96.9 0.4 multiply_reduce_fusion
  97.3 0.1 copy.152
  97.5 0.1 copy.153
  97.6 0.1 rsqrt.31
  97.8 0.1 div.29
  97.9 0.3 multiply_convert_fusion
  98.2 0.3 copy-done.7
  98.5 0.7 fusion.14
  99.3 0.1 copy.160
  99.3 0.2 fusion.9
  99.6 0.6 slice_reduce_fusion.3
  100.2 0.9 fusion.36
  101.1 0.1 fusion.67
  101.2 0.1 fusion.74
  101.4 0.3 fusion.33
  101.7 0.1 fusion.68
  101.8 0.5 fusion.10
  102.3 0.4 fusion.11
  102.8 0.4 fusion.12
  103.2 0.4 fusion.2
  103.6 0.1 copy.171
  103.7 0.8 reshape.353
  104.5 0.6 copy.173
  105.1 0.2 fusion.17
  105.3 0.4 copy.155
  105.8 0.4 fusion
  106.2 0.8 copy.172
  (36 shorter events, 0.6 us)
Async XLA Ops:
  0.6 77.1 %copy-start = (bf16[128,256]{1,0:T(8,128)(2,1)S(1)}, bf16[128,256]{1,0:T(8,128)(2,1)}, u32[]{:S(2)}) copy-start(bf16[128,256]{1,0:T(8,128)(2,1)} %param.15) | copy-start | bytes 196612
  2.3 36.1 %all-to-all-start = ((bf16[16,8,16,128]{3,2,1,0:T(8,128)(2,1)}), bf16[16,8,16,128]{3,2,1,0:T(8,128)(2,1)S(1)}, u32[]{:S(2)}, u32[]{:S(2)}) async-start(bf16[16,8,16,128]{3,2,1,0:T(8,128)(2,1)} %broadcast_in_dim.24), calls=%async_computation | async-start | bytes 1048576 | tf_op jit(solution)/shard_map/all_to_all | solution.py:78
  21.3 0.7 copy-start.1
  22.0 0.8 copy-start.2
  22.9 0.8 copy-start.8
  23.9 0.8 copy-start.5
  24.9 1.0 copy-start.6
  38.7 24.8 %collective-permute-start = (bf16[8,4,128]{2,1,0:T(4,128)(2,1)S(1)}, bf16[8,4,128]{2,1,0:T(4,128)(2,1)S(1)}, u32[]{:S(2)}, u32[]{:S(2)}) collective-permute-start(bf16[8,4,128]{2,1,0:T(4,128)(2,1)S(1)} %constant_dynamic-slice_fusion), channel_id=1, source_target_pairs={{0,0},{1,16},{2,32},{3,48},{4,64},{5,80},{6,96},{7,112},{8,128},{9... | collective-permute-start | bytes 24584 | tf_op jit(solution)/shard_map/ppermute | solution.py:88
  64.2 32.1 %all-to-all-start.1 = ((bf16[32,8,4,128]{3,1,2,0:T(8,128)(2,1)}), bf16[32,8,4,128]{3,1,2,0:T(8,128)(2,1)S(1)}, u32[]{:S(2)}, u32[]{:S(2)}) async-start(bf16[32,8,4,128]{3,1,2,0:T(8,128)(2,1)} %broadcast_in_dim.25), calls=%async_computation.1 | async-start | bytes 524288 | tf_op jit(solution)/shard_map/all_to_all | solution.py:89
  78.3 0.9 copy-start.4
  97.9 0.7 copy-start.7
  100.2 0.9 copy-start.3

commit v3 on v2

--- a/solution.py
+++ b/solution.py
@@ -9,6 +9,8 @@
 HEADS = 4
 HEAD_DIM = 32
 STEPS = 4
+COL_BITS = (3, 2, 1, 0)
+ROW_BITS = (4, 3, 1, 2, 0)
 
 
 def layer_norm(values):
@@ -43,6 +45,20 @@
     return (merged, outputs * old_scale + weighted * new_scale)
 
 
+def doubling_gather(block, axis, bits):
+    index = lax.axis_index(axis)
+    size = lax.axis_size(axis)
+    gathered = block[None]
+    for bit in bits:
+        stride = 1 << bit
+        received = lax.ppermute(gathered, axis, [(i, i ^ stride) for i in range(size)])
+        low = (index // stride) % 2 == 0
+        gathered = jnp.where(low, jnp.stack([gathered, received]), jnp.stack([received, gathered]))
+    order = sorted(range(len(bits)), key=lambda axis_pos: -bits[len(bits) - 1 - axis_pos])
+    gathered = jnp.transpose(gathered, order + list(range(len(bits), gathered.ndim)))
+    return gathered.reshape((size,) + block.shape)
+
+
 def shards(
     pair_act,
     token_mask,
@@ -74,8 +90,7 @@
     row_mask = lax.dynamic_slice_in_dim(mask_float, row_index * row_count, row_count)
     col_mask = lax.dynamic_slice_in_dim(mask_float, col_index * col_width, col_width)
 
-    spread = jnp.broadcast_to(pair_act[None], (n_col,) + pair_act.shape)
-    blocks = lax.all_to_all(spread, "col", 0, 0).transpose(1, 0, 2, 3)
+    blocks = doubling_gather(pair_act, "col", COL_BITS).transpose(1, 0, 2, 3)
     doubled = jnp.concatenate([blocks, blocks[:, :STEPS]], axis=1)
     rows_act = lax.dynamic_slice_in_dim(doubled, start, STEPS, axis=1).reshape(row_count, window, channels)
 
@@ -86,7 +101,7 @@
         for src_col in range(n_col)
     ]
     moved = lax.ppermute(mine, ("row", "col"), perm)
-    pieces = lax.all_to_all(jnp.broadcast_to(moved[None], (n_row,) + moved.shape), "row", 0, 0)
+    pieces = doubling_gather(moved, "row", ROW_BITS)
     cols_act = (
         pieces.reshape(groups, n_col, row_count, piece, channels)
         .transpose(0, 2, 1, 3, 4)

time: 108 us -> 104 us (0.963)
  waiting for transfers between devices: 29.7 us -> 23.6 us
  starting transfers between devices: 54.8 us -> 58.1 us
  local copies, waits for them, and re-layouts: 12.3 us -> 10.2 us
    ppermute x0 -> x9, starting transfers between devices: none -> 52.6 us  [doubling_gather(): lax.ppermute(gathered, axis, [(i, i ^ stride) for i in range(size)])]
    all_to_all x2 -> x0, starting transfers between devices: 31.4 us -> none  [the longest x1 18 us: shards(): blocks = lax.all_to_all(spread, 'col', 0, 0).transpose(1, 0, 2, 3)]
    all_to_all x2 -> x0, waiting for transfers between devices: 28.6 us -> none  [the longest x1 16.4 us: shards(): lax.all_to_all(jnp.broadcast_to(moved[None], (n_row,) + moved.shape), 'ro...]
    ppermute x0 -> x9, waiting for transfers between devices: none -> 20.3 us  [doubling_gather(): lax.ppermute(gathered, axis, [(i, i ^ stride) for i in range(size)])]
    ppermute x1, starting transfers between devices: 23.4 us -> 5.47 us  [shards(): moved = lax.ppermute(mine, ('row', 'col'), perm)]
    broadcast_in_dim x2 -> x0, local copies, waits for them, and re-layouts: 2.41 us -> none  [the longest x1 1.68 us: shards(): spread = jnp.broadcast_to(pair_act[None], (n_col,) + pair_act.shape)]
    ppermute x1, waiting for transfers between devices: 1.07 us -> 3.3 us  [shards(): moved = lax.ppermute(mine, ('row', 'col'), perm)]
    unnamed x21 -> x23, local copies, waits for them, and re-layouts: 4.73 us -> 4.3 us
  transfers between devices with their start and end apart: 3 -> 10, of which waited for: 3 -> 9; matrix products, arithmetic and copies ran while one was open for 5% -> 5% of each run, Pallas kernels for 0% -> 0%
where the time goes in v3:
time: 104 us; the launch traced here: 103 us
  starting transfers between devices  58.1 us (56%)
  waiting for transfers between devices  23.6 us (23%)
  local copies, waits for them, and re-layouts  10.2 us (10%)
  other arithmetic  4.96 us (5%)
  matrix products  4.29 us (4%)
  between operations  2.02 us (2%)
    ppermute x9, starting transfers between devices, doubling_gather(): lax.ppermute(gathered, axis, [(i, i ^ stride) for i in range(size)])  52.6 us
    ppermute x9, waiting for transfers between devices, doubling_gather(): lax.ppermute(gathered, axis, [(i, i ^ stride) for i in range(size)])  20.3 us
    ppermute x1, starting transfers between devices, shards(): moved = lax.ppermute(mine, ('row', 'col'), perm)  5.47 us
    unnamed x23, local copies, waits for them, and re-layouts  4.3 us
    ppermute x1, waiting for transfers between devices, shards(): moved = lax.ppermute(mine, ('row', 'col'), perm)  3.3 us
  transfers between devices with their start and end apart: 10, of which 9 were waited for; matrix products, arithmetic and copies ran while one was open for 5% of the time, Pallas kernels for 0%

profile of v3, /device:TPU:6, one launch (start us, length us, event | category | flops | bytes accessed | tf_op | source)
XLA Modules:
  0.0 103.1 jit_solution(13504113553313085988)
XLA Ops:
  0.7 15.9 %collective-permute-start = (bf16[1,8,16,128]{3,2,1,0:T(8,128)(2,1)}, bf16[1,8,16,128]{3,2,1,0:T(8,128)(2,1)S(1)}, u32[]{:S(2)}, u32[]{:S(2)}) collective-permute-start(bf16[1,8,16,128]{3,2,1,0:T(8,128)(2,1)} %bitcast.268), channel_id=1, source_target_pairs={{0,8},{1,9},{2,10},{3,11},{4,12},{5,13},{6,14},{7,15},{8,0},{9,1},... | collective-permute-start | bytes 98312 | tf_op jit(solution)/shard_map/ppermute | solution.py:54
  17.6 0.2 fusion.56
  17.8 0.7 copy-done.1
  18.4 0.8 gather_fusion
  19.3 0.2 fusion.15
  19.7 3.3 %collective-permute-start.1 = (bf16[2,1,8,16,128]{4,3,2,0,1:T(8,128)(2,1)S(1)}, bf16[2,1,8,16,128]{4,3,2,0,1:T(8,128)(2,1)S(1)}, u32[]{:S(2)}, u32[]{:S(2)}) collective-permute-start(bf16[2,1,8,16,128]{4,3,2,0,1:T(8,128)(2,1)S(1)} %fusion.58), channel_id=1, source_target_pairs={{0,4},{1,5},{2,6},{3,7},{4,0},{5,1},{6,2},{7,3},{8,12},{9,13},{10,... | collective-permute-start | bytes 196616 | tf_op jit(solution)/shard_map/ppermute | solution.py:54
  23.1 4.3 %collective-permute-done.1 = bf16[2,1,8,16,128]{4,3,2,0,1:T(8,128)(2,1)S(1)} collective-permute-done((bf16[2,1,8,16,128]{4,3,2,0,1:T(8,128)(2,1)S(1)}, bf16[2,1,8,16,128]{4,3,2,0,1:T(8,128)(2,1)S(1)}, u32[]{:S(2)}, u32[]{:S(2)}) %collective-permute-start.1) | collective-permute-done | bytes 65568 | tf_op jit(solution)/shard_map/ppermute | solution.py:54
  27.4 2.7 %collective-permute-start.2 = (bf16[2,2,1,8,16,128]{5,4,3,0,1,2:T(8,128)(2,1)S(1)}, bf16[2,2,1,8,16,128]{5,4,3,0,1,2:T(8,128)(2,1)S(1)}, u32[]{:S(2)}, u32[]{:S(2)}) collective-permute-start(bf16[2,2,1,8,16,128]{5,4,3,0,1,2:T(8,128)(2,1)S(1)} %copy.141), channel_id=1, source_target_pairs={{0,2},{1,3},{2,0},{3,1},{4,6},{5,7},{6,4},{7,5},{8,10},{9,11},{10,... | collective-permute-start | bytes 393224 | tf_op jit(solution)/shard_map/ppermute | solution.py:54
  30.3 0.8 gather_fusion.1
  31.2 0.1 reshape.2179
  31.3 0.7 copy-done.6
  32.0 0.9 reshape.2181
  32.9 0.2 copy.156
  33.1 1.1 %collective-permute-done.2 = bf16[2,2,1,8,16,128]{5,4,3,0,1,2:T(8,128)(2,1)S(1)} collective-permute-done((bf16[2,2,1,8,16,128]{5,4,3,0,1,2:T(8,128)(2,1)S(1)}, bf16[2,2,1,8,16,128]{5,4,3,0,1,2:T(8,128)(2,1)S(1)}, u32[]{:S(2)}, u32[]{:S(2)}) %collective-permute-start.2) | collective-permute-done | bytes 131104 | tf_op jit(solution)/shard_map/ppermute | solution.py:54
  34.3 1.9 %collective-permute-start.3 = (bf16[2,2,2,1,8,16,128]{6,5,4,0,1,2,3:T(8,128)(2,1)S(1)}, bf16[2,2,2,1,8,16,128]{6,5,4,0,1,2,3:T(8,128)(2,1)S(1)}, u32[]{:S(2)}, u32[]{:S(2)}) collective-permute-start(bf16[2,2,2,1,8,16,128]{6,5,4,0,1,2,3:T(8,128)(2,1)S(1)} %maximum_select_fusion.2), channel_id=1, source_target_pairs={{0,1},{1,0},{2,3},{3,2},{4,5},{5,4},{6,7},{7,6},{8,9},{9,8},{10,11... | collective-permute-start | bytes 786440 | tf_op jit(solution)/shard_map/ppermute | solution.py:54
  36.3 1.4 %collective-permute-done.3 = bf16[2,2,2,1,8,16,128]{6,5,4,0,1,2,3:T(8,128)(2,1)S(1)} collective-permute-done((bf16[2,2,2,1,8,16,128]{6,5,4,0,1,2,3:T(8,128)(2,1)S(1)}, bf16[2,2,2,1,8,16,128]{6,5,4,0,1,2,3:T(8,128)(2,1)S(1)}, u32[]{:S(2)}, u32[]{:S(2)}) %collective-permute-start.3) | collective-permute-done | bytes 262176 | tf_op jit(solution)/shard_map/ppermute | solution.py:54
  37.8 0.2 convert_reduce_fusion
  38.0 0.3 fusion.22
  38.5 5.5 %collective-permute-start.4 = (bf16[8,4,128]{2,1,0:T(4,128)(2,1)S(1)}, bf16[8,4,128]{2,1,0:T(4,128)(2,1)S(1)}, u32[]{:S(2)}, u32[]{:S(2)}) collective-permute-start(bf16[8,4,128]{2,1,0:T(4,128)(2,1)S(1)} %constant_dynamic-slice_fusion), channel_id=1, source_target_pairs={{0,0},{1,16},{2,32},{3,48},{4,64},{5,80},{6,96},{7,112},{8,128},{9... | collective-permute-start | bytes 24584 | tf_op jit(solution)/shard_map/ppermute | solution.py:103
  44.0 0.3 fusion.53
  44.3 0.3 convolution_convert_fusion
  44.6 3.3 %collective-permute-done.4 = bf16[8,4,128]{2,1,0:T(4,128)(2,1)S(1)} collective-permute-done((bf16[8,4,128]{2,1,0:T(4,128)(2,1)S(1)}, bf16[8,4,128]{2,1,0:T(4,128)(2,1)S(1)}, u32[]{:S(2)}, u32[]{:S(2)}) %collective-permute-start.4) | collective-permute-done | bytes 8224 | tf_op jit(solution)/shard_map/ppermute | solution.py:103
  47.9 9.0 %collective-permute-start.5 = (bf16[1,8,4,128]{3,2,1,0:T(4,128)(2,1)S(1)}, bf16[1,8,4,128]{3,2,1,0:T(4,128)(2,1)S(1)}, u32[]{:S(2)}, u32[]{:S(2)}) collective-permute-start(bf16[1,8,4,128]{3,2,1,0:T(4,128)(2,1)S(1)} %bitcast.283), channel_id=1, source_target_pairs={{0,256},{16,272},{32,288},{48,304},{64,320},{80,336},{96,352},{112... | collective-permute-start | bytes 24584 | tf_op jit(solution)/shard_map/ppermute | solution.py:54
  57.0 0.1 fusion.28
  57.1 1.5 %collective-permute-done.5 = bf16[1,8,4,128]{3,2,1,0:T(4,128)(2,1)S(1)} collective-permute-done((bf16[1,8,4,128]{3,2,1,0:T(4,128)(2,1)S(1)}, bf16[1,8,4,128]{3,2,1,0:T(4,128)(2,1)S(1)}, u32[]{:S(2)}, u32[]{:S(2)}) %collective-permute-start.5) | collective-permute-done | bytes 8224 | tf_op jit(solution)/shard_map/ppermute | solution.py:54
  58.6 8.2 %collective-permute-start.6 = (bf16[2,1,8,4,128]{4,3,2,1,0:T(4,128)(2,1)S(1)}, bf16[2,1,8,4,128]{4,3,2,1,0:T(4,128)(2,1)S(1)}, u32[]{:S(2)}, u32[]{:S(2)}) collective-permute-start(bf16[2,1,8,4,128]{4,3,2,1,0:T(4,128)(2,1)S(1)} %maximum_select_fusion.15), channel_id=1, source_target_pairs={{0,128},{16,144},{32,160},{48,176},{64,192},{80,208},{96,224},{112... | collective-permute-start | bytes 49160 | tf_op jit(solution)/shard_map/ppermute | solution.py:54
  66.8 1.7 %collective-permute-done.6 = bf16[2,1,8,4,128]{4,3,2,1,0:T(4,128)(2,1)S(1)} collective-permute-done((bf16[2,1,8,4,128]{4,3,2,1,0:T(4,128)(2,1)S(1)}, bf16[2,1,8,4,128]{4,3,2,1,0:T(4,128)(2,1)S(1)}, u32[]{:S(2)}, u32[]{:S(2)}) %collective-permute-start.6) | collective-permute-done | bytes 16416 | tf_op jit(solution)/shard_map/ppermute | solution.py:54
  68.6 7.7 %collective-permute-start.7 = (bf16[2,2,1,8,4,128]{5,4,3,1,2,0:T(4,128)(2,1)S(1)}, bf16[2,2,1,8,4,128]{5,4,3,1,2,0:T(4,128)(2,1)S(1)}, u32[]{:S(2)}, u32[]{:S(2)}) collective-permute-start(bf16[2,2,1,8,4,128]{5,4,3,1,2,0:T(4,128)(2,1)S(1)} %maximum_select_fusion.13), channel_id=1, source_target_pairs={{0,32},{16,48},{32,0},{48,16},{64,96},{80,112},{96,64},{112,80},{1... | collective-permute-start | bytes 98312 | tf_op jit(solution)/shard_map/ppermute | solution.py:54
  76.4 1.8 %collective-permute-done.7 = bf16[2,2,1,8,4,128]{5,4,3,1,2,0:T(4,128)(2,1)S(1)} collective-permute-done((bf16[2,2,1,8,4,128]{5,4,3,1,2,0:T(4,128)(2,1)S(1)}, bf16[2,2,1,8,4,128]{5,4,3,1,2,0:T(4,128)(2,1)S(1)}, u32[]{:S(2)}, u32[]{:S(2)}) %collective-permute-start.7) | collective-permute-done | bytes 32800 | tf_op jit(solution)/shard_map/ppermute | solution.py:54
  78.3 1.9 %collective-permute-start.8 = (bf16[2,2,2,1,8,4,128]{6,5,4,2,1,3,0:T(4,128)(2,1)S(1)}, bf16[2,2,2,1,8,4,128]{6,5,4,2,1,3,0:T(4,128)(2,1)S(1)}, u32[]{:S(2)}, u32[]{:S(2)}) collective-permute-start(bf16[2,2,2,1,8,4,128]{6,5,4,2,1,3,0:T(4,128)(2,1)S(1)} %maximum_select_fusion.11), channel_id=1, source_target_pairs={{0,64},{16,80},{32,96},{48,112},{64,0},{80,16},{96,32},{112,48},{1... | collective-permute-start | bytes 196616 | tf_op jit(solution)/shard_map/ppermute | solution.py:54
  80.3 4.2 %collective-permute-done.8 = bf16[2,2,2,1,8,4,128]{6,5,4,2,1,3,0:T(4,128)(2,1)S(1)} collective-permute-done((bf16[2,2,2,1,8,4,128]{6,5,4,2,1,3,0:T(4,128)(2,1)S(1)}, bf16[2,2,2,1,8,4,128]{6,5,4,2,1,3,0:T(4,128)(2,1)S(1)}, u32[]{:S(2)}, u32[]{:S(2)}) %collective-permute-start.8) | collective-permute-done | bytes 65568 | tf_op jit(solution)/shard_map/ppermute | solution.py:54
  84.5 1.9 %collective-permute-start.9 = (bf16[2,2,2,2,1,8,4,128]{7,6,5,3,2,1,4,0:T(4,128)(2,1)S(1)}, bf16[2,2,2,2,1,8,4,128]{7,6,5,3,2,1,4,0:T(4,128)(2,1)S(1)}, u32[]{:S(2)}, u32[]{:S(2)}) collective-permute-start(bf16[2,2,2,2,1,8,4,128]{7,6,5,3,2,1,4,0:T(4,128)(2,1)S(1)} %maximum_select_fusion.7), channel_id=1, source_target_pairs={{0,16},{16,0},{32,48},{48,32},{64,80},{80,64},{96,112},{112,96},{1... | collective-permute-start | bytes 393224 | tf_op jit(solution)/shard_map/ppermute | solution.py:54
  86.5 0.2 copy.157
  86.7 0.2 copy.165
  86.9 0.2 copy.155
  87.2 4.2 %collective-permute-done.9 = bf16[2,2,2,2,1,8,4,128]{7,6,5,3,2,1,4,0:T(4,128)(2,1)S(1)} collective-permute-done((bf16[2,2,2,2,1,8,4,128]{7,6,5,3,2,1,4,0:T(4,128)(2,1)S(1)}, bf16[2,2,2,2,1,8,4,128]{7,6,5,3,2,1,4,0:T(4,128)(2,1)S(1)}, u32[]{:S(2)}, u32[]{:S(2)}) %collective-permute-start.9) | collective-permute-done | bytes 131104 | tf_op jit(solution)/shard_map/ppermute | solution.py:54
  91.4 0.2 convert_bitcast_fusion
  91.6 0.3 reduce_sum.90
  92.1 0.1 copy.147
  92.2 0.4 multiply_reduce_fusion
  92.8 0.1 copy.150
  92.9 0.1 rsqrt.31
  93.0 0.1 div.102
  93.1 0.3 multiply_convert_fusion
  93.5 0.3 copy-done.8
  93.8 0.7 fusion.14
  94.6 0.2 fusion.9
  94.8 0.6 slice_reduce_fusion.3
  95.5 0.9 fusion.35
  96.4 0.1 fusion.70
  96.5 0.1 fusion.77
  96.6 0.3 fusion.32
  97.0 0.9 copy-done.3
  97.9 0.5 fusion.10
  98.4 0.4 fusion.11
  98.9 0.5 fusion.12
  99.3 0.4 fusion.2
  99.7 0.1 copy.170
  99.8 0.8 reshape.2183
  100.6 0.6 copy.172
  101.2 0.2 fusion.17
  101.4 0.4 copy.154
  101.9 0.4 fusion
  102.3 0.8 copy.171
  (68 shorter events, 2.1 us)
Async XLA Ops:
  0.6 43.7 %copy-start = (bf16[128,256]{1,0:T(8,128)(2,1)S(1)}, bf16[128,256]{1,0:T(8,128)(2,1)}, u32[]{:S(2)}) copy-start(bf16[128,256]{1,0:T(8,128)(2,1)} %param.15) | copy-start | bytes 196612
  0.6 16.8 %copy-start.2 = (bf16[8,16,128]{2,1,0:T(8,128)(2,1)S(1)}, bf16[8,16,128]{2,1,0:T(8,128)(2,1)}, u32[]{:S(2)}) copy-start(bf16[8,16,128]{2,1,0:T(8,128)(2,1)} %param.10) | copy-start | bytes 98308
  0.7 19.0 %collective-permute-start = (bf16[1,8,16,128]{3,2,1,0:T(8,128)(2,1)}, bf16[1,8,16,128]{3,2,1,0:T(8,128)(2,1)S(1)}, u32[]{:S(2)}, u32[]{:S(2)}) collective-permute-start(bf16[1,8,16,128]{3,2,1,0:T(8,128)(2,1)} %bitcast.268), channel_id=1, source_target_pairs={{0,8},{1,9},{2,10},{3,11},{4,12},{5,13},{6,14},{7,15},{8,0},{9,1},... | collective-permute-start | bytes 98312 | tf_op jit(solution)/shard_map/ppermute | solution.py:54
  17.7 0.7 copy-start.1
  18.4 0.9 copy-start.9
  19.7 7.7 %collective-permute-start.1 = (bf16[2,1,8,16,128]{4,3,2,0,1:T(8,128)(2,1)S(1)}, bf16[2,1,8,16,128]{4,3,2,0,1:T(8,128)(2,1)S(1)}, u32[]{:S(2)}, u32[]{:S(2)}) collective-permute-start(bf16[2,1,8,16,128]{4,3,2,0,1:T(8,128)(2,1)S(1)} %fusion.58), channel_id=1, source_target_pairs={{0,4},{1,5},{2,6},{3,7},{4,0},{5,1},{6,2},{7,3},{8,12},{9,13},{10,... | collective-permute-start | bytes 196616 | tf_op jit(solution)/shard_map/ppermute | solution.py:54
  27.4 6.9 %collective-permute-start.2 = (bf16[2,2,1,8,16,128]{5,4,3,0,1,2:T(8,128)(2,1)S(1)}, bf16[2,2,1,8,16,128]{5,4,3,0,1,2:T(8,128)(2,1)S(1)}, u32[]{:S(2)}, u32[]{:S(2)}) collective-permute-start(bf16[2,2,1,8,16,128]{5,4,3,0,1,2:T(8,128)(2,1)S(1)} %copy.141), channel_id=1, source_target_pairs={{0,2},{1,3},{2,0},{3,1},{4,6},{5,7},{6,4},{7,5},{8,10},{9,11},{10,... | collective-permute-start | bytes 393224 | tf_op jit(solution)/shard_map/ppermute | solution.py:54
  31.1 0.8 copy-start.6
  32.0 0.9 copy-start.7
  34.3 3.4 %collective-permute-start.3 = (bf16[2,2,2,1,8,16,128]{6,5,4,0,1,2,3:T(8,128)(2,1)S(1)}, bf16[2,2,2,1,8,16,128]{6,5,4,0,1,2,3:T(8,128)(2,1)S(1)}, u32[]{:S(2)}, u32[]{:S(2)}) collective-permute-start(bf16[2,2,2,1,8,16,128]{6,5,4,0,1,2,3:T(8,128)(2,1)S(1)} %maximum_select_fusion.2), channel_id=1, source_target_pairs={{0,1},{1,0},{2,3},{3,2},{4,5},{5,4},{6,7},{7,6},{8,9},{9,8},{10,11... | collective-permute-start | bytes 786440 | tf_op jit(solution)/shard_map/ppermute | solution.py:54
  38.0 6.0 %copy-start.5 = (bf16[128,512]{1,0:T(8,128)(2,1)S(1)}, bf16[128,512]{1,0:T(8,128)(2,1)}, u32[]{:S(2)}) copy-start(bf16[128,512]{1,0:T(8,128)(2,1)} %param.13) | copy-start | bytes 393220
  38.5 9.5 %collective-permute-start.4 = (bf16[8,4,128]{2,1,0:T(4,128)(2,1)S(1)}, bf16[8,4,128]{2,1,0:T(4,128)(2,1)S(1)}, u32[]{:S(2)}, u32[]{:S(2)}) collective-permute-start(bf16[8,4,128]{2,1,0:T(4,128)(2,1)S(1)} %constant_dynamic-slice_fusion), channel_id=1, source_target_pairs={{0,0},{1,16},{2,32},{3,48},{4,64},{5,80},{6,96},{7,112},{8,128},{9... | collective-permute-start | bytes 24584 | tf_op jit(solution)/shard_map/ppermute | solution.py:103
  47.9 10.7 %collective-permute-start.5 = (bf16[1,8,4,128]{3,2,1,0:T(4,128)(2,1)S(1)}, bf16[1,8,4,128]{3,2,1,0:T(4,128)(2,1)S(1)}, u32[]{:S(2)}, u32[]{:S(2)}) collective-permute-start(bf16[1,8,4,128]{3,2,1,0:T(4,128)(2,1)S(1)} %bitcast.283), channel_id=1, source_target_pairs={{0,256},{16,272},{32,288},{48,304},{64,320},{80,336},{96,352},{112... | collective-permute-start | bytes 24584 | tf_op jit(solution)/shard_map/ppermute | solution.py:54
  58.6 9.9 %collective-permute-start.6 = (bf16[2,1,8,4,128]{4,3,2,1,0:T(4,128)(2,1)S(1)}, bf16[2,1,8,4,128]{4,3,2,1,0:T(4,128)(2,1)S(1)}, u32[]{:S(2)}, u32[]{:S(2)}) collective-permute-start(bf16[2,1,8,4,128]{4,3,2,1,0:T(4,128)(2,1)S(1)} %maximum_select_fusion.15), channel_id=1, source_target_pairs={{0,128},{16,144},{32,160},{48,176},{64,192},{80,208},{96,224},{112... | collective-permute-start | bytes 49160 | tf_op jit(solution)/shard_map/ppermute | solution.py:54
  68.6 9.6 %collective-permute-start.7 = (bf16[2,2,1,8,4,128]{5,4,3,1,2,0:T(4,128)(2,1)S(1)}, bf16[2,2,1,8,4,128]{5,4,3,1,2,0:T(4,128)(2,1)S(1)}, u32[]{:S(2)}, u32[]{:S(2)}) collective-permute-start(bf16[2,2,1,8,4,128]{5,4,3,1,2,0:T(4,128)(2,1)S(1)} %maximum_select_fusion.13), channel_id=1, source_target_pairs={{0,32},{16,48},{32,0},{48,16},{64,96},{80,112},{96,64},{112,80},{1... | collective-permute-start | bytes 98312 | tf_op jit(solution)/shard_map/ppermute | solution.py:54
  78.3 6.2 %collective-permute-start.8 = (bf16[2,2,2,1,8,4,128]{6,5,4,2,1,3,0:T(4,128)(2,1)S(1)}, bf16[2,2,2,1,8,4,128]{6,5,4,2,1,3,0:T(4,128)(2,1)S(1)}, u32[]{:S(2)}, u32[]{:S(2)}) collective-permute-start(bf16[2,2,2,1,8,4,128]{6,5,4,2,1,3,0:T(4,128)(2,1)S(1)} %maximum_select_fusion.11), channel_id=1, source_target_pairs={{0,64},{16,80},{32,96},{48,112},{64,0},{80,16},{96,32},{112,48},{1... | collective-permute-start | bytes 196616 | tf_op jit(solution)/shard_map/ppermute | solution.py:54
  84.5 6.9 %collective-permute-start.9 = (bf16[2,2,2,2,1,8,4,128]{7,6,5,3,2,1,4,0:T(4,128)(2,1)S(1)}, bf16[2,2,2,2,1,8,4,128]{7,6,5,3,2,1,4,0:T(4,128)(2,1)S(1)}, u32[]{:S(2)}, u32[]{:S(2)}) collective-permute-start(bf16[2,2,2,2,1,8,4,128]{7,6,5,3,2,1,4,0:T(4,128)(2,1)S(1)} %maximum_select_fusion.7), channel_id=1, source_target_pairs={{0,16},{16,0},{32,48},{48,32},{64,80},{80,64},{96,112},{112,96},{1... | collective-permute-start | bytes 393224 | tf_op jit(solution)/shard_map/ppermute | solution.py:54
  93.1 0.7 copy-start.8
  95.4 0.9 copy-start.4
  96.9 1.0 copy-start.3

commit v4 on v3

--- a/solution.py
+++ b/solution.py
@@ -11,6 +11,7 @@
 STEPS = 4
 COL_BITS = (3, 2, 1, 0)
 ROW_BITS = (4, 3, 1, 2, 0)
+Y_SIZE = 4
 
 
 def layer_norm(values):
@@ -59,6 +60,16 @@
     return gathered.reshape((size,) + block.shape)
 
 
+def grouped_gather(block, axis, outer, inner):
+    inner_groups = [[g * inner + i for i in range(inner)] for g in range(outer)]
+    outer_groups = [[i * inner + g for i in range(outer)] for g in range(inner)]
+    spread = jnp.broadcast_to(block[None], (inner,) + block.shape)
+    near = lax.all_to_all(spread, axis, 0, 0, axis_index_groups=inner_groups)
+    spread = jnp.broadcast_to(near[None], (outer,) + near.shape)
+    far = lax.all_to_all(spread, axis, 0, 0, axis_index_groups=outer_groups)
+    return far.reshape((outer * inner,) + block.shape)
+
+
 def shards(
     pair_act,
     token_mask,
@@ -90,7 +101,8 @@
     row_mask = lax.dynamic_slice_in_dim(mask_float, row_index * row_count, row_count)
     col_mask = lax.dynamic_slice_in_dim(mask_float, col_index * col_width, col_width)
 
-    blocks = doubling_gather(pair_act, "col", COL_BITS).transpose(1, 0, 2, 3)
+    spread = jnp.broadcast_to(pair_act[None], (n_col,) + pair_act.shape)
+    blocks = lax.all_to_all(spread, "col", 0, 0).transpose(1, 0, 2, 3)
     doubled = jnp.concatenate([blocks, blocks[:, :STEPS]], axis=1)
     rows_act = lax.dynamic_slice_in_dim(doubled, start, STEPS, axis=1).reshape(row_count, window, channels)
 
@@ -101,7 +113,7 @@
         for src_col in range(n_col)
     ]
     moved = lax.ppermute(mine, ("row", "col"), perm)
-    pieces = doubling_gather(moved, "row", ROW_BITS)
+    pieces = grouped_gather(moved, "row", n_row // Y_SIZE, Y_SIZE)
     cols_act = (
         pieces.reshape(groups, n_col, row_count, piece, channels)
         .transpose(0, 2, 1, 3, 4)

time: 104 us -> 111 us (1.067)
  waiting for transfers between devices: 23.6 us -> 31.1 us
  local copies, waits for them, and re-layouts: 10.2 us -> 12.9 us
  starting transfers between devices: 58.1 us -> 56.2 us
    ppermute x9 -> x0, starting transfers between devices: 52.6 us -> none  [doubling_gather(): lax.ppermute(gathered, axis, [(i, i ^ stride) for i in range(size)])]
    all_to_all x0 -> x3, starting transfers between devices: none -> 32.8 us  [the longest x1 18 us: shards(): blocks = lax.all_to_all(spread, 'col', 0, 0).transpose(1, 0, 2, 3)]
    all_to_all x0 -> x3, waiting for transfers between devices: none -> 30 us  [the longest x1 12.6 us: grouped_gather(): far = lax.all_to_all(spread, axis, 0, 0, axis_index_groups=outer_groups)]
    ppermute x9 -> x0, waiting for transfers between devices: 20.3 us -> none  [doubling_gather(): lax.ppermute(gathered, axis, [(i, i ^ stride) for i in range(size)])]
    ppermute x1, starting transfers between devices: 5.47 us -> 23.4 us  [shards(): moved = lax.ppermute(mine, ('row', 'col'), perm)]
    broadcast_in_dim x0 -> x3, local copies, waits for them, and re-layouts: none -> 3.04 us  [the longest x1 1.68 us: shards(): spread = jnp.broadcast_to(pair_act[None], (n_col,) + pair_act.shape)]
    ppermute x1, waiting for transfers between devices: 3.3 us -> 1.07 us  [shards(): moved = lax.ppermute(mine, ('row', 'col'), perm)]
    unnamed x23 -> x21, local copies, waits for them, and re-layouts: 4.3 us -> 4.73 us
  transfers between devices with their start and end apart: 10 -> 4, of which waited for: 9 -> 4; matrix products, arithmetic and copies ran while one was open for 5% -> 4% of each run, Pallas kernels for 0% -> 0%
where the time goes in v4:
time: 111 us
  starting transfers between devices  56.2 us (51%)
  waiting for transfers between devices  31.1 us (28%)
  local copies, waits for them, and re-layouts  12.9 us (12%)
  other arithmetic  4.3 us (4%)
  matrix products  4.3 us (4%)
  between operations  1.68 us (2%)
    ppermute x1, starting transfers between devices, shards(): moved = lax.ppermute(mine, ('row', 'col'), perm)  23.4 us
    all_to_all x1, starting transfers between devices, shards(): blocks = lax.all_to_all(spread, 'col', 0, 0).transpose(1, 0, 2, 3)  18 us
    all_to_all x1, waiting for transfers between devices, grouped_gather(): far = lax.all_to_all(spread, axis, 0, 0, axis_index_groups=outer_groups)  12.6 us
    all_to_all x1, waiting for transfers between devices, shards(): blocks = lax.all_to_all(spread, 'col', 0, 0).transpose(1, 0, 2, 3)  12.2 us
    all_to_all x1, starting transfers between devices, grouped_gather(): far = lax.all_to_all(spread, axis, 0, 0, axis_index_groups=outer_groups)  11.5 us
    all_to_all x1, waiting for transfers between devices, grouped_gather(): near = lax.all_to_all(spread, axis, 0, 0, axis_index_groups=inner_groups)  5.23 us
    unnamed x21, local copies, waits for them, and re-layouts  4.73 us
    all_to_all x1, starting transfers between devices, grouped_gather(): near = lax.all_to_all(spread, axis, 0, 0, axis_index_groups=inner_groups)  3.26 us
  transfers between devices with their start and end apart: 4, of which 4 were waited for; matrix products, arithmetic and copies ran while one was open for 4% of the time, Pallas kernels for 0%

profile of v4, /device:TPU:6, one launch (start us, length us, event | category | flops | bytes accessed | tf_op | source)
XLA Modules:
  0.0 110.5 jit_solution(12294815550108743633)
XLA Ops:
  0.6 1.7 %broadcast_in_dim.26 = bf16[16,8,16,128]{3,2,1,0:T(8,128)(2,1)} broadcast(bf16[8,16,128]{2,1,0:T(8,128)(2,1)} %param.10), dimensions={1,2,3} | broadcast | bytes 557056 | tf_op jit(solution)/shard_map/broadcast_in_dim | solution.py:104
  2.3 18.0 %all-to-all-start = ((bf16[16,8,16,128]{3,2,1,0:T(8,128)(2,1)}), bf16[16,8,16,128]{3,2,1,0:T(8,128)(2,1)S(1)}, u32[]{:S(2)}, u32[]{:S(2)}) async-start(bf16[16,8,16,128]{3,2,1,0:T(8,128)(2,1)} %broadcast_in_dim.26), calls=%async_computation | async-start | bytes 1048576 | tf_op jit(solution)/shard_map/all_to_all | solution.py:105
  21.1 0.1 add.330
  21.2 0.1 add.327
  21.3 0.7 copy-done.1
  22.0 0.8 gather_fusion.1
  22.8 0.1 convert_reduce_fusion.1
  22.9 0.2 fusion.56
  23.1 0.6 copy-done.8
  23.7 0.2 fusion.15
  23.9 0.1 reshape.349
  24.0 0.7 copy-done.5
  24.7 0.2 reshape.351
  24.9 0.8 gather_fusion
  25.8 0.2 copy.157
  26.3 12.2 %all-to-all-done = bf16[16,8,16,128]{3,2,1,0:T(8,128)(2,1)S(1)} async-done(((bf16[16,8,16,128]{3,2,1,0:T(8,128)(2,1)}), bf16[16,8,16,128]{3,2,1,0:T(8,128)(2,1)S(1)}, u32[]{:S(2)}, u32[]{:S(2)}) %all-to-all-start) | async-done | bytes 524320 | tf_op jit(solution)/shard_map/all_to_all | solution.py:105
  38.5 0.2 convert_reduce_fusion
  38.7 23.4 %collective-permute-start = (bf16[8,4,128]{2,1,0:T(4,128)(2,1)S(1)}, bf16[8,4,128]{2,1,0:T(4,128)(2,1)S(1)}, u32[]{:S(2)}, u32[]{:S(2)}) collective-permute-start(bf16[8,4,128]{2,1,0:T(4,128)(2,1)S(1)} %constant_dynamic-slice_fusion), channel_id=1, source_target_pairs={{0,0},{1,16},{2,32},{3,48},{4,64},{5,80},{6,96},{7,112},{8,128},{9... | collective-permute-start | bytes 24584 | tf_op jit(solution)/shard_map/ppermute | solution.py:115
  62.2 0.3 fusion.22
  62.4 1.1 collective-permute-done
  63.5 0.6 broadcast_in_dim.27
  64.1 3.3 %all-to-all-start.1 = ((bf16[4,8,4,128]{3,1,2,0:T(8,128)(2,1)}), bf16[4,8,4,128]{3,1,2,0:T(8,128)(2,1)S(1)}, u32[]{:S(2)}, u32[]{:S(2)}) async-start(bf16[4,8,4,128]{3,1,2,0:T(8,128)(2,1)} %broadcast_in_dim.27), calls=%async_computation.1 | async-start | bytes 65536 | tf_op jit(solution)/shard_map/all_to_all | solution.py:67
  67.4 0.1 div.33
  67.6 5.2 %all-to-all-done.1 = bf16[4,8,4,128]{3,1,2,0:T(8,128)(2,1)S(1)} async-done(((bf16[4,8,4,128]{3,1,2,0:T(8,128)(2,1)}), bf16[4,8,4,128]{3,1,2,0:T(8,128)(2,1)S(1)}, u32[]{:S(2)}, u32[]{:S(2)}) %all-to-all-start.1) | async-done | bytes 32800 | tf_op jit(solution)/shard_map/all_to_all | solution.py:67
  72.8 0.7 broadcast_in_dim.28
  73.5 11.5 %all-to-all-start.2 = ((bf16[8,4,8,4,128]{4,2,3,1,0:T(8,128)(2,1)}), bf16[8,4,8,4,128]{4,2,3,1,0:T(8,128)(2,1)S(1)}, u32[]{:S(2)}, u32[]{:S(2)}) async-start(bf16[8,4,8,4,128]{4,2,3,1,0:T(8,128)(2,1)} %broadcast_in_dim.28), calls=%async_computation.2 | async-start | bytes 524288 | tf_op jit(solution)/shard_map/all_to_all | solution.py:69
  85.1 0.3 convolution_convert_fusion
  85.5 0.2 copy.158
  85.7 0.2 copy.166
  85.8 0.7 copy-done.4
  86.6 0.3 fusion.53
  86.9 0.1 fusion.29
  87.0 0.2 copy.156
  87.2 12.6 %all-to-all-done.2 = bf16[8,4,8,4,128]{4,2,3,1,0:T(8,128)(2,1)S(1)} async-done(((bf16[8,4,8,4,128]{4,2,3,1,0:T(8,128)(2,1)}), bf16[8,4,8,4,128]{4,2,3,1,0:T(8,128)(2,1)S(1)}, u32[]{:S(2)}, u32[]{:S(2)}) %all-to-all-start.2) | async-done | bytes 262176 | tf_op jit(solution)/shard_map/all_to_all | solution.py:69
  99.8 0.3 fusion.23
  100.1 0.1 copy.149
  100.2 0.1 copy.151
  100.3 0.1 copy.150
  100.4 0.4 multiply_reduce_fusion
  100.8 0.1 copy.152
  101.0 0.1 copy.153
  101.1 0.1 rsqrt.31
  101.3 0.1 div.29
  101.4 0.3 multiply_convert_fusion
  101.7 0.3 copy-done.7
  102.1 0.7 fusion.14
  102.8 0.1 copy.160
  102.9 0.2 fusion.9
  103.1 0.6 slice_reduce_fusion.3
  103.7 0.9 fusion.36
  104.6 0.1 fusion.67
  104.8 0.1 fusion.74
  104.9 0.3 fusion.33
  105.3 0.5 fusion.10
  105.8 0.4 fusion.11
  106.3 0.4 fusion.12
  106.7 0.4 fusion.2
  107.1 0.1 copy.171
  107.2 0.8 reshape.353
  108.0 0.6 copy.173
  108.6 0.2 fusion.17
  108.8 0.4 copy.155
  109.3 0.4 fusion
  109.7 0.8 copy.172
  (39 shorter events, 0.9 us)
Async XLA Ops:
  0.6 84.4 %copy-start = (bf16[128,256]{1,0:T(8,128)(2,1)S(1)}, bf16[128,256]{1,0:T(8,128)(2,1)}, u32[]{:S(2)}) copy-start(bf16[128,256]{1,0:T(8,128)(2,1)} %param.15) | copy-start | bytes 196612
  2.3 36.1 %all-to-all-start = ((bf16[16,8,16,128]{3,2,1,0:T(8,128)(2,1)}), bf16[16,8,16,128]{3,2,1,0:T(8,128)(2,1)S(1)}, u32[]{:S(2)}, u32[]{:S(2)}) async-start(bf16[16,8,16,128]{3,2,1,0:T(8,128)(2,1)} %broadcast_in_dim.26), calls=%async_computation | async-start | bytes 1048576 | tf_op jit(solution)/shard_map/all_to_all | solution.py:105
  21.3 0.7 copy-start.1
  22.0 0.8 copy-start.2
  22.9 0.8 copy-start.8
  23.9 0.8 copy-start.5
  24.9 1.0 copy-start.6
  38.7 24.8 %collective-permute-start = (bf16[8,4,128]{2,1,0:T(4,128)(2,1)S(1)}, bf16[8,4,128]{2,1,0:T(4,128)(2,1)S(1)}, u32[]{:S(2)}, u32[]{:S(2)}) collective-permute-start(bf16[8,4,128]{2,1,0:T(4,128)(2,1)S(1)} %constant_dynamic-slice_fusion), channel_id=1, source_target_pairs={{0,0},{1,16},{2,32},{3,48},{4,64},{5,80},{6,96},{7,112},{8,128},{9... | collective-permute-start | bytes 24584 | tf_op jit(solution)/shard_map/ppermute | solution.py:115
  64.1 8.7 %all-to-all-start.1 = ((bf16[4,8,4,128]{3,1,2,0:T(8,128)(2,1)}), bf16[4,8,4,128]{3,1,2,0:T(8,128)(2,1)S(1)}, u32[]{:S(2)}, u32[]{:S(2)}) async-start(bf16[4,8,4,128]{3,1,2,0:T(8,128)(2,1)} %broadcast_in_dim.27), calls=%async_computation.1 | async-start | bytes 65536 | tf_op jit(solution)/shard_map/all_to_all | solution.py:67
  73.5 26.3 %all-to-all-start.2 = ((bf16[8,4,8,4,128]{4,2,3,1,0:T(8,128)(2,1)}), bf16[8,4,8,4,128]{4,2,3,1,0:T(8,128)(2,1)S(1)}, u32[]{:S(2)}, u32[]{:S(2)}) async-start(bf16[8,4,8,4,128]{4,2,3,1,0:T(8,128)(2,1)} %broadcast_in_dim.28), calls=%async_computation.2 | async-start | bytes 524288 | tf_op jit(solution)/shard_map/all_to_all | solution.py:69
  85.7 0.9 copy-start.4
  101.4 0.7 copy-start.7
  103.7 0.9 copy-start.3

commit v5 on v4

--- a/solution.py
+++ b/solution.py
@@ -113,7 +113,7 @@
         for src_col in range(n_col)
     ]
     moved = lax.ppermute(mine, ("row", "col"), perm)
-    pieces = grouped_gather(moved, "row", n_row // Y_SIZE, Y_SIZE)
+    pieces = doubling_gather(moved, "row", ROW_BITS)
     cols_act = (
         pieces.reshape(groups, n_col, row_count, piece, channels)
         .transpose(0, 2, 1, 3, 4)

time: 111 us -> 114 us (1.027); the launches traced: 111 us -> 112 us
  starting transfers between devices: 56.2 us -> 61.4 us
  waiting for transfers between devices: 31.1 us -> 28.5 us
  local copies, waits for them, and re-layouts: 12.9 us -> 11.3 us
    ppermute x0 -> x5, starting transfers between devices: none -> 20 us  [doubling_gather(): lax.ppermute(gathered, axis, [(i, i ^ stride) for i in range(size)])]
    all_to_all x2 -> x0, waiting for transfers between devices: 17.8 us -> none  [the longest x1 12.6 us: grouped_gather(): far = lax.all_to_all(spread, axis, 0, 0, axis_index_groups=outer_groups)]
    ppermute x0 -> x5, waiting for transfers between devices: none -> 16.3 us  [doubling_gather(): lax.ppermute(gathered, axis, [(i, i ^ stride) for i in range(size)])]
    all_to_all x2 -> x0, starting transfers between devices: 14.8 us -> none  [the longest x1 11.5 us: grouped_gather(): far = lax.all_to_all(spread, axis, 0, 0, axis_index_groups=outer_groups)]
    broadcast_in_dim x2 -> x0, local copies, waits for them, and re-layouts: 1.36 us -> none  [the longest x1 0.73 us: grouped_gather(): spread = jnp.broadcast_to(near[None], (outer,) + near.shape)]
    unnamed x21 -> x22, local copies, waits for them, and re-layouts: 4.73 us -> 5.51 us
  transfers between devices with their start and end apart: 4 -> 7, of which waited for: 4 -> 6; matrix products, arithmetic and copies ran while one was open for 4% -> 4% of each run, Pallas kernels for 0% -> 0%
where the time goes in v5:
time: 114 us; the launch traced here: 112 us
  starting transfers between devices  61.4 us (54%)
  waiting for transfers between devices  28.5 us (25%)
  local copies, waits for them, and re-layouts  11.3 us (10%)
  other arithmetic  4.53 us (4%)
  matrix products  4.06 us (4%)
  between operations  1.82 us (2%)
    ppermute x1, starting transfers between devices, shards(): moved = lax.ppermute(mine, ('row', 'col'), perm)  23.4 us
    ppermute x5, starting transfers between devices, doubling_gather(): lax.ppermute(gathered, axis, [(i, i ^ stride) for i in range(size)])  20 us
    all_to_all x1, starting transfers between devices, shards(): blocks = lax.all_to_all(spread, 'col', 0, 0).transpose(1, 0, 2, 3)  18 us
    ppermute x5, waiting for transfers between devices, doubling_gather(): lax.ppermute(gathered, axis, [(i, i ^ stride) for i in range(size)])  16.3 us
    all_to_all x1, waiting for transfers between devices, shards(): blocks = lax.all_to_all(spread, 'col', 0, 0).transpose(1, 0, 2, 3)  12.1 us
    unnamed x22, local copies, waits for them, and re-layouts  5.51 us
  transfers between devices with their start and end apart: 7, of which 6 were waited for; matrix products, arithmetic and copies ran while one was open for 4% of the time, Pallas kernels for 0%

profile of v5, /device:TPU:6, one launch (start us, length us, event | category | flops | bytes accessed | tf_op | source)
XLA Modules:
  0.0 111.7 jit_solution(8793422669392833644)
XLA Ops:
  0.6 0.8 copy.139
  1.4 0.9 broadcast_in_dim.24
  2.3 18.0 %all-to-all-start = ((bf16[16,8,16,128]{3,1,2,0:T(8,128)(2,1)}), bf16[16,8,16,128]{3,1,2,0:T(8,128)(2,1)S(1)}, u32[]{:S(2)}, u32[]{:S(2)}) async-start(bf16[16,8,16,128]{3,1,2,0:T(8,128)(2,1)} %broadcast_in_dim.24), calls=%async_computation | async-start | bytes 1048576 | tf_op jit(solution)/shard_map/all_to_all | solution.py:105
  21.3 0.7 copy-done.1
  22.0 0.8 gather_fusion.1
  22.8 0.1 convert_reduce_fusion.1
  23.0 0.2 fusion.58
  23.1 0.6 copy-done.8
  23.7 0.2 fusion.15
  23.9 0.1 reshape.1391
  24.0 0.7 copy-done.5
  24.8 0.2 reshape.1393
  24.9 0.8 gather_fusion
  25.9 0.2 copy.154
  26.3 12.1 %all-to-all-done = bf16[16,8,16,128]{3,1,2,0:T(8,128)(2,1)S(1)} async-done(((bf16[16,8,16,128]{3,1,2,0:T(8,128)(2,1)}), bf16[16,8,16,128]{3,1,2,0:T(8,128)(2,1)S(1)}, u32[]{:S(2)}, u32[]{:S(2)}) %all-to-all-start) | async-done | bytes 524320 | tf_op jit(solution)/shard_map/all_to_all | solution.py:105
  38.5 0.2 convert_reduce_fusion
  38.7 0.3 fusion.22
  39.0 23.4 %collective-permute-start = (bf16[8,4,128]{2,0,1:T(8,128)(2,1)S(1)}, bf16[8,4,128]{2,0,1:T(8,128)(2,1)S(1)}, u32[]{:S(2)}, u32[]{:S(2)}) collective-permute-start(bf16[8,4,128]{2,0,1:T(8,128)(2,1)S(1)} %constant_dynamic-slice_fusion), channel_id=1, source_target_pairs={{0,0},{1,16},{2,32},{3,48},{4,64},{5,80},{6,96},{7,112},{8,128},{9... | collective-permute-start | bytes 24584 | tf_op jit(solution)/shard_map/ppermute | solution.py:115
  62.4 0.2 multiply_convert_fusion.1
  62.6 0.7 copy-done.4
  63.3 0.2 fusion.54
  63.5 0.2 convolution_convert_fusion
  63.7 2.6 %collective-permute-start.1 = (bf16[1,8,4,128]{3,1,2,0:T(8,128)(2,1)S(1)}, bf16[1,8,4,128]{3,1,2,0:T(8,128)(2,1)S(1)}, u32[]{:S(2)}, u32[]{:S(2)}) collective-permute-start(bf16[1,8,4,128]{3,1,2,0:T(8,128)(2,1)S(1)} %bitcast.253), channel_id=1, source_target_pairs={{0,256},{16,272},{32,288},{48,304},{64,320},{80,336},{96,352},{112... | collective-permute-start | bytes 24584 | tf_op jit(solution)/shard_map/ppermute | solution.py:55
  66.3 0.1 fusion.28
  66.4 6.7 %collective-permute-done.1 = bf16[1,8,4,128]{3,1,2,0:T(8,128)(2,1)S(1)} collective-permute-done((bf16[1,8,4,128]{3,1,2,0:T(8,128)(2,1)S(1)}, bf16[1,8,4,128]{3,1,2,0:T(8,128)(2,1)S(1)}, u32[]{:S(2)}, u32[]{:S(2)}) %collective-permute-start.1) | collective-permute-done | bytes 8224 | tf_op jit(solution)/shard_map/ppermute | solution.py:55
  73.2 4.5 %collective-permute-start.2 = (bf16[2,1,8,4,128]{4,2,3,0,1:T(8,128)(2,1)S(1)}, bf16[2,1,8,4,128]{4,2,3,0,1:T(8,128)(2,1)S(1)}, u32[]{:S(2)}, u32[]{:S(2)}) collective-permute-start(bf16[2,1,8,4,128]{4,2,3,0,1:T(8,128)(2,1)S(1)} %fusion.69), channel_id=1, source_target_pairs={{0,128},{16,144},{32,160},{48,176},{64,192},{80,208},{96,224},{112... | collective-permute-start | bytes 49160 | tf_op jit(solution)/shard_map/ppermute | solution.py:55
  77.7 2.0 %collective-permute-done.2 = bf16[2,1,8,4,128]{4,2,3,0,1:T(8,128)(2,1)S(1)} collective-permute-done((bf16[2,1,8,4,128]{4,2,3,0,1:T(8,128)(2,1)S(1)}, bf16[2,1,8,4,128]{4,2,3,0,1:T(8,128)(2,1)S(1)}, u32[]{:S(2)}, u32[]{:S(2)}) %collective-permute-start.2) | collective-permute-done | bytes 16416 | tf_op jit(solution)/shard_map/ppermute | solution.py:55
  79.7 5.8 %collective-permute-start.3 = (bf16[2,2,1,8,4,128]{5,3,4,0,1,2:T(8,128)(2,1)S(1)}, bf16[2,2,1,8,4,128]{5,3,4,0,1,2:T(8,128)(2,1)S(1)}, u32[]{:S(2)}, u32[]{:S(2)}) collective-permute-start(bf16[2,2,1,8,4,128]{5,3,4,0,1,2:T(8,128)(2,1)S(1)} %copy.141), channel_id=1, source_target_pairs={{0,32},{16,48},{32,0},{48,16},{64,96},{80,112},{96,64},{112,80},{1... | collective-permute-start | bytes 98312 | tf_op jit(solution)/shard_map/ppermute | solution.py:55
  85.5 1.9 %collective-permute-done.3 = bf16[2,2,1,8,4,128]{5,3,4,0,1,2:T(8,128)(2,1)S(1)} collective-permute-done((bf16[2,2,1,8,4,128]{5,3,4,0,1,2:T(8,128)(2,1)S(1)}, bf16[2,2,1,8,4,128]{5,3,4,0,1,2:T(8,128)(2,1)S(1)}, u32[]{:S(2)}, u32[]{:S(2)}) %collective-permute-start.3) | collective-permute-done | bytes 32800 | tf_op jit(solution)/shard_map/ppermute | solution.py:55
  87.4 4.5 %collective-permute-start.4 = (bf16[2,2,2,1,8,4,128]{6,4,5,0,1,2,3:T(8,128)(2,1)S(1)}, bf16[2,2,2,1,8,4,128]{6,4,5,0,1,2,3:T(8,128)(2,1)S(1)}, u32[]{:S(2)}, u32[]{:S(2)}) collective-permute-start(bf16[2,2,2,1,8,4,128]{6,4,5,0,1,2,3:T(8,128)(2,1)S(1)} %copy.142), channel_id=1, source_target_pairs={{0,64},{16,80},{32,96},{48,112},{64,0},{80,16},{96,32},{112,48},{1... | collective-permute-start | bytes 196616 | tf_op jit(solution)/shard_map/ppermute | solution.py:55
  91.9 2.2 %collective-permute-done.4 = bf16[2,2,2,1,8,4,128]{6,4,5,0,1,2,3:T(8,128)(2,1)S(1)} collective-permute-done((bf16[2,2,2,1,8,4,128]{6,4,5,0,1,2,3:T(8,128)(2,1)S(1)}, bf16[2,2,2,1,8,4,128]{6,4,5,0,1,2,3:T(8,128)(2,1)S(1)}, u32[]{:S(2)}, u32[]{:S(2)}) %collective-permute-start.4) | collective-permute-done | bytes 65568 | tf_op jit(solution)/shard_map/ppermute | solution.py:55
  94.2 2.6 %collective-permute-start.5 = (bf16[2,2,2,2,1,8,4,128]{7,5,6,1,0,2,3,4:T(8,128)(2,1)S(1)}, bf16[2,2,2,2,1,8,4,128]{7,5,6,1,0,2,3,4:T(8,128)(2,1)S(1)}, u32[]{:S(2)}, u32[]{:S(2)}) collective-permute-start(bf16[2,2,2,2,1,8,4,128]{7,5,6,1,0,2,3,4:T(8,128)(2,1)S(1)} %maximum_select_fusion.2), channel_id=1, source_target_pairs={{0,16},{16,0},{32,48},{48,32},{64,80},{80,64},{96,112},{112,96},{1... | collective-permute-start | bytes 393224 | tf_op jit(solution)/shard_map/ppermute | solution.py:55
  96.9 0.2 copy.156
  97.0 0.2 copy.164
  97.2 0.2 copy.153
  97.5 3.5 %collective-permute-done.5 = bf16[2,2,2,2,1,8,4,128]{7,5,6,1,0,2,3,4:T(8,128)(2,1)S(1)} collective-permute-done((bf16[2,2,2,2,1,8,4,128]{7,5,6,1,0,2,3,4:T(8,128)(2,1)S(1)}, bf16[2,2,2,2,1,8,4,128]{7,5,6,1,0,2,3,4:T(8,128)(2,1)S(1)}, u32[]{:S(2)}, u32[]{:S(2)}) %collective-permute-start.5) | collective-permute-done | bytes 131104 | tf_op jit(solution)/shard_map/ppermute | solution.py:55
  101.1 0.3 reduce_sum.90
  101.4 0.1 copy.147
  101.6 0.1 copy.146
  101.7 0.4 multiply_reduce_fusion
  102.2 0.1 copy.149
  102.3 0.1 rsqrt.31
  102.4 0.1 div.71
  102.5 0.3 multiply_convert_fusion
  102.9 0.3 copy-done.7
  103.2 0.7 fusion.14
  103.9 0.1 copy.158
  104.0 0.2 fusion.9
  104.2 0.6 slice_reduce_fusion.3
  104.9 0.9 fusion.36
  105.8 0.1 fusion.70
  105.9 0.1 fusion.77
  106.1 0.3 fusion.33
  106.4 0.5 fusion.10
  107.0 0.4 fusion.11
  107.4 0.4 fusion.12
  107.9 0.4 fusion.2
  108.3 0.1 copy.169
  108.4 0.8 reshape.1395
  109.2 0.6 copy.171
  109.8 0.2 fusion.17
  110.0 0.4 copy.152
  110.4 0.4 fusion
  110.8 0.8 copy.170
  (51 shorter events, 1.2 us)
Async XLA Ops:
  0.6 62.9 %copy-start = (bf16[128,256]{1,0:T(8,128)(2,1)S(1)}, bf16[128,256]{1,0:T(8,128)(2,1)}, u32[]{:S(2)}) copy-start(bf16[128,256]{1,0:T(8,128)(2,1)} %param.15) | copy-start | bytes 196612
  2.3 36.1 %all-to-all-start = ((bf16[16,8,16,128]{3,1,2,0:T(8,128)(2,1)}), bf16[16,8,16,128]{3,1,2,0:T(8,128)(2,1)S(1)}, u32[]{:S(2)}, u32[]{:S(2)}) async-start(bf16[16,8,16,128]{3,1,2,0:T(8,128)(2,1)} %broadcast_in_dim.24), calls=%async_computation | async-start | bytes 1048576 | tf_op jit(solution)/shard_map/all_to_all | solution.py:105
  21.3 0.7 copy-start.1
  22.0 0.8 copy-start.2
  22.9 0.8 copy-start.8
  23.9 0.8 copy-start.5
  24.9 1.0 copy-start.6
  39.0 24.8 %collective-permute-start = (bf16[8,4,128]{2,0,1:T(8,128)(2,1)S(1)}, bf16[8,4,128]{2,0,1:T(8,128)(2,1)S(1)}, u32[]{:S(2)}, u32[]{:S(2)}) collective-permute-start(bf16[8,4,128]{2,0,1:T(8,128)(2,1)S(1)} %constant_dynamic-slice_fusion), channel_id=1, source_target_pairs={{0,0},{1,16},{2,32},{3,48},{4,64},{5,80},{6,96},{7,112},{8,128},{9... | collective-permute-start | bytes 24584 | tf_op jit(solution)/shard_map/ppermute | solution.py:115
  62.4 0.9 copy-start.4
  63.7 9.5 %collective-permute-start.1 = (bf16[1,8,4,128]{3,1,2,0:T(8,128)(2,1)S(1)}, bf16[1,8,4,128]{3,1,2,0:T(8,128)(2,1)S(1)}, u32[]{:S(2)}, u32[]{:S(2)}) collective-permute-start(bf16[1,8,4,128]{3,1,2,0:T(8,128)(2,1)S(1)} %bitcast.253), channel_id=1, source_target_pairs={{0,256},{16,272},{32,288},{48,304},{64,320},{80,336},{96,352},{112... | collective-permute-start | bytes 24584 | tf_op jit(solution)/shard_map/ppermute | solution.py:55
  73.2 6.5 %collective-permute-start.2 = (bf16[2,1,8,4,128]{4,2,3,0,1:T(8,128)(2,1)S(1)}, bf16[2,1,8,4,128]{4,2,3,0,1:T(8,128)(2,1)S(1)}, u32[]{:S(2)}, u32[]{:S(2)}) collective-permute-start(bf16[2,1,8,4,128]{4,2,3,0,1:T(8,128)(2,1)S(1)} %fusion.69), channel_id=1, source_target_pairs={{0,128},{16,144},{32,160},{48,176},{64,192},{80,208},{96,224},{112... | collective-permute-start | bytes 49160 | tf_op jit(solution)/shard_map/ppermute | solution.py:55
  79.7 7.6 %collective-permute-start.3 = (bf16[2,2,1,8,4,128]{5,3,4,0,1,2:T(8,128)(2,1)S(1)}, bf16[2,2,1,8,4,128]{5,3,4,0,1,2:T(8,128)(2,1)S(1)}, u32[]{:S(2)}, u32[]{:S(2)}) collective-permute-start(bf16[2,2,1,8,4,128]{5,3,4,0,1,2:T(8,128)(2,1)S(1)} %copy.141), channel_id=1, source_target_pairs={{0,32},{16,48},{32,0},{48,16},{64,96},{80,112},{96,64},{112,80},{1... | collective-permute-start | bytes 98312 | tf_op jit(solution)/shard_map/ppermute | solution.py:55
  87.4 6.7 %collective-permute-start.4 = (bf16[2,2,2,1,8,4,128]{6,4,5,0,1,2,3:T(8,128)(2,1)S(1)}, bf16[2,2,2,1,8,4,128]{6,4,5,0,1,2,3:T(8,128)(2,1)S(1)}, u32[]{:S(2)}, u32[]{:S(2)}) collective-permute-start(bf16[2,2,2,1,8,4,128]{6,4,5,0,1,2,3:T(8,128)(2,1)S(1)} %copy.142), channel_id=1, source_target_pairs={{0,64},{16,80},{32,96},{48,112},{64,0},{80,16},{96,32},{112,48},{1... | collective-permute-start | bytes 196616 | tf_op jit(solution)/shard_map/ppermute | solution.py:55
  94.2 6.9 %collective-permute-start.5 = (bf16[2,2,2,2,1,8,4,128]{7,5,6,1,0,2,3,4:T(8,128)(2,1)S(1)}, bf16[2,2,2,2,1,8,4,128]{7,5,6,1,0,2,3,4:T(8,128)(2,1)S(1)}, u32[]{:S(2)}, u32[]{:S(2)}) collective-permute-start(bf16[2,2,2,2,1,8,4,128]{7,5,6,1,0,2,3,4:T(8,128)(2,1)S(1)} %maximum_select_fusion.2), channel_id=1, source_target_pairs={{0,16},{16,0},{32,48},{48,32},{64,80},{80,64},{96,112},{112,96},{1... | collective-permute-start | bytes 393224 | tf_op jit(solution)/shard_map/ppermute | solution.py:55
  102.5 0.7 copy-start.7
  104.9 0.9 copy-start.3

commit v6 on v5

--- a/solution.py
+++ b/solution.py
@@ -101,24 +101,36 @@
     row_mask = lax.dynamic_slice_in_dim(mask_float, row_index * row_count, row_count)
     col_mask = lax.dynamic_slice_in_dim(mask_float, col_index * col_width, col_width)
 
-    spread = jnp.broadcast_to(pair_act[None], (n_col,) + pair_act.shape)
-    blocks = lax.all_to_all(spread, "col", 0, 0).transpose(1, 0, 2, 3)
-    doubled = jnp.concatenate([blocks, blocks[:, :STEPS]], axis=1)
-    rows_act = lax.dynamic_slice_in_dim(doubled, start, STEPS, axis=1).reshape(row_count, window, channels)
+    partner = lax.ppermute(pair_act, "row", [(i, i ^ 1) for i in range(n_row)])
+    odd = row_index % 2 == 1
+    tile = jnp.where(odd, jnp.concatenate([partner, pair_act]), jnp.concatenate([pair_act, partner]))
 
-    mine = lax.dynamic_slice_in_dim(rows_act, col_index * piece, piece, axis=1)
+    def in_window(col):
+        return (col - start) % n_col < STEPS
+
+    received = lax.ppermute(tile, "col", [(i, i ^ 8) for i in range(n_col)])
+    held = jnp.where(in_window(col_index), tile, received)
+    mine_ok = in_window(col_index) | in_window(col_index ^ 8)
+    received = lax.ppermute(held, "col", [(i, i ^ 4) for i in range(n_col)])
+    held = jnp.where(mine_ok, held, received)
+    received = lax.ppermute(held, "col", [(i, i ^ 2) for i in range(n_col)])
+    first = ((col_index - start) % 4) // 2 == 0
+    pair = jnp.where(first, jnp.stack([held, received]), jnp.stack([received, held]))
+    received = lax.ppermute(pair, "col", [(i, i ^ 1) for i in range(n_col)])
+    even = (col_index - start) % 2 == 0
+    tiles = jnp.where(even, jnp.stack([pair, received], axis=1), jnp.stack([received, pair], axis=1))
+    tiles = tiles.reshape((STEPS,) + tile.shape)
+
+    rows_act = lax.dynamic_slice_in_dim(tiles, (row_index % groups) * row_count, row_count, axis=1)
+    rows_act = rows_act.transpose(1, 0, 2, 3).reshape(row_count, window, channels)
+
     perm = [
         (src_row * n_col + src_col, ((src_row % groups) * n_col + src_col) * n_col + src_row // groups)
         for src_row in range(n_row)
         for src_col in range(n_col)
     ]
-    moved = lax.ppermute(mine, ("row", "col"), perm)
-    pieces = doubling_gather(moved, "row", ROW_BITS)
-    cols_act = (
-        pieces.reshape(groups, n_col, row_count, piece, channels)
-        .transpose(0, 2, 1, 3, 4)
-        .reshape(groups * row_count, window, channels)
-    )
+    moved = lax.ppermute(tiles, ("row", "col"), perm)
+    cols_act = moved.transpose(1, 0, 2, 3).reshape(groups * row_count, window, channels)
 
     normed = layer_norm(pair_act)
     queries = (project(normed, query_weight) * (1.0 / math.sqrt(HEAD_DIM))).astype(jnp.bfloat16)

time: 114 us -> 97.5 us (0.86)
  the two profiles are of different devices: /device:TPU:6 before, /device:TPU:97 now
where the time goes in v6:
time: 97.5 us; the launch traced here: 96.9 us
  waiting for transfers between devices  40 us (41%)
  starting transfers between devices  36.4 us (37%)
  local copies, waits for them, and re-layouts  9.74 us (10%)
  other arithmetic  5.23 us (5%)
  matrix products  3.66 us (4%)
  between operations  1.86 us (2%)
    ppermute x1, waiting for transfers between devices, shards(): moved = lax.ppermute(tiles, ('row', 'col'), perm)  35.1 us
    ppermute x1, starting transfers between devices, shards(): received = lax.ppermute(tile, 'col', [(i, i ^ 8) for i in range(n_col)])  12.7 us
    ppermute x1, starting transfers between devices, shards(): received = lax.ppermute(pair, 'col', [(i, i ^ 1) for i in range(n_col)])  7.98 us
    unnamed x21, local copies, waits for them, and re-layouts  5.18 us
    ppermute x1, starting transfers between devices, shards(): received = lax.ppermute(held, 'col', [(i, i ^ 4) for i in range(n_col)])  4.65 us
    ppermute x1, starting transfers between devices, shards(): moved = lax.ppermute(tiles, ('row', 'col'), perm)  4.61 us
    ppermute x1, starting transfers between devices, shards(): partner = lax.ppermute(pair_act, 'row', [(i, i ^ 1) for i in range(n_row)])  3.34 us
    ppermute x1, starting transfers between devices, shards(): received = lax.ppermute(held, 'col', [(i, i ^ 2) for i in range(n_col)])  3.12 us
  transfers between devices with their start and end apart: 6, of which 4 were waited for; matrix products, arithmetic and copies ran while one was open for 6% of the time, Pallas kernels for 0%

profile of v6, /device:TPU:97, one launch (start us, length us, event | category | flops | bytes accessed | tf_op | source)
XLA Modules:
  0.0 96.9 jit_solution(12567359862505999281)
XLA Ops:
  0.6 3.3 %collective-permute-start = (bf16[8,16,128]{2,1,0:T(8,128)(2,1)}, bf16[8,16,128]{2,1,0:T(8,128)(2,1)S(1)}, u32[]{:S(2)}, u32[]{:S(2)}) collective-permute-start(bf16[8,16,128]{2,1,0:T(8,128)(2,1)} %param.10), channel_id=1, source_target_pairs={{0,16},{16,0},{32,48},{48,32},{64,80},{80,64},{96,112},{112,96},{1... | collective-permute-start | bytes 98312 | tf_op jit(solution)/shard_map/ppermute | solution.py:104
  4.7 0.9 convert_reduce_fusion
  5.7 0.1 add.348
  5.8 0.2 fusion.55
  6.0 0.4 copy-done.8
  6.3 0.2 fusion.13
  6.6 0.1 add.345
  6.7 0.7 copy-done.1
  7.3 0.8 gather_fusion
  8.2 12.7 %collective-permute-start.1 = (bf16[16,16,128]{2,1,0:T(8,128)(2,1)S(1)}, bf16[16,16,128]{2,1,0:T(8,128)(2,1)S(1)}, u32[]{:S(2)}, u32[]{:S(2)}) collective-permute-start(bf16[16,16,128]{2,1,0:T(8,128)(2,1)S(1)} %maximum_select_fusion.3), channel_id=1, source_target_pairs={{0,8},{1,9},{2,10},{3,11},{4,12},{5,13},{6,14},{7,15},{8,0},{9,1},... | collective-permute-start | bytes 196616 | tf_op jit(solution)/shard_map/ppermute | solution.py:111
  20.9 0.1 dynamic_slice.9
  21.0 1.6 %collective-permute-done.1 = bf16[16,16,128]{2,1,0:T(8,128)(2,1)S(1)} collective-permute-done((bf16[16,16,128]{2,1,0:T(8,128)(2,1)S(1)}, bf16[16,16,128]{2,1,0:T(8,128)(2,1)S(1)}, u32[]{:S(2)}, u32[]{:S(2)}) %collective-permute-start.1) | collective-permute-done | bytes 65568 | tf_op jit(solution)/shard_map/ppermute | solution.py:111
  22.6 4.7 %collective-permute-start.2 = (bf16[16,16,128]{2,1,0:T(8,128)(2,1)S(1)}, bf16[16,16,128]{2,1,0:T(8,128)(2,1)S(1)}, u32[]{:S(2)}, u32[]{:S(2)}) collective-permute-start(bf16[16,16,128]{2,1,0:T(8,128)(2,1)S(1)} %broadcast_select_fusion), channel_id=1, source_target_pairs={{0,4},{1,5},{2,6},{3,7},{4,0},{5,1},{6,2},{7,3},{8,12},{9,13},{10,... | collective-permute-start | bytes 196616 | tf_op jit(solution)/shard_map/ppermute | solution.py:114
  27.3 0.1 broadcast_multiply_fusion.2
  27.3 0.1 dynamic_slice.11
  27.4 1.7 %collective-permute-done.2 = bf16[16,16,128]{2,1,0:T(8,128)(2,1)S(1)} collective-permute-done((bf16[16,16,128]{2,1,0:T(8,128)(2,1)S(1)}, bf16[16,16,128]{2,1,0:T(8,128)(2,1)S(1)}, u32[]{:S(2)}, u32[]{:S(2)}) %collective-permute-start.2) | collective-permute-done | bytes 65568 | tf_op jit(solution)/shard_map/ppermute | solution.py:114
  29.1 3.1 %collective-permute-start.3 = (bf16[16,16,128]{2,1,0:T(8,128)(2,1)S(1)}, bf16[16,16,128]{2,1,0:T(8,128)(2,1)S(1)}, u32[]{:S(2)}, u32[]{:S(2)}) collective-permute-start(bf16[16,16,128]{2,1,0:T(8,128)(2,1)S(1)} %broadcast_select_fusion.1), channel_id=1, source_target_pairs={{0,2},{1,3},{2,0},{3,1},{4,6},{5,7},{6,4},{7,5},{8,10},{9,11},{10,... | collective-permute-start | bytes 196616 | tf_op jit(solution)/shard_map/ppermute | solution.py:116
  32.3 0.8 gather_fusion.1
  33.1 1.6 %collective-permute-done.3 = bf16[16,16,128]{2,1,0:T(8,128)(2,1)S(1)} collective-permute-done((bf16[16,16,128]{2,1,0:T(8,128)(2,1)S(1)}, bf16[16,16,128]{2,1,0:T(8,128)(2,1)S(1)}, u32[]{:S(2)}, u32[]{:S(2)}) %collective-permute-start.3) | collective-permute-done | bytes 65568 | tf_op jit(solution)/shard_map/ppermute | solution.py:116
  34.8 8.0 %collective-permute-start.4 = (bf16[2,16,16,128]{3,2,1,0:T(8,128)(2,1)S(1)}, bf16[2,16,16,128]{3,2,1,0:T(8,128)(2,1)S(1)}, u32[]{:S(2)}, u32[]{:S(2)}) collective-permute-start(bf16[2,16,16,128]{3,2,1,0:T(8,128)(2,1)S(1)} %maximum_select_fusion.2), channel_id=1, source_target_pairs={{0,1},{1,0},{2,3},{3,2},{4,5},{5,4},{6,7},{7,6},{8,9},{9,8},{10,11... | collective-permute-start | bytes 393224 | tf_op jit(solution)/shard_map/ppermute | solution.py:119
  42.8 0.1 reshape.405
  42.9 0.7 copy-done.5
  43.6 0.2 reshape.407
  43.8 0.7 copy-done.6
  44.5 0.2 copy.100
  44.8 0.1 fusion.47
  45.0 0.3 multiply_reduce_fusion.1
  45.3 4.6 %collective-permute-start.5 = (bf16[4,16,16,128]{3,2,1,0:T(8,128)(2,1)S(1)}, bf16[4,16,16,128]{3,2,1,0:T(8,128)(2,1)S(1)}, u32[]{:S(2)}, u32[]{:S(2)}) collective-permute-start(bf16[4,16,16,128]{3,2,1,0:T(8,128)(2,1)S(1)} %bitcast.227), channel_id=1, source_target_pairs={{0,0},{1,16},{2,32},{3,48},{4,64},{5,80},{6,96},{7,112},{8,128},{9... | collective-permute-start | bytes 786440 | tf_op jit(solution)/shard_map/ppermute | solution.py:132
  49.9 0.1 rsqrt.33
  50.0 0.1 div.44
  50.1 0.2 fusion.34
  50.3 0.2 convolution_convert_fusion
  50.6 0.7 copy-done.4
  51.2 0.2 fusion.58
  51.5 0.2 copy.101
  51.7 0.2 copy.109
  51.9 0.1 fusion.29
  52.0 0.2 copy.99
  52.2 35.1 %collective-permute-done.5 = bf16[4,16,16,128]{3,2,1,0:T(8,128)(2,1)S(1)} collective-permute-done((bf16[4,16,16,128]{3,2,1,0:T(8,128)(2,1)S(1)}, bf16[4,16,16,128]{3,2,1,0:T(8,128)(2,1)S(1)}, u32[]{:S(2)}, u32[]{:S(2)}) %collective-permute-start.5) | collective-permute-done | bytes 262176 | tf_op jit(solution)/shard_map/ppermute | solution.py:132
  87.4 0.2 fusion.23
  87.6 0.4 multiply_reduce_fusion
  88.0 0.1 rsqrt.31
  88.2 0.1 div.40
  88.3 0.3 fusion.22
  88.6 0.3 copy-done.7
  89.0 0.3 fusion.15
  89.3 0.2 fusion.9
  89.5 0.6 slice_reduce_fusion.3
  90.2 0.9 fusion.36
  91.0 0.1 fusion.68
  91.2 0.1 fusion.75
  91.3 0.3 fusion.60
  91.6 0.1 fusion.69
  91.7 0.5 fusion.10
  92.2 0.4 fusion.11
  92.7 0.5 fusion.12
  93.1 0.4 fusion.2
  93.6 0.1 copy.114
  93.7 0.8 reshape.409
  94.5 0.6 copy.116
  95.1 0.2 fusion.17
  95.3 0.4 copy.98
  95.7 0.4 fusion
  96.1 0.8 copy.115
  (44 shorter events, 0.6 us)
Async XLA Ops:
  0.6 49.7 %copy-start = (bf16[128,256]{1,0:T(8,128)(2,1)S(1)}, bf16[128,256]{1,0:T(8,128)(2,1)}, u32[]{:S(2)}) copy-start(bf16[128,256]{1,0:T(8,128)(2,1)} %param.15) | copy-start | bytes 196612
  0.6 7.5 %collective-permute-start = (bf16[8,16,128]{2,1,0:T(8,128)(2,1)}, bf16[8,16,128]{2,1,0:T(8,128)(2,1)S(1)}, u32[]{:S(2)}, u32[]{:S(2)}) collective-permute-start(bf16[8,16,128]{2,1,0:T(8,128)(2,1)} %param.10), channel_id=1, source_target_pairs={{0,16},{16,0},{32,48},{48,32},{64,80},{80,64},{96,112},{112,96},{1... | collective-permute-start | bytes 98312 | tf_op jit(solution)/shard_map/ppermute | solution.py:104
  4.6 1.1 %copy-start.2 = (bf16[8,16,128]{2,1,0:T(8,128)(2,1)S(1)}, bf16[8,16,128]{2,1,0:T(8,128)(2,1)}, u32[]{:S(2)}) copy-start(bf16[8,16,128]{2,1,0:T(8,128)(2,1)} %param.10) | copy-start | bytes 98308
  5.6 0.8 copy-start.8
  6.7 0.7 copy-start.1
  8.2 14.4 %collective-permute-start.1 = (bf16[16,16,128]{2,1,0:T(8,128)(2,1)S(1)}, bf16[16,16,128]{2,1,0:T(8,128)(2,1)S(1)}, u32[]{:S(2)}, u32[]{:S(2)}) collective-permute-start(bf16[16,16,128]{2,1,0:T(8,128)(2,1)S(1)} %maximum_select_fusion.3), channel_id=1, source_target_pairs={{0,8},{1,9},{2,10},{3,11},{4,12},{5,13},{6,14},{7,15},{8,0},{9,1},... | collective-permute-start | bytes 196616 | tf_op jit(solution)/shard_map/ppermute | solution.py:111
  22.6 6.5 %collective-permute-start.2 = (bf16[16,16,128]{2,1,0:T(8,128)(2,1)S(1)}, bf16[16,16,128]{2,1,0:T(8,128)(2,1)S(1)}, u32[]{:S(2)}, u32[]{:S(2)}) collective-permute-start(bf16[16,16,128]{2,1,0:T(8,128)(2,1)S(1)} %broadcast_select_fusion), channel_id=1, source_target_pairs={{0,4},{1,5},{2,6},{3,7},{4,0},{5,1},{6,2},{7,3},{8,12},{9,13},{10,... | collective-permute-start | bytes 196616 | tf_op jit(solution)/shard_map/ppermute | solution.py:114
  29.1 5.6 %collective-permute-start.3 = (bf16[16,16,128]{2,1,0:T(8,128)(2,1)S(1)}, bf16[16,16,128]{2,1,0:T(8,128)(2,1)S(1)}, u32[]{:S(2)}, u32[]{:S(2)}) collective-permute-start(bf16[16,16,128]{2,1,0:T(8,128)(2,1)S(1)} %broadcast_select_fusion.1), channel_id=1, source_target_pairs={{0,2},{1,3},{2,0},{3,1},{4,6},{5,7},{6,4},{7,5},{8,10},{9,11},{10,... | collective-permute-start | bytes 196616 | tf_op jit(solution)/shard_map/ppermute | solution.py:116
  34.8 10.0 %collective-permute-start.4 = (bf16[2,16,16,128]{3,2,1,0:T(8,128)(2,1)S(1)}, bf16[2,16,16,128]{3,2,1,0:T(8,128)(2,1)S(1)}, u32[]{:S(2)}, u32[]{:S(2)}) collective-permute-start(bf16[2,16,16,128]{3,2,1,0:T(8,128)(2,1)S(1)} %maximum_select_fusion.2), channel_id=1, source_target_pairs={{0,1},{1,0},{2,3},{3,2},{4,5},{5,4},{6,7},{7,6},{8,9},{9,8},{10,11... | collective-permute-start | bytes 393224 | tf_op jit(solution)/shard_map/ppermute | solution.py:119
  42.8 0.8 copy-start.5
  43.6 0.8 copy-start.6
  45.3 42.1 %collective-permute-start.5 = (bf16[4,16,16,128]{3,2,1,0:T(8,128)(2,1)S(1)}, bf16[4,16,16,128]{3,2,1,0:T(8,128)(2,1)S(1)}, u32[]{:S(2)}, u32[]{:S(2)}) collective-permute-start(bf16[4,16,16,128]{3,2,1,0:T(8,128)(2,1)S(1)} %bitcast.227), channel_id=1, source_target_pairs={{0,0},{1,16},{2,32},{3,48},{4,64},{5,80},{6,96},{7,112},{8,128},{9... | collective-permute-start | bytes 786440 | tf_op jit(solution)/shard_map/ppermute | solution.py:132
  50.3 0.9 copy-start.4
  88.3 0.7 copy-start.7
  90.1 0.9 copy-start.3

commit v7 on v6

--- a/solution.py
+++ b/solution.py
@@ -68,6 +68,78 @@
     spread = jnp.broadcast_to(near[None], (outer,) + near.shape)
     far = lax.all_to_all(spread, axis, 0, 0, axis_index_groups=outer_groups)
     return far.reshape((outer * inner,) + block.shape)
+
+
+def chip_position(row, col):
+    return ((col // 2) % 4, row % 4, 8 * (col // 8) + row // 4)
+
+
+def hop_count(source, target):
+    sizes = (4, 4, 16)
+    total = 0
+    for a, b, n in zip(source, target, sizes):
+        d = abs(a - b) % n
+        total += min(d, n - d)
+    return total
+
+
+def assignment(cost):
+    n = len(cost)
+    u = [0] * (n + 1)
+    v = [0] * (n + 1)
+    match = [0] * (n + 1)
+    way = [0] * (n + 1)
+    for i in range(1, n + 1):
+        match[0] = i
+        j0 = 0
+        minv = [float("inf")] * (n + 1)
+        used = [False] * (n + 1)
+        while True:
+            used[j0] = True
+            i0 = match[j0]
+            delta = float("inf")
+            j1 = 0
+            for j in range(1, n + 1):
+                if not used[j]:
+                    cur = cost[i0 - 1][j - 1] - u[i0] - v[j]
+                    if cur < minv[j]:
+                        minv[j] = cur
+                        way[j] = j0
+                    if minv[j] < delta:
+                        delta = minv[j]
+                        j1 = j
+            for j in range(n + 1):
+                if used[j]:
+                    u[match[j]] += delta
+                    v[j] -= delta
+                else:
+                    minv[j] -= delta
+            j0 = j1
+            if match[j0] == 0:
+                break
+        while True:
+            j1 = way[j0]
+            match[j0] = match[j1]
+            j0 = j1
+            if j0 == 0:
+                break
+    chosen = [0] * n
+    for j in range(1, n + 1):
+        chosen[match[j] - 1] = j - 1
+    return chosen
+
+
+def owner_perm(n_row, n_col, groups):
+    perm = []
+    for col in range(n_col):
+        sources = [(r, cc) for r in range(groups * col, groups * col + groups) for cc in range(n_col)]
+        cost = [
+            [hop_count(chip_position(*src), chip_position(p, col)) ** 2 for p in range(n_row)]
+            for src in sources
+        ]
+        for src, p in zip(sources, assignment(cost)):
+            perm.append((src[0] * n_col + src[1], p * n_col + col))
+    return perm
 
 
 def shards(
@@ -124,11 +196,7 @@
     rows_act = lax.dynamic_slice_in_dim(tiles, (row_index % groups) * row_count, row_count, axis=1)
     rows_act = rows_act.transpose(1, 0, 2, 3).reshape(row_count, window, channels)
 
-    perm = [
-        (src_row * n_col + src_col, ((src_row % groups) * n_col + src_col) * n_col + src_row // groups)
-        for src_row in range(n_row)
-        for src_col in range(n_col)
-    ]
+    perm = owner_perm(n_row, n_col, groups)
     moved = lax.ppermute(tiles, ("row", "col"), perm)
     cols_act = moved.transpose(1, 0, 2, 3).reshape(groups * row_count, window, channels)
 

time: 97.5 us -> 88.4 us (0.907)
  the two profiles are of different devices: /device:TPU:97 before, /device:TPU:129 now
where the time goes in v7:
time: 88.4 us; the launch traced here: 87.9 us
  starting transfers between devices  37.2 us (42%)
  waiting for transfers between devices  30.2 us (34%)
  local copies, waits for them, and re-layouts  9.73 us (11%)
  other arithmetic  5.23 us (6%)
  matrix products  3.65 us (4%)
  between operations  1.86 us (2%)
    ppermute x1, waiting for transfers between devices, shards(): moved = lax.ppermute(tiles, ('row', 'col'), perm)  23.9 us
    ppermute x1, starting transfers between devices, shards(): received = lax.ppermute(tile, 'col', [(i, i ^ 8) for i in range(n_col)])  10.6 us
    ppermute x1, starting transfers between devices, shards(): received = lax.ppermute(pair, 'col', [(i, i ^ 1) for i in range(n_col)])  8.03 us
    ppermute x1, starting transfers between devices, shards(): moved = lax.ppermute(tiles, ('row', 'col'), perm)  7.44 us
    unnamed x21, local copies, waits for them, and re-layouts  5.18 us
    ppermute x1, starting transfers between devices, shards(): received = lax.ppermute(held, 'col', [(i, i ^ 4) for i in range(n_col)])  4.65 us
    ppermute x1, starting transfers between devices, shards(): partner = lax.ppermute(pair_act, 'row', [(i, i ^ 1) for i in range(n_row)])  3.34 us
    ppermute x1, starting transfers between devices, shards(): received = lax.ppermute(held, 'col', [(i, i ^ 2) for i in range(n_col)])  3.12 us
  transfers between devices with their start and end apart: 6, of which 4 were waited for; matrix products, arithmetic and copies ran while one was open for 6% of the time, Pallas kernels for 0%

profile of v7, /device:TPU:129, one launch (start us, length us, event | category | flops | bytes accessed | tf_op | source)
XLA Modules:
  0.0 87.9 jit_solution(8334654966409812610)
XLA Ops:
  0.6 3.3 %collective-permute-start = (bf16[8,16,128]{2,1,0:T(8,128)(2,1)}, bf16[8,16,128]{2,1,0:T(8,128)(2,1)S(1)}, u32[]{:S(2)}, u32[]{:S(2)}) collective-permute-start(bf16[8,16,128]{2,1,0:T(8,128)(2,1)} %param.10), channel_id=1, source_target_pairs={{0,16},{16,0},{32,48},{48,32},{64,80},{80,64},{96,112},{112,96},{1... | collective-permute-start | bytes 98312 | tf_op jit(solution)/shard_map/ppermute | solution.py:176
  4.7 0.9 %convert_reduce_fusion = f32[8,16]{1,0:T(8,128)S(1)} fusion(bf16[8,16,128]{2,1,0:T(8,128)(2,1)} %param.10), kind=kLoop, calls=%fused_computation.83 | loop fusion | flops 32640 | bytes 33280 | tf_op jit(solution)/shard_map/reduce_sum | solution.py:19
  5.7 0.1 add.348
  5.8 0.2 fusion.55
  6.0 0.4 copy-done.8
  6.3 0.2 fusion.13
  6.6 0.1 add.345
  6.7 0.7 copy-done.1
  7.3 0.8 gather_fusion
  8.2 10.6 %collective-permute-start.1 = (bf16[16,16,128]{2,1,0:T(8,128)(2,1)S(1)}, bf16[16,16,128]{2,1,0:T(8,128)(2,1)S(1)}, u32[]{:S(2)}, u32[]{:S(2)}) collective-permute-start(bf16[16,16,128]{2,1,0:T(8,128)(2,1)S(1)} %maximum_select_fusion.3), channel_id=1, source_target_pairs={{0,8},{1,9},{2,10},{3,11},{4,12},{5,13},{6,14},{7,15},{8,0},{9,1},... | collective-permute-start | bytes 196616 | tf_op jit(solution)/shard_map/ppermute | solution.py:183
  18.8 0.1 dynamic_slice.9
  18.9 3.0 %collective-permute-done.1 = bf16[16,16,128]{2,1,0:T(8,128)(2,1)S(1)} collective-permute-done((bf16[16,16,128]{2,1,0:T(8,128)(2,1)S(1)}, bf16[16,16,128]{2,1,0:T(8,128)(2,1)S(1)}, u32[]{:S(2)}, u32[]{:S(2)}) %collective-permute-start.1) | collective-permute-done | bytes 65568 | tf_op jit(solution)/shard_map/ppermute | solution.py:183
  21.9 4.7 %collective-permute-start.2 = (bf16[16,16,128]{2,1,0:T(8,128)(2,1)S(1)}, bf16[16,16,128]{2,1,0:T(8,128)(2,1)S(1)}, u32[]{:S(2)}, u32[]{:S(2)}) collective-permute-start(bf16[16,16,128]{2,1,0:T(8,128)(2,1)S(1)} %broadcast_select_fusion), channel_id=1, source_target_pairs={{0,4},{1,5},{2,6},{3,7},{4,0},{5,1},{6,2},{7,3},{8,12},{9,13},{10,... | collective-permute-start | bytes 196616 | tf_op jit(solution)/shard_map/ppermute | solution.py:186
  26.6 0.1 broadcast_multiply_fusion.2
  26.6 0.1 dynamic_slice.11
  26.7 1.7 %collective-permute-done.2 = bf16[16,16,128]{2,1,0:T(8,128)(2,1)S(1)} collective-permute-done((bf16[16,16,128]{2,1,0:T(8,128)(2,1)S(1)}, bf16[16,16,128]{2,1,0:T(8,128)(2,1)S(1)}, u32[]{:S(2)}, u32[]{:S(2)}) %collective-permute-start.2) | collective-permute-done | bytes 65568 | tf_op jit(solution)/shard_map/ppermute | solution.py:186
  28.4 3.1 %collective-permute-start.3 = (bf16[16,16,128]{2,1,0:T(8,128)(2,1)S(1)}, bf16[16,16,128]{2,1,0:T(8,128)(2,1)S(1)}, u32[]{:S(2)}, u32[]{:S(2)}) collective-permute-start(bf16[16,16,128]{2,1,0:T(8,128)(2,1)S(1)} %broadcast_select_fusion.1), channel_id=1, source_target_pairs={{0,2},{1,3},{2,0},{3,1},{4,6},{5,7},{6,4},{7,5},{8,10},{9,11},{10,... | collective-permute-start | bytes 196616 | tf_op jit(solution)/shard_map/ppermute | solution.py:188
  31.6 0.8 gather_fusion.1
  32.4 1.6 %collective-permute-done.3 = bf16[16,16,128]{2,1,0:T(8,128)(2,1)S(1)} collective-permute-done((bf16[16,16,128]{2,1,0:T(8,128)(2,1)S(1)}, bf16[16,16,128]{2,1,0:T(8,128)(2,1)S(1)}, u32[]{:S(2)}, u32[]{:S(2)}) %collective-permute-start.3) | collective-permute-done | bytes 65568 | tf_op jit(solution)/shard_map/ppermute | solution.py:188
  34.1 8.0 %collective-permute-start.4 = (bf16[2,16,16,128]{3,2,1,0:T(8,128)(2,1)S(1)}, bf16[2,16,16,128]{3,2,1,0:T(8,128)(2,1)S(1)}, u32[]{:S(2)}, u32[]{:S(2)}) collective-permute-start(bf16[2,16,16,128]{3,2,1,0:T(8,128)(2,1)S(1)} %maximum_select_fusion.2), channel_id=1, source_target_pairs={{0,1},{1,0},{2,3},{3,2},{4,5},{5,4},{6,7},{7,6},{8,9},{9,8},{10,11... | collective-permute-start | bytes 393224 | tf_op jit(solution)/shard_map/ppermute | solution.py:191
  42.2 0.1 reshape.405
  42.3 0.7 copy-done.5
  43.0 0.2 reshape.407
  43.2 0.7 copy-done.6
  43.8 0.2 copy.100
  44.1 0.1 fusion.47
  44.4 0.3 multiply_reduce_fusion.1
  44.6 7.4 %collective-permute-start.5 = (bf16[4,16,16,128]{3,2,1,0:T(8,128)(2,1)S(1)}, bf16[4,16,16,128]{3,2,1,0:T(8,128)(2,1)S(1)}, u32[]{:S(2)}, u32[]{:S(2)}) collective-permute-start(bf16[4,16,16,128]{3,2,1,0:T(8,128)(2,1)S(1)} %bitcast.227), channel_id=1, source_target_pairs={{0,192},{1,240},{2,176},{3,64},{4,0},{5,48},{6,112},{7,128},{8,304... | collective-permute-start | bytes 786440 | tf_op jit(solution)/shard_map/ppermute | solution.py:200
  52.1 0.1 rsqrt.33
  52.2 0.1 div.44
  52.3 0.2 fusion.34
  52.5 0.2 convolution_convert_fusion
  52.7 0.7 copy-done.4
  53.4 0.2 fusion.58
  53.7 0.2 copy.101
  53.9 0.2 copy.109
  54.1 0.1 fusion.29
  54.2 0.2 copy.99
  54.4 23.9 %collective-permute-done.5 = bf16[4,16,16,128]{3,2,1,0:T(8,128)(2,1)S(1)} collective-permute-done((bf16[4,16,16,128]{3,2,1,0:T(8,128)(2,1)S(1)}, bf16[4,16,16,128]{3,2,1,0:T(8,128)(2,1)S(1)}, u32[]{:S(2)}, u32[]{:S(2)}) %collective-permute-start.5) | collective-permute-done | bytes 262176 | tf_op jit(solution)/shard_map/ppermute | solution.py:200
  78.3 0.2 fusion.23
  78.5 0.4 multiply_reduce_fusion
  79.0 0.1 rsqrt.31
  79.1 0.1 div.40
  79.2 0.3 fusion.22
  79.6 0.3 copy-done.7
  79.9 0.3 fusion.15
  80.2 0.2 fusion.9
  80.4 0.6 slice_reduce_fusion.3
  81.1 0.9 %fusion.36 = (f32[8,4,16]{2,1,0:T(4,128)S(1)}, f32[8,4,16]{2,1,0:T(4,128)S(1)}, f32[8,4,16]{2,1,0:T(4,128)S(1)}, f32[8,4,16]{2,1,0:T(4,128)S(1)}) fusion(f32[8,4,16,64]{3,2,1,0:T(8,128)S(1)} %fusion.9, f32[8,4,16]{2,1,0:T(4,128)S(1)} %get-tuple-element.19, f32[8,4,16]{2,1,0:T(4,128)S(1)} %get-tuple-element.22, f32[8,4,16]{2,1,0:T(4,128)S(1)} %get-tuple-element.21, ...), kind=kLoop, calls=%fused_computation.67 | loop fusion | flops 63488 | bytes 147456 | tf_op jit(solution)/shard_map/reduce_sum | solution.py:40
  82.0 0.1 fusion.68
  82.1 0.1 fusion.75
  82.2 0.3 fusion.60
  82.5 0.1 fusion.69
  82.6 0.5 fusion.10
  83.2 0.4 fusion.11
  83.6 0.5 fusion.12
  84.1 0.4 fusion.2
  84.5 0.1 copy.114
  84.6 0.8 reshape.409
  85.4 0.6 copy.116
  86.0 0.2 fusion.17
  86.2 0.4 copy.98
  86.6 0.4 fusion
  87.0 0.8 copy.115
  (44 shorter events, 0.6 us)
Async XLA Ops:
  0.6 51.9 %copy-start = (bf16[128,256]{1,0:T(8,128)(2,1)S(1)}, bf16[128,256]{1,0:T(8,128)(2,1)}, u32[]{:S(2)}) copy-start(bf16[128,256]{1,0:T(8,128)(2,1)} %param.15) | copy-start | bytes 196612
  0.6 7.5 %collective-permute-start = (bf16[8,16,128]{2,1,0:T(8,128)(2,1)}, bf16[8,16,128]{2,1,0:T(8,128)(2,1)S(1)}, u32[]{:S(2)}, u32[]{:S(2)}) collective-permute-start(bf16[8,16,128]{2,1,0:T(8,128)(2,1)} %param.10), channel_id=1, source_target_pairs={{0,16},{16,0},{32,48},{48,32},{64,80},{80,64},{96,112},{112,96},{1... | collective-permute-start | bytes 98312 | tf_op jit(solution)/shard_map/ppermute | solution.py:176
  4.6 1.1 %copy-start.2 = (bf16[8,16,128]{2,1,0:T(8,128)(2,1)S(1)}, bf16[8,16,128]{2,1,0:T(8,128)(2,1)}, u32[]{:S(2)}) copy-start(bf16[8,16,128]{2,1,0:T(8,128)(2,1)} %param.10) | copy-start | bytes 98308
  5.6 0.8 copy-start.8
  6.7 0.7 copy-start.1
  8.2 13.7 %collective-permute-start.1 = (bf16[16,16,128]{2,1,0:T(8,128)(2,1)S(1)}, bf16[16,16,128]{2,1,0:T(8,128)(2,1)S(1)}, u32[]{:S(2)}, u32[]{:S(2)}) collective-permute-start(bf16[16,16,128]{2,1,0:T(8,128)(2,1)S(1)} %maximum_select_fusion.3), channel_id=1, source_target_pairs={{0,8},{1,9},{2,10},{3,11},{4,12},{5,13},{6,14},{7,15},{8,0},{9,1},... | collective-permute-start | bytes 196616 | tf_op jit(solution)/shard_map/ppermute | solution.py:183
  21.9 6.5 %collective-permute-start.2 = (bf16[16,16,128]{2,1,0:T(8,128)(2,1)S(1)}, bf16[16,16,128]{2,1,0:T(8,128)(2,1)S(1)}, u32[]{:S(2)}, u32[]{:S(2)}) collective-permute-start(bf16[16,16,128]{2,1,0:T(8,128)(2,1)S(1)} %broadcast_select_fusion), channel_id=1, source_target_pairs={{0,4},{1,5},{2,6},{3,7},{4,0},{5,1},{6,2},{7,3},{8,12},{9,13},{10,... | collective-permute-start | bytes 196616 | tf_op jit(solution)/shard_map/ppermute | solution.py:186
  28.4 5.6 %collective-permute-start.3 = (bf16[16,16,128]{2,1,0:T(8,128)(2,1)S(1)}, bf16[16,16,128]{2,1,0:T(8,128)(2,1)S(1)}, u32[]{:S(2)}, u32[]{:S(2)}) collective-permute-start(bf16[16,16,128]{2,1,0:T(8,128)(2,1)S(1)} %broadcast_select_fusion.1), channel_id=1, source_target_pairs={{0,2},{1,3},{2,0},{3,1},{4,6},{5,7},{6,4},{7,5},{8,10},{9,11},{10,... | collective-permute-start | bytes 196616 | tf_op jit(solution)/shard_map/ppermute | solution.py:188
  34.1 10.0 %collective-permute-start.4 = (bf16[2,16,16,128]{3,2,1,0:T(8,128)(2,1)S(1)}, bf16[2,16,16,128]{3,2,1,0:T(8,128)(2,1)S(1)}, u32[]{:S(2)}, u32[]{:S(2)}) collective-permute-start(bf16[2,16,16,128]{3,2,1,0:T(8,128)(2,1)S(1)} %maximum_select_fusion.2), channel_id=1, source_target_pairs={{0,1},{1,0},{2,3},{3,2},{4,5},{5,4},{6,7},{7,6},{8,9},{9,8},{10,11... | collective-permute-start | bytes 393224 | tf_op jit(solution)/shard_map/ppermute | solution.py:191
  42.1 0.8 copy-start.5
  43.0 0.8 copy-start.6
  44.6 33.6 %collective-permute-start.5 = (bf16[4,16,16,128]{3,2,1,0:T(8,128)(2,1)S(1)}, bf16[4,16,16,128]{3,2,1,0:T(8,128)(2,1)S(1)}, u32[]{:S(2)}, u32[]{:S(2)}) collective-permute-start(bf16[4,16,16,128]{3,2,1,0:T(8,128)(2,1)S(1)} %bitcast.227), channel_id=1, source_target_pairs={{0,192},{1,240},{2,176},{3,64},{4,0},{5,48},{6,112},{7,128},{8,304... | collective-permute-start | bytes 786440 | tf_op jit(solution)/shard_map/ppermute | solution.py:200
  52.5 0.9 %copy-start.4 = (bf16[128,512]{1,0:T(8,128)(2,1)S(1)}, bf16[128,512]{1,0:T(8,128)(2,1)}, u32[]{:S(2)}) copy-start(bf16[128,512]{1,0:T(8,128)(2,1)} %param.13) | copy-start | bytes 393220
  79.2 0.7 copy-start.7
  81.1 0.9 %copy-start.3 = (f32[4,8,16]{2,1,0:T(8,128)S(1)}, f32[4,8,16]{2,1,0:T(8,128)}, u32[]{:S(2)}) copy-start(f32[4,8,16]{2,1,0:T(8,128)} %param.18) | copy-start | bytes 6148

commit v8 on v7

--- a/solution.py
+++ b/solution.py
@@ -173,16 +173,17 @@
     row_mask = lax.dynamic_slice_in_dim(mask_float, row_index * row_count, row_count)
     col_mask = lax.dynamic_slice_in_dim(mask_float, col_index * col_width, col_width)
 
-    partner = lax.ppermute(pair_act, "row", [(i, i ^ 1) for i in range(n_row)])
-    odd = row_index % 2 == 1
-    tile = jnp.where(odd, jnp.concatenate([partner, pair_act]), jnp.concatenate([pair_act, partner]))
-
     def in_window(col):
         return (col - start) % n_col < STEPS
 
-    received = lax.ppermute(tile, "col", [(i, i ^ 8) for i in range(n_col)])
-    held = jnp.where(in_window(col_index), tile, received)
+    received = lax.ppermute(pair_act, "col", [(i, i ^ 8) for i in range(n_col)])
+    held = jnp.where(in_window(col_index), pair_act, received)
     mine_ok = in_window(col_index) | in_window(col_index ^ 8)
+
+    partner = lax.ppermute(held, "row", [(i, i ^ 1) for i in range(n_row)])
+    odd = row_index % 2 == 1
+    held = jnp.where(odd, jnp.concatenate([partner, held]), jnp.concatenate([held, partner]))
+
     received = lax.ppermute(held, "col", [(i, i ^ 4) for i in range(n_col)])
     held = jnp.where(mine_ok, held, received)
     received = lax.ppermute(held, "col", [(i, i ^ 2) for i in range(n_col)])
@@ -191,7 +192,7 @@
     received = lax.ppermute(pair, "col", [(i, i ^ 1) for i in range(n_col)])
     even = (col_index - start) % 2 == 0
     tiles = jnp.where(even, jnp.stack([pair, received], axis=1), jnp.stack([received, pair], axis=1))
-    tiles = tiles.reshape((STEPS,) + tile.shape)
+    tiles = tiles.reshape((STEPS,) + held.shape)
 
     rows_act = lax.dynamic_slice_in_dim(tiles, (row_index % groups) * row_count, row_count, axis=1)
     rows_act = rows_act.transpose(1, 0, 2, 3).reshape(row_count, window, channels)

time: 88.4 us -> 85.3 us (0.965)
  waiting for transfers between devices: 30.2 us -> 25.9 us
  starting transfers between devices: 37.2 us -> 38.4 us
    ppermute x1, starting transfers between devices: 7.44 us -> 10.4 us  [shards(): moved = lax.ppermute(tiles, ('row', 'col'), perm)]
    ppermute x1, waiting for transfers between devices: 23.9 us -> 21.9 us  [shards(): moved = lax.ppermute(tiles, ('row', 'col'), perm)]
    ppermute x1, starting transfers between devices: 8.03 us -> 6.31 us  [shards(): received = lax.ppermute(pair, 'col', [(i, i ^ 1) for i in range(n_col)])]
    ppermute x2, waiting for transfers between devices: 2.98 us -> 1.34 us  [the longest x1 1.34 us: shards(): partner = lax.ppermute(held, 'row', [(i, i ^ 1) for i in range(n_row)])]
  transfers between devices with their start and end apart: 6 -> 6, of which waited for: 4 -> 4; matrix products, arithmetic and copies ran while one was open for 6% -> 7% of each run, Pallas kernels for 0% -> 0%
where the time goes in v8:
time: 85.3 us; the launch traced here: 84.7 us
  starting transfers between devices  38.4 us (45%)
  waiting for transfers between devices  25.9 us (30%)
  local copies, waits for them, and re-layouts  9.64 us (11%)
  other arithmetic  5.22 us (6%)
  matrix products  3.67 us (4%)
  between operations  1.88 us (2%)
    ppermute x1, waiting for transfers between devices, shards(): moved = lax.ppermute(tiles, ('row', 'col'), perm)  21.9 us
    ppermute x1, starting transfers between devices, shards(): received = lax.ppermute(pair_act, 'col', [(i, i ^ 8) for i in range(n_col)])  10.8 us
    ppermute x1, starting transfers between devices, shards(): moved = lax.ppermute(tiles, ('row', 'col'), perm)  10.4 us
    ppermute x1, starting transfers between devices, shards(): received = lax.ppermute(pair, 'col', [(i, i ^ 1) for i in range(n_col)])  6.31 us
    unnamed x21, local copies, waits for them, and re-layouts  5.08 us
    ppermute x1, starting transfers between devices, shards(): received = lax.ppermute(held, 'col', [(i, i ^ 4) for i in range(n_col)])  4.65 us
    ppermute x1, starting transfers between devices, shards(): partner = lax.ppermute(held, 'row', [(i, i ^ 1) for i in range(n_row)])  3.2 us
    ppermute x1, starting transfers between devices, shards(): received = lax.ppermute(held, 'col', [(i, i ^ 2) for i in range(n_col)])  3.12 us
  transfers between devices with their start and end apart: 6, of which 4 were waited for; matrix products, arithmetic and copies ran while one was open for 7% of the time, Pallas kernels for 0%

profile of v8, /device:TPU:129, one launch (start us, length us, event | category | flops | bytes accessed | tf_op | source)
XLA Modules:
  0.0 84.7 jit_solution(7523425606880419133)
XLA Ops:
  0.6 10.8 %collective-permute-start = (bf16[8,16,128]{2,1,0:T(8,128)(2,1)}, bf16[8,16,128]{2,1,0:T(8,128)(2,1)S(1)}, u32[]{:S(2)}, u32[]{:S(2)}) collective-permute-start(bf16[8,16,128]{2,1,0:T(8,128)(2,1)} %param.10), channel_id=1, source_target_pairs={{0,8},{1,9},{2,10},{3,11},{4,12},{5,13},{6,14},{7,15},{8,0},{9,1},... | collective-permute-start | bytes 98312 | tf_op jit(solution)/shard_map/ppermute | solution.py:179
  12.1 0.9 %convert_reduce_fusion = f32[8,16]{1,0:T(8,128)S(1)} fusion(bf16[8,16,128]{2,1,0:T(8,128)(2,1)} %param.10), kind=kLoop, calls=%fused_computation.83 | loop fusion | flops 32640 | bytes 33280 | tf_op jit(solution)/shard_map/reduce_sum | solution.py:19
  13.1 0.1 add.348
  13.2 0.2 fusion.55
  13.4 0.4 copy-done.8
  13.8 0.2 fusion.13
  14.0 0.1 add.345
  14.1 0.6 copy-done.1
  14.7 0.8 gather_fusion
  15.5 3.2 %collective-permute-start.1 = (bf16[8,16,128]{2,1,0:T(8,128)(2,1)S(1)}, bf16[8,16,128]{2,1,0:T(8,128)(2,1)S(1)}, u32[]{:S(2)}, u32[]{:S(2)}) collective-permute-start(bf16[8,16,128]{2,1,0:T(8,128)(2,1)S(1)} %broadcast_select_fusion.1), channel_id=1, source_target_pairs={{0,16},{16,0},{32,48},{48,32},{64,80},{80,64},{96,112},{112,96},{1... | collective-permute-start | bytes 98312 | tf_op jit(solution)/shard_map/ppermute | solution.py:183
  18.8 0.1 dynamic_slice.9
  18.8 1.3 %collective-permute-done.1 = bf16[8,16,128]{2,1,0:T(8,128)(2,1)S(1)} collective-permute-done((bf16[8,16,128]{2,1,0:T(8,128)(2,1)S(1)}, bf16[8,16,128]{2,1,0:T(8,128)(2,1)S(1)}, u32[]{:S(2)}, u32[]{:S(2)}) %collective-permute-start.1) | collective-permute-done | bytes 32800 | tf_op jit(solution)/shard_map/ppermute | solution.py:183
  20.2 4.7 %collective-permute-start.2 = (bf16[16,16,128]{2,1,0:T(8,128)(2,1)S(1)}, bf16[16,16,128]{2,1,0:T(8,128)(2,1)S(1)}, u32[]{:S(2)}, u32[]{:S(2)}) collective-permute-start(bf16[16,16,128]{2,1,0:T(8,128)(2,1)S(1)} %maximum_select_fusion.3), channel_id=1, source_target_pairs={{0,4},{1,5},{2,6},{3,7},{4,0},{5,1},{6,2},{7,3},{8,12},{9,13},{10,... | collective-permute-start | bytes 196616 | tf_op jit(solution)/shard_map/ppermute | solution.py:187
  24.8 0.1 broadcast_multiply_fusion.2
  24.9 0.1 dynamic_slice.11
  25.0 1.7 %collective-permute-done.2 = bf16[16,16,128]{2,1,0:T(8,128)(2,1)S(1)} collective-permute-done((bf16[16,16,128]{2,1,0:T(8,128)(2,1)S(1)}, bf16[16,16,128]{2,1,0:T(8,128)(2,1)S(1)}, u32[]{:S(2)}, u32[]{:S(2)}) %collective-permute-start.2) | collective-permute-done | bytes 65568 | tf_op jit(solution)/shard_map/ppermute | solution.py:187
  26.7 3.1 %collective-permute-start.3 = (bf16[16,16,128]{2,1,0:T(8,128)(2,1)S(1)}, bf16[16,16,128]{2,1,0:T(8,128)(2,1)S(1)}, u32[]{:S(2)}, u32[]{:S(2)}) collective-permute-start(bf16[16,16,128]{2,1,0:T(8,128)(2,1)S(1)} %broadcast_select_fusion), channel_id=1, source_target_pairs={{0,2},{1,3},{2,0},{3,1},{4,6},{5,7},{6,4},{7,5},{8,10},{9,11},{10,... | collective-permute-start | bytes 196616 | tf_op jit(solution)/shard_map/ppermute | solution.py:189
  29.9 0.8 gather_fusion.1
  30.7 1.0 %collective-permute-done.3 = bf16[16,16,128]{2,1,0:T(8,128)(2,1)S(1)} collective-permute-done((bf16[16,16,128]{2,1,0:T(8,128)(2,1)S(1)}, bf16[16,16,128]{2,1,0:T(8,128)(2,1)S(1)}, u32[]{:S(2)}, u32[]{:S(2)}) %collective-permute-start.3) | collective-permute-done | bytes 65568 | tf_op jit(solution)/shard_map/ppermute | solution.py:189
  31.7 6.3 %collective-permute-start.4 = (bf16[2,16,16,128]{3,2,1,0:T(8,128)(2,1)S(1)}, bf16[2,16,16,128]{3,2,1,0:T(8,128)(2,1)S(1)}, u32[]{:S(2)}, u32[]{:S(2)}) collective-permute-start(bf16[2,16,16,128]{3,2,1,0:T(8,128)(2,1)S(1)} %maximum_select_fusion.2), channel_id=1, source_target_pairs={{0,1},{1,0},{2,3},{3,2},{4,5},{5,4},{6,7},{7,6},{8,9},{9,8},{10,11... | collective-permute-start | bytes 393224 | tf_op jit(solution)/shard_map/ppermute | solution.py:192
  38.1 0.1 reshape.405
  38.2 0.7 copy-done.5
  38.9 0.2 reshape.407
  39.1 0.7 copy-done.6
  39.8 0.2 copy.100
  40.1 0.1 fusion.47
  40.3 0.3 multiply_reduce_fusion.1
  40.6 10.4 %collective-permute-start.5 = (bf16[4,16,16,128]{3,2,1,0:T(8,128)(2,1)S(1)}, bf16[4,16,16,128]{3,2,1,0:T(8,128)(2,1)S(1)}, u32[]{:S(2)}, u32[]{:S(2)}) collective-permute-start(bf16[4,16,16,128]{3,2,1,0:T(8,128)(2,1)S(1)} %bitcast.227), channel_id=1, source_target_pairs={{0,192},{1,240},{2,176},{3,64},{4,0},{5,48},{6,112},{7,128},{8,304... | collective-permute-start | bytes 786440 | tf_op jit(solution)/shard_map/ppermute | solution.py:201
  51.0 0.1 rsqrt.33
  51.1 0.1 div.44
  51.2 0.2 fusion.34
  51.4 0.2 convolution_convert_fusion
  51.6 0.7 copy-done.4
  52.3 0.2 fusion.58
  52.6 0.2 copy.101
  52.8 0.2 copy.109
  52.9 0.1 fusion.29
  53.1 0.2 copy.99
  53.3 21.9 %collective-permute-done.5 = bf16[4,16,16,128]{3,2,1,0:T(8,128)(2,1)S(1)} collective-permute-done((bf16[4,16,16,128]{3,2,1,0:T(8,128)(2,1)S(1)}, bf16[4,16,16,128]{3,2,1,0:T(8,128)(2,1)S(1)}, u32[]{:S(2)}, u32[]{:S(2)}) %collective-permute-start.5) | collective-permute-done | bytes 262176 | tf_op jit(solution)/shard_map/ppermute | solution.py:201
  75.2 0.2 fusion.23
  75.4 0.4 multiply_reduce_fusion
  75.8 0.1 rsqrt.31
  76.0 0.1 div.40
  76.1 0.3 fusion.22
  76.4 0.3 copy-done.7
  76.8 0.3 fusion.15
  77.1 0.2 fusion.9
  77.3 0.6 slice_reduce_fusion.3
  77.9 0.9 %fusion.36 = (f32[8,4,16]{2,1,0:T(4,128)S(1)}, f32[8,4,16]{2,1,0:T(4,128)S(1)}, f32[8,4,16]{2,1,0:T(4,128)S(1)}, f32[8,4,16]{2,1,0:T(4,128)S(1)}) fusion(f32[8,4,16,64]{3,2,1,0:T(8,128)S(1)} %fusion.9, f32[8,4,16]{2,1,0:T(4,128)S(1)} %get-tuple-element.19, f32[8,4,16]{2,1,0:T(4,128)S(1)} %get-tuple-element.22, f32[8,4,16]{2,1,0:T(4,128)S(1)} %get-tuple-element.21, ...), kind=kLoop, calls=%fused_computation.67 | loop fusion | flops 63488 | bytes 147456 | tf_op jit(solution)/shard_map/reduce_sum | solution.py:40
  78.8 0.1 fusion.68
  79.0 0.1 fusion.75
  79.1 0.3 fusion.60
  79.4 0.1 fusion.69
  79.5 0.5 fusion.10
  80.0 0.4 fusion.11
  80.5 0.5 fusion.12
  80.9 0.4 fusion.2
  81.3 0.1 copy.114
  81.5 0.8 reshape.409
  82.3 0.6 copy.116
  82.9 0.2 fusion.17
  83.1 0.4 copy.98
  83.5 0.4 fusion
  83.9 0.8 copy.115
  (44 shorter events, 0.6 us)
Async XLA Ops:
  0.6 50.7 %copy-start = (bf16[128,256]{1,0:T(8,128)(2,1)S(1)}, bf16[128,256]{1,0:T(8,128)(2,1)}, u32[]{:S(2)}) copy-start(bf16[128,256]{1,0:T(8,128)(2,1)} %param.15) | copy-start | bytes 196612
  0.6 14.9 %collective-permute-start = (bf16[8,16,128]{2,1,0:T(8,128)(2,1)}, bf16[8,16,128]{2,1,0:T(8,128)(2,1)S(1)}, u32[]{:S(2)}, u32[]{:S(2)}) collective-permute-start(bf16[8,16,128]{2,1,0:T(8,128)(2,1)} %param.10), channel_id=1, source_target_pairs={{0,8},{1,9},{2,10},{3,11},{4,12},{5,13},{6,14},{7,15},{8,0},{9,1},... | collective-permute-start | bytes 98312 | tf_op jit(solution)/shard_map/ppermute | solution.py:179
  12.1 1.1 %copy-start.2 = (bf16[8,16,128]{2,1,0:T(8,128)(2,1)S(1)}, bf16[8,16,128]{2,1,0:T(8,128)(2,1)}, u32[]{:S(2)}) copy-start(bf16[8,16,128]{2,1,0:T(8,128)(2,1)} %param.10) | copy-start | bytes 98308
  13.0 0.8 copy-start.8
  14.0 0.7 copy-start.1
  15.5 4.7 %collective-permute-start.1 = (bf16[8,16,128]{2,1,0:T(8,128)(2,1)S(1)}, bf16[8,16,128]{2,1,0:T(8,128)(2,1)S(1)}, u32[]{:S(2)}, u32[]{:S(2)}) collective-permute-start(bf16[8,16,128]{2,1,0:T(8,128)(2,1)S(1)} %broadcast_select_fusion.1), channel_id=1, source_target_pairs={{0,16},{16,0},{32,48},{48,32},{64,80},{80,64},{96,112},{112,96},{1... | collective-permute-start | bytes 98312 | tf_op jit(solution)/shard_map/ppermute | solution.py:183
  20.2 6.5 %collective-permute-start.2 = (bf16[16,16,128]{2,1,0:T(8,128)(2,1)S(1)}, bf16[16,16,128]{2,1,0:T(8,128)(2,1)S(1)}, u32[]{:S(2)}, u32[]{:S(2)}) collective-permute-start(bf16[16,16,128]{2,1,0:T(8,128)(2,1)S(1)} %maximum_select_fusion.3), channel_id=1, source_target_pairs={{0,4},{1,5},{2,6},{3,7},{4,0},{5,1},{6,2},{7,3},{8,12},{9,13},{10,... | collective-permute-start | bytes 196616 | tf_op jit(solution)/shard_map/ppermute | solution.py:187
  26.7 5.0 %collective-permute-start.3 = (bf16[16,16,128]{2,1,0:T(8,128)(2,1)S(1)}, bf16[16,16,128]{2,1,0:T(8,128)(2,1)S(1)}, u32[]{:S(2)}, u32[]{:S(2)}) collective-permute-start(bf16[16,16,128]{2,1,0:T(8,128)(2,1)S(1)} %broadcast_select_fusion), channel_id=1, source_target_pairs={{0,2},{1,3},{2,0},{3,1},{4,6},{5,7},{6,4},{7,5},{8,10},{9,11},{10,... | collective-permute-start | bytes 196616 | tf_op jit(solution)/shard_map/ppermute | solution.py:189
  31.7 8.3 %collective-permute-start.4 = (bf16[2,16,16,128]{3,2,1,0:T(8,128)(2,1)S(1)}, bf16[2,16,16,128]{3,2,1,0:T(8,128)(2,1)S(1)}, u32[]{:S(2)}, u32[]{:S(2)}) collective-permute-start(bf16[2,16,16,128]{3,2,1,0:T(8,128)(2,1)S(1)} %maximum_select_fusion.2), channel_id=1, source_target_pairs={{0,1},{1,0},{2,3},{3,2},{4,5},{5,4},{6,7},{7,6},{8,9},{9,8},{10,11... | collective-permute-start | bytes 393224 | tf_op jit(solution)/shard_map/ppermute | solution.py:192
  38.1 0.8 copy-start.5
  38.9 0.8 copy-start.6
  40.6 34.6 %collective-permute-start.5 = (bf16[4,16,16,128]{3,2,1,0:T(8,128)(2,1)S(1)}, bf16[4,16,16,128]{3,2,1,0:T(8,128)(2,1)S(1)}, u32[]{:S(2)}, u32[]{:S(2)}) collective-permute-start(bf16[4,16,16,128]{3,2,1,0:T(8,128)(2,1)S(1)} %bitcast.227), channel_id=1, source_target_pairs={{0,192},{1,240},{2,176},{3,64},{4,0},{5,48},{6,112},{7,128},{8,304... | collective-permute-start | bytes 786440 | tf_op jit(solution)/shard_map/ppermute | solution.py:201
  51.4 0.9 %copy-start.4 = (bf16[128,512]{1,0:T(8,128)(2,1)S(1)}, bf16[128,512]{1,0:T(8,128)(2,1)}, u32[]{:S(2)}) copy-start(bf16[128,512]{1,0:T(8,128)(2,1)} %param.13) | copy-start | bytes 393220
  76.1 0.7 copy-start.7
  77.9 0.9 %copy-start.3 = (f32[4,8,16]{2,1,0:T(8,128)S(1)}, f32[4,8,16]{2,1,0:T(8,128)}, u32[]{:S(2)}) copy-start(f32[4,8,16]{2,1,0:T(8,128)} %param.18) | copy-start | bytes 6148

commit v9 on v8

--- a/solution.py
+++ b/solution.py
@@ -1,3 +1,5 @@
+import collections
+import itertools
 import math
 
 import jax
@@ -129,17 +131,47 @@
     return chosen
 
 
-def owner_perm(n_row, n_col, groups):
-    perm = []
-    for col in range(n_col):
-        sources = [(r, cc) for r in range(groups * col, groups * col + groups) for cc in range(n_col)]
-        cost = [
-            [hop_count(chip_position(*src), chip_position(p, col)) ** 2 for p in range(n_row)]
-            for src in sources
-        ]
-        for src, p in zip(sources, assignment(cost)):
-            perm.append((src[0] * n_col + src[1], p * n_col + col))
-    return perm
+def route(source, target):
+    sizes = (4, 4, 16)
+    routes = []
+    for order in itertools.permutations(range(3)):
+        cur = list(source)
+        links = []
+        for dim in order:
+            n = sizes[dim]
+            delta = (target[dim] - cur[dim]) % n
+            step = 1 if delta <= n - delta else -1
+            while cur[dim] != target[dim]:
+                links.append((order, tuple(cur), dim, step))
+                cur[dim] = (cur[dim] + step) % n
+        routes.append(links)
+    return [link for links in routes for link in links]
+
+
+def owner_perm(n_row, n_col, groups, sweeps=3):
+    load = collections.Counter()
+    chosen = {}
+    paths = {}
+    for _ in range(sweeps):
+        for col in range(n_col):
+            sources = [(r, cc) for r in range(groups * col, groups * col + groups) for cc in range(n_col)]
+            for src, p in chosen.get(col, []):
+                for link in paths[(src, p, col)]:
+                    load[link] -= 1
+            cost = []
+            for src in sources:
+                row_cost = []
+                for p in range(n_row):
+                    key = (src, p, col)
+                    if key not in paths:
+                        paths[key] = route(chip_position(*src), chip_position(p, col))
+                    row_cost.append(sum(2 * load[link] + 1 for link in paths[key]))
+                cost.append(row_cost)
+            chosen[col] = list(zip(sources, assignment(cost)))
+            for src, p in chosen[col]:
+                for link in paths[(src, p, col)]:
+                    load[link] += 1
+    return [(src[0] * n_col + src[1], p * n_col + col) for col in range(n_col) for src, p in chosen[col]]
 
 
 def shards(

time: 85.3 us -> 83.4 us (0.978)
  waiting for transfers between devices: 25.9 us -> 22.5 us
  starting transfers between devices: 38.4 us -> 40 us
    ppermute x1, waiting for transfers between devices: 21.9 us -> 18.4 us  [shards(): moved = lax.ppermute(tiles, ('row', 'col'), perm)]
    ppermute x1, starting transfers between devices: 10.4 us -> 11.9 us  [shards(): moved = lax.ppermute(tiles, ('row', 'col'), perm)]
where the time goes in v9:
time: 83.4 us; the launch traced here: 82.8 us
  starting transfers between devices  40 us (48%)
  waiting for transfers between devices  22.5 us (27%)
  local copies, waits for them, and re-layouts  9.65 us (12%)
  other arithmetic  5.22 us (6%)
  matrix products  3.65 us (4%)
  between operations  1.87 us (2%)
    ppermute x1, waiting for transfers between devices, shards(): moved = lax.ppermute(tiles, ('row', 'col'), perm)  18.4 us
    ppermute x1, starting transfers between devices, shards(): moved = lax.ppermute(tiles, ('row', 'col'), perm)  11.9 us
    ppermute x1, starting transfers between devices, shards(): received = lax.ppermute(pair_act, 'col', [(i, i ^ 8) for i in range(n_col)])  10.8 us
    ppermute x1, starting transfers between devices, shards(): received = lax.ppermute(pair, 'col', [(i, i ^ 1) for i in range(n_col)])  6.31 us
    unnamed x21, local copies, waits for them, and re-layouts  5.09 us
    ppermute x1, starting transfers between devices, shards(): received = lax.ppermute(held, 'col', [(i, i ^ 4) for i in range(n_col)])  4.65 us
    ppermute x1, starting transfers between devices, shards(): partner = lax.ppermute(held, 'row', [(i, i ^ 1) for i in range(n_row)])  3.2 us
    ppermute x1, starting transfers between devices, shards(): received = lax.ppermute(held, 'col', [(i, i ^ 2) for i in range(n_col)])  3.12 us
  transfers between devices with their start and end apart: 6, of which 4 were waited for; matrix products, arithmetic and copies ran while one was open for 7% of the time, Pallas kernels for 0%

profile of v9, /device:TPU:129, one launch (start us, length us, event | category | flops | bytes accessed | tf_op | source)
XLA Modules:
  0.0 82.8 jit_solution(15669779087486844190)
XLA Ops:
  0.6 10.8 %collective-permute-start = (bf16[8,16,128]{2,1,0:T(8,128)(2,1)}, bf16[8,16,128]{2,1,0:T(8,128)(2,1)S(1)}, u32[]{:S(2)}, u32[]{:S(2)}) collective-permute-start(bf16[8,16,128]{2,1,0:T(8,128)(2,1)} %param.10), channel_id=1, source_target_pairs={{0,8},{1,9},{2,10},{3,11},{4,12},{5,13},{6,14},{7,15},{8,0},{9,1},... | collective-permute-start | bytes 98312 | tf_op jit(solution)/shard_map/ppermute | solution.py:211
  12.1 0.9 %convert_reduce_fusion = f32[8,16]{1,0:T(8,128)S(1)} fusion(bf16[8,16,128]{2,1,0:T(8,128)(2,1)} %param.10), kind=kLoop, calls=%fused_computation.83 | loop fusion | flops 32640 | bytes 33280 | tf_op jit(solution)/shard_map/reduce_sum | solution.py:21
  13.1 0.1 add.348
  13.2 0.2 fusion.55
  13.4 0.4 copy-done.8
  13.8 0.2 fusion.13
  14.0 0.1 add.345
  14.1 0.6 copy-done.1
  14.7 0.8 gather_fusion
  15.5 3.2 %collective-permute-start.1 = (bf16[8,16,128]{2,1,0:T(8,128)(2,1)S(1)}, bf16[8,16,128]{2,1,0:T(8,128)(2,1)S(1)}, u32[]{:S(2)}, u32[]{:S(2)}) collective-permute-start(bf16[8,16,128]{2,1,0:T(8,128)(2,1)S(1)} %broadcast_select_fusion.1), channel_id=1, source_target_pairs={{0,16},{16,0},{32,48},{48,32},{64,80},{80,64},{96,112},{112,96},{1... | collective-permute-start | bytes 98312 | tf_op jit(solution)/shard_map/ppermute | solution.py:215
  18.8 0.1 dynamic_slice.9
  18.8 1.3 %collective-permute-done.1 = bf16[8,16,128]{2,1,0:T(8,128)(2,1)S(1)} collective-permute-done((bf16[8,16,128]{2,1,0:T(8,128)(2,1)S(1)}, bf16[8,16,128]{2,1,0:T(8,128)(2,1)S(1)}, u32[]{:S(2)}, u32[]{:S(2)}) %collective-permute-start.1) | collective-permute-done | bytes 32800 | tf_op jit(solution)/shard_map/ppermute | solution.py:215
  20.2 4.7 %collective-permute-start.2 = (bf16[16,16,128]{2,1,0:T(8,128)(2,1)S(1)}, bf16[16,16,128]{2,1,0:T(8,128)(2,1)S(1)}, u32[]{:S(2)}, u32[]{:S(2)}) collective-permute-start(bf16[16,16,128]{2,1,0:T(8,128)(2,1)S(1)} %maximum_select_fusion.3), channel_id=1, source_target_pairs={{0,4},{1,5},{2,6},{3,7},{4,0},{5,1},{6,2},{7,3},{8,12},{9,13},{10,... | collective-permute-start | bytes 196616 | tf_op jit(solution)/shard_map/ppermute | solution.py:219
  24.8 0.1 broadcast_multiply_fusion.2
  24.9 0.1 dynamic_slice.11
  25.0 1.7 %collective-permute-done.2 = bf16[16,16,128]{2,1,0:T(8,128)(2,1)S(1)} collective-permute-done((bf16[16,16,128]{2,1,0:T(8,128)(2,1)S(1)}, bf16[16,16,128]{2,1,0:T(8,128)(2,1)S(1)}, u32[]{:S(2)}, u32[]{:S(2)}) %collective-permute-start.2) | collective-permute-done | bytes 65568 | tf_op jit(solution)/shard_map/ppermute | solution.py:219
  26.7 3.1 %collective-permute-start.3 = (bf16[16,16,128]{2,1,0:T(8,128)(2,1)S(1)}, bf16[16,16,128]{2,1,0:T(8,128)(2,1)S(1)}, u32[]{:S(2)}, u32[]{:S(2)}) collective-permute-start(bf16[16,16,128]{2,1,0:T(8,128)(2,1)S(1)} %broadcast_select_fusion), channel_id=1, source_target_pairs={{0,2},{1,3},{2,0},{3,1},{4,6},{5,7},{6,4},{7,5},{8,10},{9,11},{10,... | collective-permute-start | bytes 196616 | tf_op jit(solution)/shard_map/ppermute | solution.py:221
  29.9 0.8 gather_fusion.1
  30.7 1.0 %collective-permute-done.3 = bf16[16,16,128]{2,1,0:T(8,128)(2,1)S(1)} collective-permute-done((bf16[16,16,128]{2,1,0:T(8,128)(2,1)S(1)}, bf16[16,16,128]{2,1,0:T(8,128)(2,1)S(1)}, u32[]{:S(2)}, u32[]{:S(2)}) %collective-permute-start.3) | collective-permute-done | bytes 65568 | tf_op jit(solution)/shard_map/ppermute | solution.py:221
  31.7 6.3 %collective-permute-start.4 = (bf16[2,16,16,128]{3,2,1,0:T(8,128)(2,1)S(1)}, bf16[2,16,16,128]{3,2,1,0:T(8,128)(2,1)S(1)}, u32[]{:S(2)}, u32[]{:S(2)}) collective-permute-start(bf16[2,16,16,128]{3,2,1,0:T(8,128)(2,1)S(1)} %maximum_select_fusion.2), channel_id=1, source_target_pairs={{0,1},{1,0},{2,3},{3,2},{4,5},{5,4},{6,7},{7,6},{8,9},{9,8},{10,11... | collective-permute-start | bytes 393224 | tf_op jit(solution)/shard_map/ppermute | solution.py:224
  38.1 0.1 reshape.405
  38.2 0.7 copy-done.5
  38.9 0.2 reshape.407
  39.1 0.7 copy-done.6
  39.8 0.2 copy.100
  40.1 0.1 fusion.47
  40.3 0.3 multiply_reduce_fusion.1
  40.6 11.9 %collective-permute-start.5 = (bf16[4,16,16,128]{3,2,1,0:T(8,128)(2,1)S(1)}, bf16[4,16,16,128]{3,2,1,0:T(8,128)(2,1)S(1)}, u32[]{:S(2)}, u32[]{:S(2)}) collective-permute-start(bf16[4,16,16,128]{3,2,1,0:T(8,128)(2,1)S(1)} %bitcast.227), channel_id=1, source_target_pairs={{0,48},{1,176},{2,0},{3,64},{4,192},{5,240},{6,128},{7,112},{8,448... | collective-permute-start | bytes 786440 | tf_op jit(solution)/shard_map/ppermute | solution.py:233
  52.5 0.1 rsqrt.33
  52.6 0.1 div.44
  52.7 0.2 fusion.34
  53.0 0.2 convolution_convert_fusion
  53.2 0.7 copy-done.4
  53.9 0.2 fusion.58
  54.1 0.2 copy.101
  54.3 0.2 copy.109
  54.5 0.1 fusion.29
  54.7 0.2 copy.99
  54.9 18.4 %collective-permute-done.5 = bf16[4,16,16,128]{3,2,1,0:T(8,128)(2,1)S(1)} collective-permute-done((bf16[4,16,16,128]{3,2,1,0:T(8,128)(2,1)S(1)}, bf16[4,16,16,128]{3,2,1,0:T(8,128)(2,1)S(1)}, u32[]{:S(2)}, u32[]{:S(2)}) %collective-permute-start.5) | collective-permute-done | bytes 262176 | tf_op jit(solution)/shard_map/ppermute | solution.py:233
  73.3 0.2 fusion.23
  73.5 0.4 multiply_reduce_fusion
  73.9 0.1 rsqrt.31
  74.1 0.1 div.40
  74.2 0.3 fusion.22
  74.6 0.3 copy-done.7
  74.9 0.3 fusion.15
  75.2 0.2 fusion.9
  75.4 0.6 slice_reduce_fusion.3
  76.1 0.9 %fusion.36 = (f32[8,4,16]{2,1,0:T(4,128)S(1)}, f32[8,4,16]{2,1,0:T(4,128)S(1)}, f32[8,4,16]{2,1,0:T(4,128)S(1)}, f32[8,4,16]{2,1,0:T(4,128)S(1)}) fusion(f32[8,4,16,64]{3,2,1,0:T(8,128)S(1)} %fusion.9, f32[8,4,16]{2,1,0:T(4,128)S(1)} %get-tuple-element.19, f32[8,4,16]{2,1,0:T(4,128)S(1)} %get-tuple-element.22, f32[8,4,16]{2,1,0:T(4,128)S(1)} %get-tuple-element.21, ...), kind=kLoop, calls=%fused_computation.67 | loop fusion | flops 63488 | bytes 147456 | tf_op jit(solution)/shard_map/reduce_sum | solution.py:42
  77.0 0.1 fusion.68
  77.1 0.1 fusion.75
  77.2 0.3 fusion.60
  77.5 0.1 fusion.69
  77.6 0.5 fusion.10
  78.1 0.4 fusion.11
  78.6 0.5 fusion.12
  79.1 0.4 fusion.2
  79.5 0.1 copy.114
  79.6 0.8 reshape.409
  80.4 0.6 copy.116
  81.0 0.2 fusion.17
  81.2 0.4 copy.98
  81.6 0.4 fusion
  82.0 0.8 %copy.115 = f32[8,16,128]{2,1,0:T(8,128)} copy(f32[8,16,128]{1,0,2:T(8,128)S(1)} %fusion) | data formatting | bytes 131072
  (44 shorter events, 0.6 us)
Async XLA Ops:
  0.6 52.3 %copy-start = (bf16[128,256]{1,0:T(8,128)(2,1)S(1)}, bf16[128,256]{1,0:T(8,128)(2,1)}, u32[]{:S(2)}) copy-start(bf16[128,256]{1,0:T(8,128)(2,1)} %param.15) | copy-start | bytes 196612
  0.6 14.9 %collective-permute-start = (bf16[8,16,128]{2,1,0:T(8,128)(2,1)}, bf16[8,16,128]{2,1,0:T(8,128)(2,1)S(1)}, u32[]{:S(2)}, u32[]{:S(2)}) collective-permute-start(bf16[8,16,128]{2,1,0:T(8,128)(2,1)} %param.10), channel_id=1, source_target_pairs={{0,8},{1,9},{2,10},{3,11},{4,12},{5,13},{6,14},{7,15},{8,0},{9,1},... | collective-permute-start | bytes 98312 | tf_op jit(solution)/shard_map/ppermute | solution.py:211
  12.1 1.1 %copy-start.2 = (bf16[8,16,128]{2,1,0:T(8,128)(2,1)S(1)}, bf16[8,16,128]{2,1,0:T(8,128)(2,1)}, u32[]{:S(2)}) copy-start(bf16[8,16,128]{2,1,0:T(8,128)(2,1)} %param.10) | copy-start | bytes 98308
  13.0 0.8 copy-start.8
  14.0 0.7 copy-start.1
  15.5 4.7 %collective-permute-start.1 = (bf16[8,16,128]{2,1,0:T(8,128)(2,1)S(1)}, bf16[8,16,128]{2,1,0:T(8,128)(2,1)S(1)}, u32[]{:S(2)}, u32[]{:S(2)}) collective-permute-start(bf16[8,16,128]{2,1,0:T(8,128)(2,1)S(1)} %broadcast_select_fusion.1), channel_id=1, source_target_pairs={{0,16},{16,0},{32,48},{48,32},{64,80},{80,64},{96,112},{112,96},{1... | collective-permute-start | bytes 98312 | tf_op jit(solution)/shard_map/ppermute | solution.py:215
  20.2 6.5 %collective-permute-start.2 = (bf16[16,16,128]{2,1,0:T(8,128)(2,1)S(1)}, bf16[16,16,128]{2,1,0:T(8,128)(2,1)S(1)}, u32[]{:S(2)}, u32[]{:S(2)}) collective-permute-start(bf16[16,16,128]{2,1,0:T(8,128)(2,1)S(1)} %maximum_select_fusion.3), channel_id=1, source_target_pairs={{0,4},{1,5},{2,6},{3,7},{4,0},{5,1},{6,2},{7,3},{8,12},{9,13},{10,... | collective-permute-start | bytes 196616 | tf_op jit(solution)/shard_map/ppermute | solution.py:219
  26.7 5.0 %collective-permute-start.3 = (bf16[16,16,128]{2,1,0:T(8,128)(2,1)S(1)}, bf16[16,16,128]{2,1,0:T(8,128)(2,1)S(1)}, u32[]{:S(2)}, u32[]{:S(2)}) collective-permute-start(bf16[16,16,128]{2,1,0:T(8,128)(2,1)S(1)} %broadcast_select_fusion), channel_id=1, source_target_pairs={{0,2},{1,3},{2,0},{3,1},{4,6},{5,7},{6,4},{7,5},{8,10},{9,11},{10,... | collective-permute-start | bytes 196616 | tf_op jit(solution)/shard_map/ppermute | solution.py:221
  31.7 8.3 %collective-permute-start.4 = (bf16[2,16,16,128]{3,2,1,0:T(8,128)(2,1)S(1)}, bf16[2,16,16,128]{3,2,1,0:T(8,128)(2,1)S(1)}, u32[]{:S(2)}, u32[]{:S(2)}) collective-permute-start(bf16[2,16,16,128]{3,2,1,0:T(8,128)(2,1)S(1)} %maximum_select_fusion.2), channel_id=1, source_target_pairs={{0,1},{1,0},{2,3},{3,2},{4,5},{5,4},{6,7},{7,6},{8,9},{9,8},{10,11... | collective-permute-start | bytes 393224 | tf_op jit(solution)/shard_map/ppermute | solution.py:224
  38.1 0.8 %copy-start.5 = (f32[8,16,128]{2,1,0:T(8,128)S(1)}, f32[8,16,128]{2,1,0:T(8,128)}, u32[]{:S(2)}) copy-start(f32[8,16,128]{2,1,0:T(8,128)} %param.19) | copy-start | bytes 196612
  38.9 0.8 %copy-start.6 = (f32[8,16,128]{2,1,0:T(8,128)S(1)}, f32[8,16,128]{2,1,0:T(8,128)}, u32[]{:S(2)}) copy-start(f32[8,16,128]{2,1,0:T(8,128)} %param.17) | copy-start | bytes 196612
  40.6 32.7 %collective-permute-start.5 = (bf16[4,16,16,128]{3,2,1,0:T(8,128)(2,1)S(1)}, bf16[4,16,16,128]{3,2,1,0:T(8,128)(2,1)S(1)}, u32[]{:S(2)}, u32[]{:S(2)}) collective-permute-start(bf16[4,16,16,128]{3,2,1,0:T(8,128)(2,1)S(1)} %bitcast.227), channel_id=1, source_target_pairs={{0,48},{1,176},{2,0},{3,64},{4,192},{5,240},{6,128},{7,112},{8,448... | collective-permute-start | bytes 786440 | tf_op jit(solution)/shard_map/ppermute | solution.py:233
  52.9 0.9 %copy-start.4 = (bf16[128,512]{1,0:T(8,128)(2,1)S(1)}, bf16[128,512]{1,0:T(8,128)(2,1)}, u32[]{:S(2)}) copy-start(bf16[128,512]{1,0:T(8,128)(2,1)} %param.13) | copy-start | bytes 393220
  74.2 0.7 copy-start.7
  76.1 0.9 %copy-start.3 = (f32[4,8,16]{2,1,0:T(8,128)S(1)}, f32[4,8,16]{2,1,0:T(8,128)}, u32[]{:S(2)}) copy-start(f32[4,8,16]{2,1,0:T(8,128)} %param.18) | copy-start | bytes 6148

commit v10 on v9

--- a/solution.py
+++ b/solution.py
@@ -231,7 +231,7 @@
 
     perm = owner_perm(n_row, n_col, groups)
     moved = lax.ppermute(tiles, ("row", "col"), perm)
-    cols_act = moved.transpose(1, 0, 2, 3).reshape(groups * row_count, window, channels)
+    cols_act = moved
 
     normed = layer_norm(pair_act)
     queries = (project(normed, query_weight) * (1.0 / math.sqrt(HEAD_DIM))).astype(jnp.bfloat16)
@@ -245,13 +245,17 @@
     )
     right = gate_pair(
         project(cols_normed, triangle_weight[:, 2 * TRI_DIM :]),
-        col_mask[:, None, None] * key_keep[None, :, None],
+        col_mask[None, :, None, None] * key_keep.reshape(STEPS, 1, col_width, 1),
     )
     key_value = project(rows_normed, key_value_weight).astype(jnp.bfloat16)
-    pair_bias = jnp.transpose(project(cols_normed, bias_weight).astype(jnp.bfloat16), (2, 0, 1))
+    pair_bias = jnp.transpose(project(cols_normed, bias_weight).astype(jnp.bfloat16), (3, 1, 0, 2))
+    pair_bias = pair_bias.reshape(HEADS, col_width, window)
 
     triangle_sums = triangle_carry + jnp.einsum(
-        "ikc,jkc->ijc", left, right, preferred_element_type=jnp.float32
+        "itkc,tjkc->ijc",
+        left.reshape(row_count, STEPS, col_width, TRI_DIM),
+        right,
+        preferred_element_type=jnp.float32,
     )
 
     keys = key_value[..., :width].reshape(row_count, window, HEADS, HEAD_DIM)

time: 83.4 us -> 88.6 us (1.062)
  matrix products: 3.65 us -> 7.18 us
  starting transfers between devices: 40 us -> 36.6 us
  local copies, waits for them, and re-layouts: 9.65 us -> 12.5 us
  other arithmetic: 5.22 us -> 7.08 us
    convert_element_type x2 -> x1, local copies, waits for them, and re-layouts: 0.62 us -> 2.96 us  [gate_pair(): (jax.nn.sigmoid(gate_part) * value_part * pair_keep).astype(jnp.bfloat16)]
    dot_general x1, matrix products: 0.38 us -> 2.49 us  [shards(): jnp.einsum('itkc,tjkc->ijc', left.reshape(row_count, STEPS, col_width, TR...]
    ppermute x1, starting transfers between devices: 11.9 us -> 9.9 us  [shards(): moved = lax.ppermute(tiles, ('row', 'col'), perm)]
    unnamed x21 -> x15, local copies, waits for them, and re-layouts: 5.09 us -> 3.48 us
    dot_general x5, matrix products: 1.2 us -> 2.64 us  [project(): result = jnp.dot(flattened, weight, preferred_element_type=jnp.float32)]
    reshape x0 -> x1, local copies, waits for them, and re-layouts: none -> 1.43 us  [shards(): left.reshape(row_count, STEPS, col_width, TRI_DIM)]
  transfers between devices with their start and end apart: 6 -> 6, of which waited for: 4 -> 4; matrix products, arithmetic and copies ran while one was open for 7% -> 12% of each run, Pallas kernels for 0% -> 0%
where the time goes in v10:
time: 88.6 us; the launch traced here: 87.9 us
  starting transfers between devices  36.6 us (41%)
  waiting for transfers between devices  22.7 us (26%)
  local copies, waits for them, and re-layouts  12.5 us (14%)
  matrix products  7.18 us (8%)
  other arithmetic  7.08 us (8%)
  between operations  1.83 us (2%)
    ppermute x1, waiting for transfers between devices, shards(): moved = lax.ppermute(tiles, ('row', 'col'), perm)  17.9 us
    ppermute x1, starting transfers between devices, shards(): received = lax.ppermute(pair_act, 'col', [(i, i ^ 8) for i in range(n_col)])  10.8 us
    ppermute x1, starting transfers between devices, shards(): moved = lax.ppermute(tiles, ('row', 'col'), perm)  9.9 us
    ppermute x1, starting transfers between devices, shards(): received = lax.ppermute(pair, 'col', [(i, i ^ 1) for i in range(n_col)])  6.44 us
    ppermute x1, starting transfers between devices, shards(): received = lax.ppermute(held, 'col', [(i, i ^ 4) for i in range(n_col)])  3.91 us
    unnamed x15, local copies, waits for them, and re-layouts  3.48 us
    ppermute x1, starting transfers between devices, shards(): partner = lax.ppermute(held, 'row', [(i, i ^ 1) for i in range(n_row)])  3.19 us
    convert_element_type x1, local copies, waits for them, and re-layouts, gate_pair(): (jax.nn.sigmoid(gate_part) * value_part * pair_keep).astype(jnp.bfloat16)  2.96 us
  transfers between devices with their start and end apart: 6, of which 4 were waited for; matrix products, arithmetic and copies ran while one was open for 12% of the time, Pallas kernels for 0%

profile of v10, /device:TPU:129, one launch (start us, length us, event | category | flops | bytes accessed | tf_op | source)
XLA Modules:
  0.0 87.9 jit_solution(839944154774377167)
XLA Ops:
  0.7 10.8 %collective-permute-start = (bf16[8,16,128]{2,1,0:T(8,128)(2,1)}, bf16[8,16,128]{2,1,0:T(8,128)(2,1)S(1)}, u32[]{:S(2)}, u32[]{:S(2)}) collective-permute-start(bf16[8,16,128]{2,1,0:T(8,128)(2,1)} %param.10), channel_id=1, source_target_pairs={{0,8},{1,9},{2,10},{3,11},{4,12},{5,13},{6,14},{7,15},{8,0},{9,1},... | collective-permute-start | bytes 98312 | tf_op jit(solution)/shard_map/ppermute | solution.py:211
  12.1 0.8 convert_reduce_fusion.1
  13.0 0.1 iota_add_fusion
  13.1 0.1 add.358
  13.2 0.9 %fusion.59 = f32[8,16]{1,0:T(8,128)S(1)} fusion(bf16[8,16,128]{2,1,0:T(8,128)(2,1)} %param.10, f32[8,16]{1,0:T(8,128)S(1)} %broadcast_multiply_fusion.3), kind=kLoop, calls=%fused_computation.87 | loop fusion | flops 65408 | bytes 33792 | tf_op jit(solution)/shard_map/reduce_sum | solution.py:23
  14.1 0.7 convert_element_type.83
  14.8 0.8 gather_fusion
  15.6 0.1 gather.11
  15.7 1.0 %fusion.15 = bf16[8,16,128]{2,1,0:T(8,128)(2,1)S(1)} fusion(bf16[8,16,128]{2,1,0:T(8,128)(2,1)} %param.10, bf16[128,128]{1,0:T(8,128)(2,1)} %param.14, f32[8,16]{1,0:T(8,128)S(1)} %add_rsqrt_fusion.2, f32[8,16]{1,0:T(8,128)S(1)} %broadcast_multiply_fusion.3), kind=kOutput, calls=%fused_computation.26 | convolution fusion | flops 4292608 | bytes 99328 | tf_op jit(solution)/shard_map/dot_general | solution.py:29
  16.7 0.1 and_select_fusion
  16.7 0.1 dynamic_slice.9
  16.8 0.8 broadcast_select_fusion.1
  17.6 3.2 %collective-permute-start.1 = (bf16[8,16,128]{2,1,0:T(8,128)(2,1)S(1)}, bf16[8,16,128]{2,1,0:T(8,128)(2,1)S(1)}, u32[]{:S(2)}, u32[]{:S(2)}) collective-permute-start(bf16[8,16,128]{2,1,0:T(8,128)(2,1)S(1)} %broadcast_select_fusion.1), channel_id=1, source_target_pairs={{0,16},{16,0},{32,48},{48,32},{64,80},{80,64},{96,112},{112,96},{1... | collective-permute-start | bytes 98312 | tf_op jit(solution)/shard_map/ppermute | solution.py:215
  20.8 0.1 broadcast_multiply_fusion
  20.9 0.1 add.366
  20.9 1.3 %collective-permute-done.1 = bf16[8,16,128]{2,1,0:T(8,128)(2,1)S(1)} collective-permute-done((bf16[8,16,128]{2,1,0:T(8,128)(2,1)S(1)}, bf16[8,16,128]{2,1,0:T(8,128)(2,1)S(1)}, u32[]{:S(2)}, u32[]{:S(2)}) %collective-permute-start.1) | collective-permute-done | bytes 32800 | tf_op jit(solution)/shard_map/ppermute | solution.py:215
  22.2 3.9 %collective-permute-start.2 = (bf16[16,16,128]{2,1,0:T(8,128)(2,1)S(1)}, bf16[16,16,128]{2,1,0:T(8,128)(2,1)S(1)}, u32[]{:S(2)}, u32[]{:S(2)}) collective-permute-start(bf16[16,16,128]{2,1,0:T(8,128)(2,1)S(1)} %maximum_select_fusion.3), channel_id=1, source_target_pairs={{0,4},{1,5},{2,6},{3,7},{4,0},{5,1},{6,2},{7,3},{8,12},{9,13},{10,... | collective-permute-start | bytes 196616 | tf_op jit(solution)/shard_map/ppermute | solution.py:219
  26.2 0.1 dynamic_slice.11
  26.3 2.5 %collective-permute-done.2 = bf16[16,16,128]{2,1,0:T(8,128)(2,1)S(1)} collective-permute-done((bf16[16,16,128]{2,1,0:T(8,128)(2,1)S(1)}, bf16[16,16,128]{2,1,0:T(8,128)(2,1)S(1)}, u32[]{:S(2)}, u32[]{:S(2)}) %collective-permute-start.2) | collective-permute-done | bytes 65568 | tf_op jit(solution)/shard_map/ppermute | solution.py:219
  28.8 2.4 %collective-permute-start.3 = (bf16[16,16,128]{2,1,0:T(8,128)(2,1)S(1)}, bf16[16,16,128]{2,1,0:T(8,128)(2,1)S(1)}, u32[]{:S(2)}, u32[]{:S(2)}) collective-permute-start(bf16[16,16,128]{2,1,0:T(8,128)(2,1)S(1)} %broadcast_select_fusion), channel_id=1, source_target_pairs={{0,2},{1,3},{2,0},{3,1},{4,6},{5,7},{6,4},{7,5},{8,10},{9,11},{10,... | collective-permute-start | bytes 196616 | tf_op jit(solution)/shard_map/ppermute | solution.py:221
  31.2 0.1 broadcast_multiply_fusion.4
  31.2 1.5 %gather_fusion.1 = s32[64]{0:T(128)S(1)} fusion(s32[256]{0:T(256)} %param.11, s32[1024]{0:T(1024)S(1)} %pad_clamp_fusion), kind=kCustom, calls=%fused_computation.1 | custom fusion | bytes 768 | tf_op jit(solution)/shard_map/jit(_take)/gather | solution.py:203
  32.7 1.1 %collective-permute-done.3 = bf16[16,16,128]{2,1,0:T(8,128)(2,1)S(1)} collective-permute-done((bf16[16,16,128]{2,1,0:T(8,128)(2,1)S(1)}, bf16[16,16,128]{2,1,0:T(8,128)(2,1)S(1)}, u32[]{:S(2)}, u32[]{:S(2)}) %collective-permute-start.3) | collective-permute-done | bytes 65568 | tf_op jit(solution)/shard_map/ppermute | solution.py:221
  33.8 6.4 %collective-permute-start.4 = (bf16[2,16,16,128]{3,2,1,0:T(8,128)(2,1)S(1)}, bf16[2,16,16,128]{3,2,1,0:T(8,128)(2,1)S(1)}, u32[]{:S(2)}, u32[]{:S(2)}) collective-permute-start(bf16[2,16,16,128]{3,2,1,0:T(8,128)(2,1)S(1)} %maximum_select_fusion.2), channel_id=1, source_target_pairs={{0,1},{1,0},{2,3},{3,2},{4,5},{5,4},{6,7},{7,6},{8,9},{9,8},{10,11... | collective-permute-start | bytes 393224 | tf_op jit(solution)/shard_map/ppermute | solution.py:224
  40.3 0.1 reshape.376
  40.4 0.2 reshape.378
  40.6 1.0 %copy.68 = f32[8,16,128]{1,0,2:T(8,128)} copy(f32[8,16,128]{2,1,0:T(8,128)S(1)} %copy-done.4) | data formatting | bytes 131072 | tf_op args[7]
  41.7 0.1 fusion.51
  41.9 0.3 multiply_reduce_fusion
  42.2 9.9 %collective-permute-start.5 = (bf16[4,16,16,128]{3,2,1,0:T(8,128)(2,1)S(1)}, bf16[4,16,16,128]{3,2,1,0:T(8,128)(2,1)S(1)}, u32[]{:S(2)}, u32[]{:S(2)}) collective-permute-start(bf16[4,16,16,128]{3,2,1,0:T(8,128)(2,1)S(1)} %bitcast.221), channel_id=1, source_target_pairs={{0,48},{1,176},{2,0},{3,64},{4,192},{5,240},{6,128},{7,112},{8,448... | collective-permute-start | bytes 786440 | tf_op jit(solution)/shard_map/ppermute | solution.py:233
  52.1 0.1 rsqrt.29
  52.2 0.1 div.41
  52.3 0.2 fusion.35
  52.5 0.2 convolution_convert_fusion
  52.7 0.2 fusion.63
  52.9 0.1 fusion.91
  53.0 0.2 copy.69
  53.2 0.2 copy.77
  53.4 0.1 fusion.30
  53.5 1.4 %copy.67 = bf16[8,4,16,128]{2,0,1,3:T(8,128)(2,1)S(1)} copy(bf16[8,4,16,128]{3,2,1,0:T(8,128)(2,1)S(1)} %bitcast.229) | data formatting | bytes 262144 | tf_op jit(solution)/shard_map/reshape | solution.py:256
  55.0 17.9 %collective-permute-done.5 = bf16[4,16,16,128]{3,2,1,0:T(8,128)(2,1)S(1)} collective-permute-done((bf16[4,16,16,128]{3,2,1,0:T(8,128)(2,1)S(1)}, bf16[4,16,16,128]{3,2,1,0:T(8,128)(2,1)S(1)}, u32[]{:S(2)}, u32[]{:S(2)}) %collective-permute-start.5) | collective-permute-done | bytes 262176 | tf_op jit(solution)/shard_map/ppermute | solution.py:233
  72.8 0.2 convert_reduce_fusion
  73.0 0.4 fusion.18
  73.5 0.8 fusion.14
  74.3 0.1 copy.71
  74.4 0.1 reshape.382
  74.5 0.2 fusion.9
  74.7 0.6 slice_reduce_fusion.3
  75.3 0.9 %fusion.37 = (f32[8,4,16]{2,1,0:T(4,128)S(1)}, f32[8,4,16]{2,1,0:T(4,128)S(1)}, f32[8,4,16]{2,1,0:T(4,128)S(1)}, f32[8,4,16]{2,1,0:T(4,128)S(1)}) fusion(f32[8,4,16,64]{3,2,1,0:T(8,128)S(1)} %fusion.9, f32[8,4,16]{2,1,0:T(4,128)S(1)} %get-tuple-element.16, f32[8,4,16]{2,1,0:T(4,128)S(1)} %get-tuple-element.19, f32[8,4,16]{2,1,0:T(4,128)S(1)} %get-tuple-element.18, ...), kind=kLoop, calls=%fused_computation.67 | loop fusion | flops 63488 | bytes 147456 | tf_op jit(solution)/shard_map/reduce_sum | solution.py:42
  76.2 0.1 fusion.71
  76.3 0.1 fusion.78
  76.5 0.1 fusion.72
  76.6 0.5 fusion.10
  77.1 0.4 fusion.11
  77.6 0.4 fusion.12
  78.0 0.4 fusion.2
  78.4 0.1 copy.82
  78.5 0.8 reshape.380
  79.3 0.6 copy.84
  79.9 0.5 fusion.45
  80.4 0.2 fusion.21
  80.6 3.0 %copy.66 = bf16[4,16,16,128]{2,1,0,3:T(8,128)(2,1)S(1)} copy(bf16[4,16,16,128]{3,2,1,0:T(8,128)(2,1)S(1)} %fusion.21) | data formatting | bytes 524288 | tf_op jit(solution)/shard_map/convert_element_type | solution.py:36
  83.6 2.5 %fusion = f32[8,16,128]{1,0,2:T(8,128)} fusion(f32[8,16,128]{1,0,2:T(8,128)} %copy.68, bf16[4,16,16,128]{2,1,0,3:T(8,128)(2,1)S(1)} %copy.66, bf16[8,4,16,128]{2,0,1,3:T(8,128)(2,1)S(1)} %copy.67), kind=kOutput, calls=%fused_computation.3 | convolution fusion | flops 2113536 | bytes 524288 | tf_op jit(solution)/shard_map/itkc,tjkc->ijc/dot_general | solution.py:254
  86.1 1.8 %copy.83 = f32[8,16,128]{2,1,0:T(8,128)} copy(f32[8,16,128]{1,0,2:T(8,128)} %fusion) | data formatting | bytes 131072
  (34 shorter events, 0.3 us)
Async XLA Ops:
  0.6 51.9 %copy-start = (bf16[128,256]{1,0:T(8,128)(2,1)S(1)}, bf16[128,256]{1,0:T(8,128)(2,1)}, u32[]{:S(2)}) copy-start(bf16[128,256]{1,0:T(8,128)(2,1)} %param.15) | copy-start | bytes 196612
  0.6 39.8 %copy-start.3 = (f32[8,16,128]{2,1,0:T(8,128)S(1)}, f32[8,16,128]{2,1,0:T(8,128)}, u32[]{:S(2)}) copy-start(f32[8,16,128]{2,1,0:T(8,128)} %param.19) | copy-start | bytes 196612
  0.7 39.9 %copy-start.4 = (f32[8,16,128]{2,1,0:T(8,128)S(1)}, f32[8,16,128]{2,1,0:T(8,128)}, u32[]{:S(2)}) copy-start(f32[8,16,128]{2,1,0:T(8,128)} %param.17) | copy-start | bytes 196612
  0.7 16.1 %collective-permute-start = (bf16[8,16,128]{2,1,0:T(8,128)(2,1)}, bf16[8,16,128]{2,1,0:T(8,128)(2,1)S(1)}, u32[]{:S(2)}, u32[]{:S(2)}) collective-permute-start(bf16[8,16,128]{2,1,0:T(8,128)(2,1)} %param.10), channel_id=1, source_target_pairs={{0,8},{1,9},{2,10},{3,11},{4,12},{5,13},{6,14},{7,15},{8,0},{9,1},... | collective-permute-start | bytes 98312 | tf_op jit(solution)/shard_map/ppermute | solution.py:211
  17.6 4.6 %collective-permute-start.1 = (bf16[8,16,128]{2,1,0:T(8,128)(2,1)S(1)}, bf16[8,16,128]{2,1,0:T(8,128)(2,1)S(1)}, u32[]{:S(2)}, u32[]{:S(2)}) collective-permute-start(bf16[8,16,128]{2,1,0:T(8,128)(2,1)S(1)} %broadcast_select_fusion.1), channel_id=1, source_target_pairs={{0,16},{16,0},{32,48},{48,32},{64,80},{80,64},{96,112},{112,96},{1... | collective-permute-start | bytes 98312 | tf_op jit(solution)/shard_map/ppermute | solution.py:215
  22.2 6.5 %collective-permute-start.2 = (bf16[16,16,128]{2,1,0:T(8,128)(2,1)S(1)}, bf16[16,16,128]{2,1,0:T(8,128)(2,1)S(1)}, u32[]{:S(2)}, u32[]{:S(2)}) collective-permute-start(bf16[16,16,128]{2,1,0:T(8,128)(2,1)S(1)} %maximum_select_fusion.3), channel_id=1, source_target_pairs={{0,4},{1,5},{2,6},{3,7},{4,0},{5,1},{6,2},{7,3},{8,12},{9,13},{10,... | collective-permute-start | bytes 196616 | tf_op jit(solution)/shard_map/ppermute | solution.py:219
  28.8 5.0 %collective-permute-start.3 = (bf16[16,16,128]{2,1,0:T(8,128)(2,1)S(1)}, bf16[16,16,128]{2,1,0:T(8,128)(2,1)S(1)}, u32[]{:S(2)}, u32[]{:S(2)}) collective-permute-start(bf16[16,16,128]{2,1,0:T(8,128)(2,1)S(1)} %broadcast_select_fusion), channel_id=1, source_target_pairs={{0,2},{1,3},{2,0},{3,1},{4,6},{5,7},{6,4},{7,5},{8,10},{9,11},{10,... | collective-permute-start | bytes 196616 | tf_op jit(solution)/shard_map/ppermute | solution.py:221
  33.8 18.9 %copy-start.2 = (bf16[128,512]{1,0:T(8,128)(2,1)S(1)}, bf16[128,512]{1,0:T(8,128)(2,1)}, u32[]{:S(2)}) copy-start(bf16[128,512]{1,0:T(8,128)(2,1)} %param.13) | copy-start | bytes 393220
  33.8 7.8 %collective-permute-start.4 = (bf16[2,16,16,128]{3,2,1,0:T(8,128)(2,1)S(1)}, bf16[2,16,16,128]{3,2,1,0:T(8,128)(2,1)S(1)}, u32[]{:S(2)}, u32[]{:S(2)}) collective-permute-start(bf16[2,16,16,128]{3,2,1,0:T(8,128)(2,1)S(1)} %maximum_select_fusion.2), channel_id=1, source_target_pairs={{0,1},{1,0},{2,3},{3,2},{4,5},{5,4},{6,7},{7,6},{8,9},{9,8},{10,11... | collective-permute-start | bytes 393224 | tf_op jit(solution)/shard_map/ppermute | solution.py:224
  42.2 30.7 %collective-permute-start.5 = (bf16[4,16,16,128]{3,2,1,0:T(8,128)(2,1)S(1)}, bf16[4,16,16,128]{3,2,1,0:T(8,128)(2,1)S(1)}, u32[]{:S(2)}, u32[]{:S(2)}) collective-permute-start(bf16[4,16,16,128]{3,2,1,0:T(8,128)(2,1)S(1)} %bitcast.221), channel_id=1, source_target_pairs={{0,48},{1,176},{2,0},{3,64},{4,192},{5,240},{6,128},{7,112},{8,448... | collective-permute-start | bytes 786440 | tf_op jit(solution)/shard_map/ppermute | solution.py:233
  52.9 20.5 %copy-start.5 = (bf16[128,4]{0,1:T(4,128)(2,1)S(1)}, bf16[128,4]{0,1:T(4,128)(2,1)}, u32[]{:S(2)}) copy-start(bf16[128,4]{0,1:T(4,128)(2,1)} %param.16) | copy-start | bytes 3076
  73.5 2.8 %copy-start.1 = (f32[4,8,16]{2,1,0:T(8,128)S(1)}, f32[4,8,16]{2,1,0:T(8,128)}, u32[]{:S(2)}) copy-start(f32[4,8,16]{2,1,0:T(8,128)} %param.18) | copy-start | bytes 6148

commit v11 on v9

--- a/solution.py
+++ b/solution.py
@@ -3,6 +3,7 @@
 import math
 
 import jax
+import numpy as np
 import jax.numpy as jnp
 from jax import lax
 from jax.sharding import PartitionSpec as P
@@ -230,7 +231,14 @@
     rows_act = rows_act.transpose(1, 0, 2, 3).reshape(row_count, window, channels)
 
     perm = owner_perm(n_row, n_col, groups)
-    moved = lax.ppermute(tiles, ("row", "col"), perm)
+    half_of = np.zeros(n_row * n_col, np.int32)
+    for src, dst in perm:
+        half_of[src] = (dst // n_col) % groups
+    half = jnp.asarray(half_of)[row_index * n_col + col_index]
+    sent = lax.dynamic_slice_in_dim(tiles, half * row_count, row_count, axis=1)
+    got = lax.ppermute(sent, ("row", "col"), perm)
+    other = lax.ppermute(got, "row", [(i, i ^ 1) for i in range(n_row)])
+    moved = jnp.where(odd, jnp.concatenate([other, got], axis=1), jnp.concatenate([got, other], axis=1))
     cols_act = moved.transpose(1, 0, 2, 3).reshape(groups * row_count, window, channels)
 
     normed = layer_norm(pair_act)

time: 83.4 us -> 82.5 us (0.989)
  the two profiles are of different devices: /device:TPU:129 before, /device:TPU:15 now
where the time goes in v11:
time: 82.5 us; the launch traced here: 81.9 us
  starting transfers between devices  35.7 us (43%)
  waiting for transfers between devices  23.7 us (29%)
  local copies, waits for them, and re-layouts  10.9 us (13%)
  other arithmetic  5.26 us (6%)
  matrix products  3.66 us (4%)
  between operations  2.57 us (3%)
    ppermute x1, starting transfers between devices, shards(): received = lax.ppermute(pair_act, 'col', [(i, i ^ 8) for i in range(n_col)])  15.6 us
    ppermute x1, waiting for transfers between devices, shards(): got = lax.ppermute(sent, ('row', 'col'), perm)  11.4 us
    ppermute x1, starting transfers between devices, shards(): received = lax.ppermute(pair, 'col', [(i, i ^ 1) for i in range(n_col)])  6.31 us
    unnamed x21, local copies, waits for them, and re-layouts  5.11 us
    ppermute x1, waiting for transfers between devices, shards(): other = lax.ppermute(got, 'row', [(i, i ^ 1) for i in range(n_row)])  4.86 us
    ppermute x1, starting transfers between devices, shards(): got = lax.ppermute(sent, ('row', 'col'), perm)  4.39 us
    ppermute x1, waiting for transfers between devices, shards(): received = lax.ppermute(held, 'col', [(i, i ^ 4) for i in range(n_col)])  3.33 us
    ppermute x1, starting transfers between devices, shards(): received = lax.ppermute(held, 'col', [(i, i ^ 4) for i in range(n_col)])  3.03 us
  transfers between devices with their start and end apart: 7, of which 5 were waited for; matrix products, arithmetic and copies ran while one was open for 7% of the time, Pallas kernels for 0%

profile of v11, /device:TPU:15, one launch (start us, length us, event | category | flops | bytes accessed | tf_op | source)
XLA Modules:
  0.0 81.9 jit_solution(7188532299531887069)
XLA Ops:
  0.6 15.6 %collective-permute-start = (bf16[8,16,128]{2,1,0:T(8,128)(2,1)}, bf16[8,16,128]{2,1,0:T(8,128)(2,1)S(1)}, u32[]{:S(2)}, u32[]{:S(2)}) collective-permute-start(bf16[8,16,128]{2,1,0:T(8,128)(2,1)} %param.11), channel_id=1, source_target_pairs={{0,8},{1,9},{2,10},{3,11},{4,12},{5,13},{6,14},{7,15},{8,0},{9,1},... | collective-permute-start | bytes 98312 | tf_op jit(solution)/shard_map/ppermute | solution.py:212
  16.9 0.9 %convert_reduce_fusion = f32[8,16]{1,0:T(8,128)S(1)} fusion(bf16[8,16,128]{2,1,0:T(8,128)(2,1)} %param.11), kind=kLoop, calls=%fused_computation.84 | loop fusion | flops 32640 | bytes 33280 | tf_op jit(solution)/shard_map/reduce_sum | solution.py:22
  17.9 0.1 add.360
  18.0 0.2 fusion.55
  18.2 0.4 copy-done.8
  18.6 0.2 fusion.13
  18.8 0.1 add.357
  18.9 0.6 copy-done.1
  19.5 0.8 gather_fusion
  20.3 2.1 %collective-permute-start.1 = (bf16[8,16,128]{2,1,0:T(8,128)(2,1)S(1)}, bf16[8,16,128]{2,1,0:T(8,128)(2,1)S(1)}, u32[]{:S(2)}, u32[]{:S(2)}) collective-permute-start(bf16[8,16,128]{2,1,0:T(8,128)(2,1)S(1)} %broadcast_select_fusion.1), channel_id=1, source_target_pairs={{0,16},{16,0},{32,48},{48,32},{64,80},{80,64},{96,112},{112,96},{1... | collective-permute-start | bytes 98312 | tf_op jit(solution)/shard_map/ppermute | solution.py:216
  22.4 0.1 dynamic_slice.17
  22.5 2.5 %collective-permute-done.1 = bf16[8,16,128]{2,1,0:T(8,128)(2,1)S(1)} collective-permute-done((bf16[8,16,128]{2,1,0:T(8,128)(2,1)S(1)}, bf16[8,16,128]{2,1,0:T(8,128)(2,1)S(1)}, u32[]{:S(2)}, u32[]{:S(2)}) %collective-permute-start.1) | collective-permute-done | bytes 32800 | tf_op jit(solution)/shard_map/ppermute | solution.py:216
  25.0 3.0 %collective-permute-start.2 = (bf16[16,16,128]{2,1,0:T(8,128)(2,1)S(1)}, bf16[16,16,128]{2,1,0:T(8,128)(2,1)S(1)}, u32[]{:S(2)}, u32[]{:S(2)}) collective-permute-start(bf16[16,16,128]{2,1,0:T(8,128)(2,1)S(1)} %maximum_select_fusion.4), channel_id=1, source_target_pairs={{0,4},{1,5},{2,6},{3,7},{4,0},{5,1},{6,2},{7,3},{8,12},{9,13},{10,... | collective-permute-start | bytes 196616 | tf_op jit(solution)/shard_map/ppermute | solution.py:220
  28.2 3.3 %collective-permute-done.2 = bf16[16,16,128]{2,1,0:T(8,128)(2,1)S(1)} collective-permute-done((bf16[16,16,128]{2,1,0:T(8,128)(2,1)S(1)}, bf16[16,16,128]{2,1,0:T(8,128)(2,1)S(1)}, u32[]{:S(2)}, u32[]{:S(2)}) %collective-permute-start.2) | collective-permute-done | bytes 65568 | tf_op jit(solution)/shard_map/ppermute | solution.py:220
  31.5 2.5 %collective-permute-start.3 = (bf16[16,16,128]{2,1,0:T(8,128)(2,1)S(1)}, bf16[16,16,128]{2,1,0:T(8,128)(2,1)S(1)}, u32[]{:S(2)}, u32[]{:S(2)}) collective-permute-start(bf16[16,16,128]{2,1,0:T(8,128)(2,1)S(1)} %broadcast_select_fusion), channel_id=1, source_target_pairs={{0,2},{1,3},{2,0},{3,1},{4,6},{5,7},{6,4},{7,5},{8,10},{9,11},{10,... | collective-permute-start | bytes 196616 | tf_op jit(solution)/shard_map/ppermute | solution.py:222
  34.1 0.8 gather_fusion.1
  34.9 1.7 %collective-permute-done.3 = bf16[16,16,128]{2,1,0:T(8,128)(2,1)S(1)} collective-permute-done((bf16[16,16,128]{2,1,0:T(8,128)(2,1)S(1)}, bf16[16,16,128]{2,1,0:T(8,128)(2,1)S(1)}, u32[]{:S(2)}, u32[]{:S(2)}) %collective-permute-start.3) | collective-permute-done | bytes 65568 | tf_op jit(solution)/shard_map/ppermute | solution.py:222
  36.5 6.3 %collective-permute-start.4 = (bf16[2,16,16,128]{3,2,1,0:T(8,128)(2,1)S(1)}, bf16[2,16,16,128]{3,2,1,0:T(8,128)(2,1)S(1)}, u32[]{:S(2)}, u32[]{:S(2)}) collective-permute-start(bf16[2,16,16,128]{3,2,1,0:T(8,128)(2,1)S(1)} %maximum_select_fusion.3), channel_id=1, source_target_pairs={{0,1},{1,0},{2,3},{3,2},{4,5},{5,4},{6,7},{7,6},{8,9},{9,8},{10,11... | collective-permute-start | bytes 393224 | tf_op jit(solution)/shard_map/ppermute | solution.py:225
  42.9 1.3 %dynamic_slice.15 = s32[1]{0:T(128)} dynamic-slice(s32[512]{0:T(512)} %constant.143.clone, s32[]{:T(128)S(6)} %select_n.232), dynamic_slice_sizes={1} | dynamic-slice | bytes 12 | tf_op jit(solution)/shard_map/dynamic_slice | solution.py:237
  44.9 0.1 reshape.407
  45.0 0.7 copy-done.5
  45.7 0.2 reshape.409
  45.9 0.7 copy-done.6
  46.5 0.2 copy.101
  46.9 0.1 fusion.47
  47.0 0.3 multiply_reduce_fusion.1
  47.3 0.1 rsqrt.33
  47.5 0.1 div.44
  47.6 0.2 fusion.34
  47.8 0.2 convolution_convert_fusion
  48.1 0.2 copy.102
  48.2 4.4 %collective-permute-start.5 = (bf16[4,8,16,128]{3,2,1,0:T(8,128)(2,1)S(1)}, bf16[4,8,16,128]{3,2,1,0:T(8,128)(2,1)S(1)}, u32[]{:S(2)}, u32[]{:S(2)}) collective-permute-start(bf16[4,8,16,128]{3,2,1,0:T(8,128)(2,1)S(1)} %get-tuple-element.30), channel_id=1, source_target_pairs={{0,48},{1,176},{2,0},{3,64},{4,192},{5,240},{6,128},{7,112},{8,448... | collective-permute-start | bytes 393224 | tf_op jit(solution)/shard_map/ppermute | solution.py:239
  52.6 0.2 copy.110
  52.8 0.7 copy-done.4
  53.5 0.2 fusion.58
  53.7 11.4 %collective-permute-done.5 = bf16[4,8,16,128]{3,2,1,0:T(8,128)(2,1)S(1)} collective-permute-done((bf16[4,8,16,128]{3,2,1,0:T(8,128)(2,1)S(1)}, bf16[4,8,16,128]{3,2,1,0:T(8,128)(2,1)S(1)}, u32[]{:S(2)}, u32[]{:S(2)}) %collective-permute-start.5) | collective-permute-done | bytes 131104 | tf_op jit(solution)/shard_map/ppermute | solution.py:239
  65.1 1.9 %collective-permute-start.6 = (bf16[4,8,16,128]{3,2,1,0:T(8,128)(2,1)S(1)}, bf16[4,8,16,128]{3,2,1,0:T(8,128)(2,1)S(1)}, u32[]{:S(2)}, u32[]{:S(2)}) collective-permute-start(bf16[4,8,16,128]{3,2,1,0:T(8,128)(2,1)S(1)} %collective-permute-done.5), channel_id=1, source_target_pairs={{0,16},{16,0},{32,48},{48,32},{64,80},{80,64},{96,112},{112,96},{1... | collective-permute-start | bytes 393224 | tf_op jit(solution)/shard_map/ppermute | solution.py:240
  67.0 0.1 fusion.29
  67.2 0.2 copy.100
  67.4 4.9 %collective-permute-done.6 = bf16[4,8,16,128]{3,2,1,0:T(8,128)(2,1)S(1)} collective-permute-done((bf16[4,8,16,128]{3,2,1,0:T(8,128)(2,1)S(1)}, bf16[4,8,16,128]{3,2,1,0:T(8,128)(2,1)S(1)}, u32[]{:S(2)}, u32[]{:S(2)}) %collective-permute-start.6) | collective-permute-done | bytes 131104 | tf_op jit(solution)/shard_map/ppermute | solution.py:240
  72.2 0.2 fusion.23
  72.5 0.4 multiply_reduce_fusion
  73.0 0.1 rsqrt.31
  73.0 0.1 div.40
  73.2 0.3 fusion.22
  73.6 0.3 copy-done.7
  73.9 0.3 fusion.15
  74.2 0.2 fusion.9
  74.4 0.6 slice_reduce_fusion.3
  75.1 0.9 %fusion.36 = (f32[8,4,16]{2,1,0:T(4,128)S(1)}, f32[8,4,16]{2,1,0:T(4,128)S(1)}, f32[8,4,16]{2,1,0:T(4,128)S(1)}, f32[8,4,16]{2,1,0:T(4,128)S(1)}) fusion(f32[8,4,16,64]{3,2,1,0:T(8,128)S(1)} %fusion.9, f32[8,4,16]{2,1,0:T(4,128)S(1)} %get-tuple-element.19, f32[8,4,16]{2,1,0:T(4,128)S(1)} %get-tuple-element.22, f32[8,4,16]{2,1,0:T(4,128)S(1)} %get-tuple-element.21, ...), kind=kLoop, calls=%fused_computation.68 | loop fusion | flops 63488 | bytes 147456 | tf_op jit(solution)/shard_map/reduce_sum | solution.py:43
  76.0 0.1 fusion.68
  76.1 0.1 fusion.75
  76.2 0.3 fusion.60
  76.6 0.5 fusion.10
  77.2 0.4 fusion.11
  77.6 0.5 fusion.12
  78.1 0.4 fusion.2
  78.5 0.1 copy.115
  78.6 0.8 reshape.411
  79.4 0.6 copy.117
  80.0 0.2 fusion.17
  80.2 0.4 copy.99
  80.6 0.4 fusion
  81.0 0.8 %copy.116 = f32[8,16,128]{2,1,0:T(8,128)} copy(f32[8,16,128]{1,0,2:T(8,128)S(1)} %fusion) | data formatting | bytes 131072
  (47 shorter events, 0.8 us)
Async XLA Ops:
  0.6 47.1 %copy-start = (bf16[128,256]{1,0:T(8,128)(2,1)S(1)}, bf16[128,256]{1,0:T(8,128)(2,1)}, u32[]{:S(2)}) copy-start(bf16[128,256]{1,0:T(8,128)(2,1)} %param.16) | copy-start | bytes 196612
  0.6 19.7 %collective-permute-start = (bf16[8,16,128]{2,1,0:T(8,128)(2,1)}, bf16[8,16,128]{2,1,0:T(8,128)(2,1)S(1)}, u32[]{:S(2)}, u32[]{:S(2)}) collective-permute-start(bf16[8,16,128]{2,1,0:T(8,128)(2,1)} %param.11), channel_id=1, source_target_pairs={{0,8},{1,9},{2,10},{3,11},{4,12},{5,13},{6,14},{7,15},{8,0},{9,1},... | collective-permute-start | bytes 98312 | tf_op jit(solution)/shard_map/ppermute | solution.py:212
  16.9 1.1 %copy-start.2 = (bf16[8,16,128]{2,1,0:T(8,128)(2,1)S(1)}, bf16[8,16,128]{2,1,0:T(8,128)(2,1)}, u32[]{:S(2)}) copy-start(bf16[8,16,128]{2,1,0:T(8,128)(2,1)} %param.11) | copy-start | bytes 98308
  17.8 0.8 copy-start.8
  18.8 0.7 copy-start.1
  20.3 4.7 %collective-permute-start.1 = (bf16[8,16,128]{2,1,0:T(8,128)(2,1)S(1)}, bf16[8,16,128]{2,1,0:T(8,128)(2,1)S(1)}, u32[]{:S(2)}, u32[]{:S(2)}) collective-permute-start(bf16[8,16,128]{2,1,0:T(8,128)(2,1)S(1)} %broadcast_select_fusion.1), channel_id=1, source_target_pairs={{0,16},{16,0},{32,48},{48,32},{64,80},{80,64},{96,112},{112,96},{1... | collective-permute-start | bytes 98312 | tf_op jit(solution)/shard_map/ppermute | solution.py:216
  25.0 6.5 %collective-permute-start.2 = (bf16[16,16,128]{2,1,0:T(8,128)(2,1)S(1)}, bf16[16,16,128]{2,1,0:T(8,128)(2,1)S(1)}, u32[]{:S(2)}, u32[]{:S(2)}) collective-permute-start(bf16[16,16,128]{2,1,0:T(8,128)(2,1)S(1)} %maximum_select_fusion.4), channel_id=1, source_target_pairs={{0,4},{1,5},{2,6},{3,7},{4,0},{5,1},{6,2},{7,3},{8,12},{9,13},{10,... | collective-permute-start | bytes 196616 | tf_op jit(solution)/shard_map/ppermute | solution.py:220
  31.5 5.0 %collective-permute-start.3 = (bf16[16,16,128]{2,1,0:T(8,128)(2,1)S(1)}, bf16[16,16,128]{2,1,0:T(8,128)(2,1)S(1)}, u32[]{:S(2)}, u32[]{:S(2)}) collective-permute-start(bf16[16,16,128]{2,1,0:T(8,128)(2,1)S(1)} %broadcast_select_fusion), channel_id=1, source_target_pairs={{0,2},{1,3},{2,0},{3,1},{4,6},{5,7},{6,4},{7,5},{8,10},{9,11},{10,... | collective-permute-start | bytes 196616 | tf_op jit(solution)/shard_map/ppermute | solution.py:222
  36.5 10.3 %collective-permute-start.4 = (bf16[2,16,16,128]{3,2,1,0:T(8,128)(2,1)S(1)}, bf16[2,16,16,128]{3,2,1,0:T(8,128)(2,1)S(1)}, u32[]{:S(2)}, u32[]{:S(2)}) collective-permute-start(bf16[2,16,16,128]{3,2,1,0:T(8,128)(2,1)S(1)} %maximum_select_fusion.3), channel_id=1, source_target_pairs={{0,1},{1,0},{2,3},{3,2},{4,5},{5,4},{6,7},{7,6},{8,9},{9,8},{10,11... | collective-permute-start | bytes 393224 | tf_op jit(solution)/shard_map/ppermute | solution.py:225
  44.9 0.8 %copy-start.5 = (f32[8,16,128]{2,1,0:T(8,128)S(1)}, f32[8,16,128]{2,1,0:T(8,128)}, u32[]{:S(2)}) copy-start(f32[8,16,128]{2,1,0:T(8,128)} %param.20) | copy-start | bytes 196612
  45.7 0.8 %copy-start.6 = (f32[8,16,128]{2,1,0:T(8,128)S(1)}, f32[8,16,128]{2,1,0:T(8,128)}, u32[]{:S(2)}) copy-start(f32[8,16,128]{2,1,0:T(8,128)} %param.18) | copy-start | bytes 196612
  48.2 16.9 %collective-permute-start.5 = (bf16[4,8,16,128]{3,2,1,0:T(8,128)(2,1)S(1)}, bf16[4,8,16,128]{3,2,1,0:T(8,128)(2,1)S(1)}, u32[]{:S(2)}, u32[]{:S(2)}) collective-permute-start(bf16[4,8,16,128]{3,2,1,0:T(8,128)(2,1)S(1)} %get-tuple-element.30), channel_id=1, source_target_pairs={{0,48},{1,176},{2,0},{3,64},{4,192},{5,240},{6,128},{7,112},{8,448... | collective-permute-start | bytes 393224 | tf_op jit(solution)/shard_map/ppermute | solution.py:239
  52.6 0.9 %copy-start.4 = (bf16[128,512]{1,0:T(8,128)(2,1)S(1)}, bf16[128,512]{1,0:T(8,128)(2,1)}, u32[]{:S(2)}) copy-start(bf16[128,512]{1,0:T(8,128)(2,1)} %param.14) | copy-start | bytes 393220
  65.1 7.1 %collective-permute-start.6 = (bf16[4,8,16,128]{3,2,1,0:T(8,128)(2,1)S(1)}, bf16[4,8,16,128]{3,2,1,0:T(8,128)(2,1)S(1)}, u32[]{:S(2)}, u32[]{:S(2)}) collective-permute-start(bf16[4,8,16,128]{3,2,1,0:T(8,128)(2,1)S(1)} %collective-permute-done.5), channel_id=1, source_target_pairs={{0,16},{16,0},{32,48},{48,32},{64,80},{80,64},{96,112},{112,96},{1... | collective-permute-start | bytes 393224 | tf_op jit(solution)/shard_map/ppermute | solution.py:240
  73.2 0.7 copy-start.7
  75.1 0.9 %copy-start.3 = (f32[4,8,16]{2,1,0:T(8,128)S(1)}, f32[4,8,16]{2,1,0:T(8,128)}, u32[]{:S(2)}) copy-start(f32[4,8,16]{2,1,0:T(8,128)} %param.19) | copy-start | bytes 6148

commit v12 on v9

--- a/solution.py
+++ b/solution.py
@@ -165,7 +165,8 @@
                     key = (src, p, col)
                     if key not in paths:
                         paths[key] = route(chip_position(*src), chip_position(p, col))
-                    row_cost.append(sum(2 * load[link] + 1 for link in paths[key]))
+                    mismatch = (p - src[0]) % groups != 0
+                    row_cost.append(sum(2 * load[link] + 1 for link in paths[key]) + mismatch * 10**6)
                 cost.append(row_cost)
             chosen[col] = list(zip(sources, assignment(cost)))
             for src, p in chosen[col]:
@@ -226,11 +227,14 @@
     tiles = jnp.where(even, jnp.stack([pair, received], axis=1), jnp.stack([received, pair], axis=1))
     tiles = tiles.reshape((STEPS,) + held.shape)
 
-    rows_act = lax.dynamic_slice_in_dim(tiles, (row_index % groups) * row_count, row_count, axis=1)
-    rows_act = rows_act.transpose(1, 0, 2, 3).reshape(row_count, window, channels)
+    own_rows = lax.dynamic_slice_in_dim(tiles, (row_index % groups) * row_count, row_count, axis=1)
+    rows_act = own_rows.transpose(1, 0, 2, 3).reshape(row_count, window, channels)
 
     perm = owner_perm(n_row, n_col, groups)
-    moved = lax.ppermute(tiles, ("row", "col"), perm)
+    sent = own_rows
+    got = lax.ppermute(sent, ("row", "col"), perm)
+    other = lax.ppermute(got, "row", [(i, i ^ 1) for i in range(n_row)])
+    moved = jnp.where(odd, jnp.concatenate([other, got], axis=1), jnp.concatenate([got, other], axis=1))
     cols_act = moved.transpose(1, 0, 2, 3).reshape(groups * row_count, window, channels)
 
     normed = layer_norm(pair_act)

time: 83.4 us -> 79.1 us (0.948)
  the two profiles are of different devices: /device:TPU:129 before, /device:TPU:6 now
where the time goes in v12:
time: 79.1 us; the launch traced here: 77.9 us
  starting transfers between devices  36.6 us (46%)
  waiting for transfers between devices  20.8 us (26%)
  local copies, waits for them, and re-layouts  9.66 us (12%)
  other arithmetic  5.25 us (7%)
  matrix products  3.67 us (5%)
  between operations  1.89 us (2%)
    ppermute x1, starting transfers between devices, shards(): received = lax.ppermute(pair_act, 'col', [(i, i ^ 8) for i in range(n_col)])  15.9 us
    ppermute x1, waiting for transfers between devices, shards(): got = lax.ppermute(sent, ('row', 'col'), perm)  8.41 us
    ppermute x1, starting transfers between devices, shards(): got = lax.ppermute(sent, ('row', 'col'), perm)  5.93 us
    unnamed x21, local copies, waits for them, and re-layouts  5.11 us
    ppermute x1, waiting for transfers between devices, shards(): received = lax.ppermute(held, 'col', [(i, i ^ 4) for i in range(n_col)])  4.2 us
    ppermute x1, starting transfers between devices, shards(): partner = lax.ppermute(held, 'row', [(i, i ^ 1) for i in range(n_row)])  3.48 us
    ppermute x1, waiting for transfers between devices, shards(): other = lax.ppermute(got, 'row', [(i, i ^ 1) for i in range(n_row)])  3.46 us
    ppermute x1, starting transfers between devices, shards(): other = lax.ppermute(got, 'row', [(i, i ^ 1) for i in range(n_row)])  3.37 us
  transfers between devices with their start and end apart: 7, of which 5 were waited for; matrix products, arithmetic and copies ran while one was open for 7% of the time, Pallas kernels for 0%

profile of v12, /device:TPU:6, one launch (start us, length us, event | category | flops | bytes accessed | tf_op | source)
XLA Modules:
  0.0 77.9 jit_solution(4354203708876004234)
XLA Ops:
  0.6 15.9 %collective-permute-start = (bf16[8,16,128]{2,1,0:T(8,128)(2,1)}, bf16[8,16,128]{2,1,0:T(8,128)(2,1)S(1)}, u32[]{:S(2)}, u32[]{:S(2)}) collective-permute-start(bf16[8,16,128]{2,1,0:T(8,128)(2,1)} %param.10), channel_id=1, source_target_pairs={{0,8},{1,9},{2,10},{3,11},{4,12},{5,13},{6,14},{7,15},{8,0},{9,1},... | collective-permute-start | bytes 98312 | tf_op jit(solution)/shard_map/ppermute | solution.py:212
  17.2 0.9 %convert_reduce_fusion = f32[8,16]{1,0:T(8,128)S(1)} fusion(bf16[8,16,128]{2,1,0:T(8,128)(2,1)} %param.10), kind=kLoop, calls=%fused_computation.84 | loop fusion | flops 32640 | bytes 33280 | tf_op jit(solution)/shard_map/reduce_sum | solution.py:21
  18.2 0.1 add.349
  18.3 0.2 fusion.55
  18.5 0.4 copy-done.8
  18.9 0.2 fusion.13
  19.1 0.1 add.346
  19.2 0.6 copy-done.1
  19.8 0.8 %gather_fusion = f32[64]{0:T(128)S(1)} fusion(f32[256]{0:T(256)S(1)} %convert_element_type.96, s32[1024]{0:T(1024)S(1)} %pad_clamp_fusion), kind=kCustom, calls=%fused_computation | custom fusion | bytes 768 | tf_op jit(solution)/shard_map/jit(_take)/gather | solution.py:205
  20.6 3.5 %collective-permute-start.1 = (bf16[8,16,128]{2,1,0:T(8,128)(2,1)S(1)}, bf16[8,16,128]{2,1,0:T(8,128)(2,1)S(1)}, u32[]{:S(2)}, u32[]{:S(2)}) collective-permute-start(bf16[8,16,128]{2,1,0:T(8,128)(2,1)S(1)} %broadcast_select_fusion.1), channel_id=1, source_target_pairs={{0,16},{16,0},{32,48},{48,32},{64,80},{80,64},{96,112},{112,96},{1... | collective-permute-start | bytes 98312 | tf_op jit(solution)/shard_map/ppermute | solution.py:216
  24.1 0.1 dynamic_slice.10
  24.2 2.2 %collective-permute-done.1 = bf16[8,16,128]{2,1,0:T(8,128)(2,1)S(1)} collective-permute-done((bf16[8,16,128]{2,1,0:T(8,128)(2,1)S(1)}, bf16[8,16,128]{2,1,0:T(8,128)(2,1)S(1)}, u32[]{:S(2)}, u32[]{:S(2)}) %collective-permute-start.1) | collective-permute-done | bytes 32800 | tf_op jit(solution)/shard_map/ppermute | solution.py:216
  26.4 3.3 %collective-permute-start.2 = (bf16[16,16,128]{2,1,0:T(8,128)(2,1)S(1)}, bf16[16,16,128]{2,1,0:T(8,128)(2,1)S(1)}, u32[]{:S(2)}, u32[]{:S(2)}) collective-permute-start(bf16[16,16,128]{2,1,0:T(8,128)(2,1)S(1)} %maximum_select_fusion.4), channel_id=1, source_target_pairs={{0,4},{1,5},{2,6},{3,7},{4,0},{5,1},{6,2},{7,3},{8,12},{9,13},{10,... | collective-permute-start | bytes 196616 | tf_op jit(solution)/shard_map/ppermute | solution.py:220
  29.9 4.2 %collective-permute-done.2 = bf16[16,16,128]{2,1,0:T(8,128)(2,1)S(1)} collective-permute-done((bf16[16,16,128]{2,1,0:T(8,128)(2,1)S(1)}, bf16[16,16,128]{2,1,0:T(8,128)(2,1)S(1)}, u32[]{:S(2)}, u32[]{:S(2)}) %collective-permute-start.2) | collective-permute-done | bytes 65568 | tf_op jit(solution)/shard_map/ppermute | solution.py:220
  34.1 2.7 %collective-permute-start.3 = (bf16[16,16,128]{2,1,0:T(8,128)(2,1)S(1)}, bf16[16,16,128]{2,1,0:T(8,128)(2,1)S(1)}, u32[]{:S(2)}, u32[]{:S(2)}) collective-permute-start(bf16[16,16,128]{2,1,0:T(8,128)(2,1)S(1)} %broadcast_select_fusion), channel_id=1, source_target_pairs={{0,2},{1,3},{2,0},{3,1},{4,6},{5,7},{6,4},{7,5},{8,10},{9,11},{10,... | collective-permute-start | bytes 196616 | tf_op jit(solution)/shard_map/ppermute | solution.py:222
  36.9 0.8 %gather_fusion.1 = s32[64]{0:T(128)S(1)} fusion(s32[256]{0:T(256)S(1)} %copy-done.1, s32[1024]{0:T(1024)S(1)} %pad_clamp_fusion), kind=kCustom, calls=%fused_computation.1 | custom fusion | bytes 768 | tf_op jit(solution)/shard_map/jit(_take)/gather | solution.py:204
  37.7 2.5 %collective-permute-done.3 = bf16[16,16,128]{2,1,0:T(8,128)(2,1)S(1)} collective-permute-done((bf16[16,16,128]{2,1,0:T(8,128)(2,1)S(1)}, bf16[16,16,128]{2,1,0:T(8,128)(2,1)S(1)}, u32[]{:S(2)}, u32[]{:S(2)}) %collective-permute-start.3) | collective-permute-done | bytes 65568 | tf_op jit(solution)/shard_map/ppermute | solution.py:222
  40.3 1.9 %collective-permute-start.4 = (bf16[2,16,16,128]{3,2,1,0:T(8,128)(2,1)S(1)}, bf16[2,16,16,128]{3,2,1,0:T(8,128)(2,1)S(1)}, u32[]{:S(2)}, u32[]{:S(2)}) collective-permute-start(bf16[2,16,16,128]{3,2,1,0:T(8,128)(2,1)S(1)} %maximum_select_fusion.3), channel_id=1, source_target_pairs={{0,1},{1,0},{2,3},{3,2},{4,5},{5,4},{6,7},{7,6},{8,9},{9,8},{10,11... | collective-permute-start | bytes 393224 | tf_op jit(solution)/shard_map/ppermute | solution.py:225
  42.3 0.1 reshape.405
  42.4 0.7 copy-done.5
  43.1 0.2 reshape.407
  43.3 0.7 copy-done.6
  43.9 0.2 copy.100
  44.2 0.1 fusion.47
  44.4 0.3 multiply_reduce_fusion.1
  44.7 5.9 %collective-permute-start.5 = (bf16[4,8,16,128]{3,2,1,0:T(8,128)(2,1)S(1)}, bf16[4,8,16,128]{3,2,1,0:T(8,128)(2,1)S(1)}, u32[]{:S(2)}, u32[]{:S(2)}) collective-permute-start(bf16[4,8,16,128]{3,2,1,0:T(8,128)(2,1)S(1)} %get-tuple-element.28), channel_id=1, source_target_pairs={{0,0},{1,32},{2,192},{3,128},{4,96},{5,64},{6,160},{7,224},{8,320}... | collective-permute-start | bytes 393224 | tf_op jit(solution)/shard_map/ppermute | solution.py:235
  50.7 0.1 rsqrt.33
  50.8 0.1 div.44
  50.9 0.2 fusion.34
  51.1 0.2 convolution_convert_fusion
  51.4 0.2 copy.101
  51.6 0.2 copy.109
  51.8 0.7 copy-done.4
  52.5 0.2 fusion.58
  52.7 8.4 %collective-permute-done.5 = bf16[4,8,16,128]{3,2,1,0:T(8,128)(2,1)S(1)} collective-permute-done((bf16[4,8,16,128]{3,2,1,0:T(8,128)(2,1)S(1)}, bf16[4,8,16,128]{3,2,1,0:T(8,128)(2,1)S(1)}, u32[]{:S(2)}, u32[]{:S(2)}) %collective-permute-start.5) | collective-permute-done | bytes 131104 | tf_op jit(solution)/shard_map/ppermute | solution.py:235
  61.1 3.4 %collective-permute-start.6 = (bf16[4,8,16,128]{3,2,1,0:T(8,128)(2,1)S(1)}, bf16[4,8,16,128]{3,2,1,0:T(8,128)(2,1)S(1)}, u32[]{:S(2)}, u32[]{:S(2)}) collective-permute-start(bf16[4,8,16,128]{3,2,1,0:T(8,128)(2,1)S(1)} %collective-permute-done.5), channel_id=1, source_target_pairs={{0,16},{16,0},{32,48},{48,32},{64,80},{80,64},{96,112},{112,96},{1... | collective-permute-start | bytes 393224 | tf_op jit(solution)/shard_map/ppermute | solution.py:236
  64.5 0.1 fusion.29
  64.6 0.2 copy.99
  64.8 3.5 %collective-permute-done.6 = bf16[4,8,16,128]{3,2,1,0:T(8,128)(2,1)S(1)} collective-permute-done((bf16[4,8,16,128]{3,2,1,0:T(8,128)(2,1)S(1)}, bf16[4,8,16,128]{3,2,1,0:T(8,128)(2,1)S(1)}, u32[]{:S(2)}, u32[]{:S(2)}) %collective-permute-start.6) | collective-permute-done | bytes 131104 | tf_op jit(solution)/shard_map/ppermute | solution.py:236
  68.3 0.2 fusion.23
  68.5 0.4 multiply_reduce_fusion
  69.0 0.1 rsqrt.31
  69.1 0.1 div.40
  69.3 0.3 fusion.22
  69.6 0.3 copy-done.7
  69.9 0.3 fusion.15
  70.2 0.2 fusion.9
  70.5 0.6 slice_reduce_fusion.3
  71.1 0.9 %fusion.36 = (f32[8,4,16]{2,1,0:T(4,128)S(1)}, f32[8,4,16]{2,1,0:T(4,128)S(1)}, f32[8,4,16]{2,1,0:T(4,128)S(1)}, f32[8,4,16]{2,1,0:T(4,128)S(1)}) fusion(f32[8,4,16,64]{3,2,1,0:T(8,128)S(1)} %fusion.9, f32[8,4,16]{2,1,0:T(4,128)S(1)} %get-tuple-element.19, f32[8,4,16]{2,1,0:T(4,128)S(1)} %get-tuple-element.22, f32[8,4,16]{2,1,0:T(4,128)S(1)} %get-tuple-element.21, ...), kind=kLoop, calls=%fused_computation.68 | loop fusion | flops 63488 | bytes 147456 | tf_op jit(solution)/shard_map/reduce_sum | solution.py:42
  72.0 0.1 fusion.68
  72.1 0.1 fusion.75
  72.3 0.3 fusion.60
  72.6 0.1 fusion.69
  72.6 0.5 fusion.10
  73.2 0.4 fusion.11
  73.7 0.5 fusion.12
  74.1 0.4 fusion.2
  74.5 0.1 copy.114
  74.6 0.8 %reshape.409 = f32[8,16,128]{2,1,0:T(8,128)} reshape(f32[8,16,4,32]{3,2,1,0:T(4,128)S(1)} %copy.114) | data formatting | bytes 131072 | tf_op jit(solution)/shard_map/reshape | solution.py:276
  75.4 0.6 copy.116
  76.0 0.2 fusion.17
  76.2 0.4 copy.98
  76.7 0.4 fusion
  77.1 0.8 %copy.115 = f32[8,16,128]{2,1,0:T(8,128)} copy(f32[8,16,128]{1,0,2:T(8,128)S(1)} %fusion) | data formatting | bytes 131072
  (46 shorter events, 0.7 us)
Async XLA Ops:
  0.6 50.5 %copy-start = (bf16[128,256]{1,0:T(8,128)(2,1)S(1)}, bf16[128,256]{1,0:T(8,128)(2,1)}, u32[]{:S(2)}) copy-start(bf16[128,256]{1,0:T(8,128)(2,1)} %param.15) | copy-start | bytes 196612
  0.6 19.9 %collective-permute-start = (bf16[8,16,128]{2,1,0:T(8,128)(2,1)}, bf16[8,16,128]{2,1,0:T(8,128)(2,1)S(1)}, u32[]{:S(2)}, u32[]{:S(2)}) collective-permute-start(bf16[8,16,128]{2,1,0:T(8,128)(2,1)} %param.10), channel_id=1, source_target_pairs={{0,8},{1,9},{2,10},{3,11},{4,12},{5,13},{6,14},{7,15},{8,0},{9,1},... | collective-permute-start | bytes 98312 | tf_op jit(solution)/shard_map/ppermute | solution.py:212
  17.2 1.1 %copy-start.2 = (bf16[8,16,128]{2,1,0:T(8,128)(2,1)S(1)}, bf16[8,16,128]{2,1,0:T(8,128)(2,1)}, u32[]{:S(2)}) copy-start(bf16[8,16,128]{2,1,0:T(8,128)(2,1)} %param.10) | copy-start | bytes 98308
  18.1 0.8 copy-start.8
  19.1 0.7 copy-start.1
  20.6 5.8 %collective-permute-start.1 = (bf16[8,16,128]{2,1,0:T(8,128)(2,1)S(1)}, bf16[8,16,128]{2,1,0:T(8,128)(2,1)S(1)}, u32[]{:S(2)}, u32[]{:S(2)}) collective-permute-start(bf16[8,16,128]{2,1,0:T(8,128)(2,1)S(1)} %broadcast_select_fusion.1), channel_id=1, source_target_pairs={{0,16},{16,0},{32,48},{48,32},{64,80},{80,64},{96,112},{112,96},{1... | collective-permute-start | bytes 98312 | tf_op jit(solution)/shard_map/ppermute | solution.py:216
  26.4 7.7 %collective-permute-start.2 = (bf16[16,16,128]{2,1,0:T(8,128)(2,1)S(1)}, bf16[16,16,128]{2,1,0:T(8,128)(2,1)S(1)}, u32[]{:S(2)}, u32[]{:S(2)}) collective-permute-start(bf16[16,16,128]{2,1,0:T(8,128)(2,1)S(1)} %maximum_select_fusion.4), channel_id=1, source_target_pairs={{0,4},{1,5},{2,6},{3,7},{4,0},{5,1},{6,2},{7,3},{8,12},{9,13},{10,... | collective-permute-start | bytes 196616 | tf_op jit(solution)/shard_map/ppermute | solution.py:220
  34.1 6.2 %collective-permute-start.3 = (bf16[16,16,128]{2,1,0:T(8,128)(2,1)S(1)}, bf16[16,16,128]{2,1,0:T(8,128)(2,1)S(1)}, u32[]{:S(2)}, u32[]{:S(2)}) collective-permute-start(bf16[16,16,128]{2,1,0:T(8,128)(2,1)S(1)} %broadcast_select_fusion), channel_id=1, source_target_pairs={{0,2},{1,3},{2,0},{3,1},{4,6},{5,7},{6,4},{7,5},{8,10},{9,11},{10,... | collective-permute-start | bytes 196616 | tf_op jit(solution)/shard_map/ppermute | solution.py:222
  40.3 3.9 %collective-permute-start.4 = (bf16[2,16,16,128]{3,2,1,0:T(8,128)(2,1)S(1)}, bf16[2,16,16,128]{3,2,1,0:T(8,128)(2,1)S(1)}, u32[]{:S(2)}, u32[]{:S(2)}) collective-permute-start(bf16[2,16,16,128]{3,2,1,0:T(8,128)(2,1)S(1)} %maximum_select_fusion.3), channel_id=1, source_target_pairs={{0,1},{1,0},{2,3},{3,2},{4,5},{5,4},{6,7},{7,6},{8,9},{9,8},{10,11... | collective-permute-start | bytes 393224 | tf_op jit(solution)/shard_map/ppermute | solution.py:225
  42.2 0.8 %copy-start.5 = (f32[8,16,128]{2,1,0:T(8,128)S(1)}, f32[8,16,128]{2,1,0:T(8,128)}, u32[]{:S(2)}) copy-start(f32[8,16,128]{2,1,0:T(8,128)} %param.19) | copy-start | bytes 196612
  43.1 0.8 %copy-start.6 = (f32[8,16,128]{2,1,0:T(8,128)S(1)}, f32[8,16,128]{2,1,0:T(8,128)}, u32[]{:S(2)}) copy-start(f32[8,16,128]{2,1,0:T(8,128)} %param.17) | copy-start | bytes 196612
  44.7 16.4 %collective-permute-start.5 = (bf16[4,8,16,128]{3,2,1,0:T(8,128)(2,1)S(1)}, bf16[4,8,16,128]{3,2,1,0:T(8,128)(2,1)S(1)}, u32[]{:S(2)}, u32[]{:S(2)}) collective-permute-start(bf16[4,8,16,128]{3,2,1,0:T(8,128)(2,1)S(1)} %get-tuple-element.28), channel_id=1, source_target_pairs={{0,0},{1,32},{2,192},{3,128},{4,96},{5,64},{6,160},{7,224},{8,320}... | collective-permute-start | bytes 393224 | tf_op jit(solution)/shard_map/ppermute | solution.py:235
  51.6 0.9 %copy-start.4 = (bf16[128,512]{1,0:T(8,128)(2,1)S(1)}, bf16[128,512]{1,0:T(8,128)(2,1)}, u32[]{:S(2)}) copy-start(bf16[128,512]{1,0:T(8,128)(2,1)} %param.13) | copy-start | bytes 393220
  61.1 7.2 %collective-permute-start.6 = (bf16[4,8,16,128]{3,2,1,0:T(8,128)(2,1)S(1)}, bf16[4,8,16,128]{3,2,1,0:T(8,128)(2,1)S(1)}, u32[]{:S(2)}, u32[]{:S(2)}) collective-permute-start(bf16[4,8,16,128]{3,2,1,0:T(8,128)(2,1)S(1)} %collective-permute-done.5), channel_id=1, source_target_pairs={{0,16},{16,0},{32,48},{48,32},{64,80},{80,64},{96,112},{112,96},{1... | collective-permute-start | bytes 393224 | tf_op jit(solution)/shard_map/ppermute | solution.py:236
  69.3 0.7 copy-start.7
  71.1 0.9 %copy-start.3 = (f32[4,8,16]{2,1,0:T(8,128)S(1)}, f32[4,8,16]{2,1,0:T(8,128)}, u32[]{:S(2)}) copy-start(f32[4,8,16]{2,1,0:T(8,128)} %param.18) | copy-start | bytes 6148
